TPU v7x, 256 devices: a whole 4x4x8 slice. The times are simulated.
256 devices in a mesh: sub: 64 (over z, x, core), harm: 4 (over y).
Axes of the slice: x: 4, y: 4, z: 8, core: 2. Of those that a mesh axis runs over, the one named last changes fastest.
Arguments:
- right_side: float32 [16, 128, 16384], P(None, None, 'sub'), may hold values from -6 to 6
- border_side: float32 [16, 128, 2048], P(None, None, 'sub'), may hold values from -6 to 6
- precond_tiles: bfloat16 [32768, 128, 128], P('sub', 'harm'), may hold values from -0.375 to 0.375
- tile_out: int32 [32768], P('sub'), may hold values from 0 to 255
- tile_in: int32 [32768], P('sub'), may hold values from 0 to 255
- couple_tiles: bfloat16 [16384, 128, 128], P('sub', 'harm'), may hold values from -0.1875 to 0.1875
- return_tiles: bfloat16 [16384, 128, 128], P('sub', 'harm'), may hold values from -0.5 to 0.5
- couple_node: int32 [16384], P('sub'), may hold values from 0 to 255
- border_owner: int32 [16384, 1], P('sub'), may hold values from 0 to 63; in each aligned block of 256 rows (0 to 255, 256 to 511, ...) at most 8 rows name the same one
- border_row: int32 [16384], P('sub'), may hold values from 0 to 31
- border_inverse: bfloat16 [2048, 128, 128], P('sub', 'harm'), may hold values from -0.5 to 0.5
Outputs:
- interior_update: float32 [16, 128, 16384], P(None, 'harm', 'sub')
- border_update: float32 [16, 128, 2048], P(None, 'harm', 'sub')
Inputs may be any that keep to these rules, and one draw needn't show every extreme that they name: `border_owner`: among the rows of one subcircuit at most 8 name one owner, a bound that some block reaches of them.
All inputs are finite; a program needn't handle non-finite values.
Results may differ from a plain program's by a relative error of at most 0.005.
Values may be sent and summed in bfloat16 or wider, within the bound.
No kernel may reach another device: no remote copies, remote signals or barrier semaphores. Data moves between devices by JAX's collectives and lax.ppermute only.
A program may use at most 128 MiB of HBM per device.

v0:
```python
import jax
import jax.numpy as jnp
from jax import lax
from jax.sharding import PartitionSpec as P


def collect(values, targets, row_total, first_row=0):
    marks = (
        first_row + jnp.arange(row_total, dtype=jnp.int32)[:, None] == targets[None, :]
    ).astype(jnp.float32)
    flat_rows = values.reshape(values.shape[0], -1)
    summed = jnp.dot(
        marks, flat_rows, precision=lax.Precision.HIGHEST, preferred_element_type=jnp.float32
    )
    return summed.reshape((row_total,) + values.shape[1:])


def tile_product(tile_set, columns, targets, segment_total):
    product = jnp.einsum("tok,trk->tro", tile_set, columns, preferred_element_type=jnp.float32)
    return collect(product, targets, segment_total)


def on_device(
    right_side,
    border_side,
    precond_tiles,
    tile_out,
    tile_in,
    couple_tiles,
    return_tiles,
    couple_node,
    border_owner,
    border_row,
    border_inverse,
):
    harm_block = precond_tiles.shape[1]
    node_count = right_side.shape[2]
    row_count = border_side.shape[2]
    touch_count = couple_node.shape[0]
    sub_count = lax.axis_size("sub")
    harm_offset = lax.axis_index("harm") * harm_block
    side_nodes = jnp.transpose(right_side, (2, 0, 1))
    border_nodes = jnp.transpose(border_side, (2, 0, 1))
    own_border = lax.dynamic_slice_in_dim(border_nodes, harm_offset, harm_block, 2)
    own_side = lax.dynamic_slice_in_dim(side_nodes, harm_offset, harm_block, 2)
    side_low = side_nodes.astype(jnp.bfloat16)
    first_pass = tile_product(precond_tiles, side_low[tile_in], tile_out, node_count).astype(
        jnp.bfloat16
    )
    first_full = lax.all_gather(first_pass, "harm", axis=2, tiled=True)
    partials = jnp.einsum(
        "tok,trk->tro", couple_tiles, first_full[couple_node], preferred_element_type=jnp.float32
    )
    owner_list = border_owner[:, 0]
    value_shape = partials.shape[1:]
    capacity = min(touch_count, max(4, 2 * touch_count // sub_count))
    owner_marks = (owner_list[:, None] == jnp.arange(sub_count, dtype=jnp.int32)[None, :]).astype(
        jnp.int32
    )
    earlier = jnp.cumsum(owner_marks, axis=0) - owner_marks
    slot_index = owner_list * capacity + jnp.sum(earlier * owner_marks, axis=1)
    slot_place = jnp.arange(sub_count * capacity, dtype=jnp.int32)[:, None] == slot_index[None, :]
    place_float = slot_place.astype(jnp.float32)
    send_values = jnp.dot(
        place_float,
        partials.reshape(touch_count, -1),
        precision=lax.Precision.HIGHEST,
        preferred_element_type=jnp.float32,
    )
    send_rows = jnp.sum(slot_place.astype(jnp.int32) * border_row[None, :], axis=1)
    send_values = send_values.reshape((sub_count, capacity) + value_shape)
    send_rows = send_rows.reshape((sub_count, capacity))
    arrived, arrived_rows = (
        lax.all_to_all(send_values, "sub", split_axis=0, concat_axis=0, tiled=True),
        lax.all_to_all(send_rows, "sub", split_axis=0, concat_axis=0, tiled=True),
    )
    incoming = collect(
        arrived.reshape((sub_count * capacity,) + value_shape), arrived_rows.reshape(-1), row_count
    )
    residual_low = (own_border - incoming).astype(jnp.bfloat16)
    residual_full = lax.all_gather(residual_low, "harm", axis=2, tiled=True)
    solved = jnp.einsum(
        "bok,brk->bro", border_inverse, residual_full, preferred_element_type=jnp.float32
    )
    solved, solved_low = (solved, solved.astype(jnp.bfloat16))
    replies = solved_low[arrived_rows]
    returned = lax.all_to_all(replies, "sub", split_axis=0, concat_axis=0, tiled=True)
    returned_flat = returned.reshape(sub_count * capacity, -1)
    touch_low = jnp.dot(
        slot_place.astype(jnp.bfloat16).T, returned_flat, preferred_element_type=jnp.float32
    )
    touch_low = touch_low.astype(jnp.bfloat16).reshape((touch_count,) + value_shape)
    touch_full = lax.all_gather(touch_low, "harm", axis=2, tiled=True)
    correction = tile_product(return_tiles, touch_full, couple_node, node_count)
    update_low = (own_side - correction).astype(jnp.bfloat16)
    update_full = lax.all_gather(update_low, "harm", axis=2, tiled=True)
    second_pass = tile_product(precond_tiles, update_full[tile_in], tile_out, node_count)
    return (jnp.transpose(second_pass, (1, 2, 0)), jnp.transpose(solved, (1, 2, 0)))


def solution(mesh):
    in_specs = (
        P(None, None, "sub"),
        P(None, None, "sub"),
        P("sub", "harm", None),
        P("sub"),
        P("sub"),
        P("sub", "harm", None),
        P("sub", "harm", None),
        P("sub"),
        P("sub", None),
        P("sub"),
        P("sub", "harm", None),
    )
    out_specs = (P(None, "harm", "sub"), P(None, "harm", "sub"))
    return jax.shard_map(
        on_device, mesh=mesh, in_specs=in_specs, out_specs=out_specs, check_vma=False
    )
```

profile of v0, /device:TPU:1, one launch (start us, length us, event | category | flops | bytes accessed | tf_op | source)
XLA Modules:
  0.0 257.2 jit_solution(11936853341196245962)
XLA Ops:
  8.1 2.2 copy.72
  10.3 2.7 %gather_fusion = bf16[512,16,128]{2,1,0:T(8,128)(2,1)} fusion(bf16[256,16,128]{2,1,0:T(8,128)(2,1)S(1)} %bitcast.106, s32[1024]{0:T(1024)S(1)} %pad_clamp_fusion.2), kind=kCustom, calls=%fused_computation | custom fusion | bytes 4196352 | tf_op jit(solution)/shard_map/gather | solution.py:47
  13.0 7.1 %fusion.34 = f32[512,16,32]{2,1,0:T(8,128)} fusion(bf16[512,16,128]{2,1,0:T(8,128)(2,1)} %gather_fusion, bf16[512,32,128]{2,1,0:T(8,128)(2,1)} %param.13), kind=kOutput, calls=%fused_computation.53 | convolution fusion | flops 67108864 | bytes 7340032 | tf_op jit(solution)/shard_map/tok,trk->tro/dot_general | solution.py:19
  20.1 2.8 %copy.73 = f32[512,16,32]{0,2,1:T(8,128)S(1)} copy(f32[512,16,32]{2,1,0:T(8,128)} %fusion.34) | data formatting | bytes 2097152 | tf_op jit(solution)/shard_map/tok,trk->tro/dot_general | solution.py:19
  26.4 13.0 %all-to-all-start = ((s32[64,1,8]{2,1,0:T(1,128)}), s32[64,1,8]{2,1,0:T(1,128)S(1)}, u32[]{:S(2)}, u32[]{:S(2)}) async-start(s32[64,1,8]{2,1,0:T(1,128)} %bitcast.6), calls=%async_computation | async-start | bytes 65536 | tf_op jit(solution)/shard_map/all_to_all | solution.py:75
  39.4 13.7 %all-gather.4.cloned.1.call-done = bf16[256,16,128]{0,1,2:T(8,128)(2,1)} async-done(((bf16[256,16,32]{0,1,2:T(8,128)(2,1)}), bf16[256,16,128]{0,1,2:T(8,128)(2,1)}) %all-gather.4.cloned.1.call-update) | async-done | bytes 1048592 | tf_op jit(solution)/shard_map/all_gather | solution.py:50
  53.0 3.2 %copy.75 = bf16[256,16,128]{2,1,0:T(8,128)(2,1)} copy(bf16[256,16,128]{0,1,2:T(8,128)(2,1)} %all-gather.4.cloned.1.call-done) | data formatting | bytes 2097152 | tf_op jit(solution)/shard_map/all_gather | solution.py:50
  56.2 2.1 gather_fusion.1
  58.3 2.6 fusion.35
  60.8 2.5 copy.76
  63.3 3.4 %fusion.29 = f32[64,16,8,32]{3,2,1,0:T(8,128)} fusion(f32[256,16,32]{0,2,1:T(8,128)S(1)} %copy.76, s32[256]{0:T(256)S(1)} %multiply_add_fusion.1, s32[64,8]{1,0:T(8,128)S(1)} %multiply_add_fusion), kind=kOutput, calls=%fused_computation.52 | convolution fusion | flops 805437440 | bytes 1575936 | tf_op jit(solution)/shard_map/dot_general | solution.py:64
  66.7 4.7 %reshape.169 = f32[64,1,4096]{2,1,0:T(1,128)} reshape(f32[64,16,8,32]{3,2,1,0:T(8,128)} %fusion.29) | data formatting | bytes 2097152
  71.4 12.7 %all-to-all-start.1 = ((f32[64,1,4096]{2,1,0:T(1,128)}), f32[64,1,4096]{2,1,0:T(1,128)S(1)}, u32[]{:S(2)}, u32[]{:S(2)}) async-start(f32[64,1,4096]{2,1,0:T(1,128)} %reshape.169), calls=%async_computation.1 | async-start | bytes 2097152 | tf_op jit(solution)/shard_map/all_to_all | solution.py:74
  85.8 26.5 %all-to-all-done.1 = f32[64,1,4096]{2,1,0:T(1,128)S(1)} async-done(((f32[64,1,4096]{2,1,0:T(1,128)}), f32[64,1,4096]{2,1,0:T(1,128)S(1)}, u32[]{:S(2)}, u32[]{:S(2)}) %all-to-all-start.1) | async-done | bytes 1048608 | tf_op jit(solution)/shard_map/all_to_all | solution.py:74
  112.8 3.3 %reduce.6 = f32[64,4096]{1,0:T(8,128)S(1)} reduce(f32[64,1,4096]{2,1,0:T(1,128)S(1)} %all-to-all-done.1, f32[]{:T(128)} %broadcast.92), dimensions={1}, to_apply=%all_to_all.16.reduce_sub_computation | reduce | bytes 2097156 | tf_op jit(solution)/shard_map/all_to_all | solution.py:74
  116.1 2.7 %reshape.170 = f32[64,16,8,32]{3,2,1,0:T(8,128)} reshape(f32[64,4096]{1,0:T(8,128)S(1)} %reduce.6) | data formatting | bytes 2097152
  118.8 5.1 %copy.77 = f32[64,8,16,32]{3,2,1,0:T(8,128)} copy(f32[64,8,16,32]{3,1,2,0:T(8,128)} %bitcast.105) | data formatting | bytes 2097152 | tf_op jit(solution)/shard_map/all_to_all | solution.py:74
  123.8 3.5 %reshape_reshape.3 = f32[512,512]{1,0:T(8,128)S(1)} reshape(f32[64,8,16,32]{3,2,1,0:T(8,128)} %copy.77) | data formatting | bytes 2097152 | tf_op jit(solution)/shard_map/reshape;reshape | solution.py:11
  129.8 10.7 %all_gather.13 = bf16[32,16,128]{0,1,2:T(8,128)(2,1)S(1)} all-gather(bf16[32,16,32]{0,1,2:T(8,128)(2,1)S(1)} %copy.79), channel_id=1, replica_groups=mesh['sub'=64,'harm'=4] {'harm'}, dimensions={2}, use_global_device_ids=true | all-gather | bytes 163840 | tf_op jit(solution)/shard_map/all_gather | solution.py:81
  141.3 2.8 %gather_fusion.2 = bf16[512,16,32]{2,1,0:T(8,128)(2,1)} fusion(bf16[32,16,32]{2,1,0:T(8,128)(2,1)S(1)} %get-tuple-element.12, s32[1024]{0:T(1024)S(1)} %pad_clamp_fusion), kind=kCustom, calls=%fused_computation.2 | custom fusion | bytes 1050624 | tf_op jit(solution)/shard_map/gather | solution.py:86
  144.1 3.7 %reshape.171 = bf16[64,2,2048]{2,1,0:T(2,128)(2,1)S(1)} reshape(bf16[64,8,16,32]{3,2,1,0:T(8,128)(2,1)} %bitcast.107) | data formatting | bytes 1048576
  147.8 26.2 %all_to_all.22 = bf16[64,2,2048]{2,1,0:T(2,128)(2,1)S(1)} all-to-all(bf16[64,2,2048]{2,1,0:T(2,128)(2,1)S(1)} %reshape.171), channel_id=1, replica_groups=mesh['sub'=64,'harm'=4] {'sub'}, dimensions={0} | all-to-all | bytes 1048576 | tf_op jit(solution)/shard_map/all_to_all | solution.py:87
  175.1 2.1 reshape.114
  178.6 19.6 %all-gather.6.cloned.1.call-done = bf16[256,16,128]{0,1,2:T(8,128)(2,1)} async-done(((bf16[256,16,32]{0,1,2:T(8,128)(2,1)}), bf16[256,16,128]{0,1,2:T(8,128)(2,1)}) %all-gather.6.cloned.1.call-update) | async-done | bytes 1048592 | tf_op jit(solution)/shard_map/all_gather | solution.py:93
  198.2 2.5 copy.83
  200.6 2.8 %fusion.36 = f32[256,16,32]{2,1,0:T(8,128)S(1)} fusion(bf16[256,16,128]{2,1,0:T(8,128)(2,1)S(1)} %copy.83, bf16[256,32,128]{2,1,0:T(8,128)(2,1)} %param.17), kind=kOutput, calls=%fused_computation.55 | convolution fusion | flops 33554432 | bytes 3670016 | tf_op jit(solution)/shard_map/tok,trk->tro/dot_general | solution.py:19
  207.7 26.3 %all-gather.8.cloned.1.call-done = bf16[256,16,128]{0,1,2:T(8,128)(2,1)} async-done(((bf16[256,16,32]{0,1,2:T(8,128)(2,1)}), bf16[256,16,128]{0,1,2:T(8,128)(2,1)}) %all-gather.8.cloned.1.call-update) | async-done | bytes 1048592 | tf_op jit(solution)/shard_map/all_gather | solution.py:96
  234.0 2.5 copy.86
  236.4 2.7 %gather_fusion.3 = bf16[512,16,128]{2,1,0:T(8,128)(2,1)} fusion(bf16[256,16,128]{2,1,0:T(8,128)(2,1)S(1)} %copy.86, s32[1024]{0:T(1024)S(1)} %pad_clamp_fusion.2), kind=kCustom, calls=%fused_computation.3 | custom fusion | bytes 4196352 | tf_op jit(solution)/shard_map/gather | solution.py:97
  239.2 7.1 %fusion.37 = f32[512,16,32]{2,1,0:T(8,128)} fusion(bf16[512,16,128]{2,1,0:T(8,128)(2,1)} %gather_fusion.3, bf16[512,32,128]{2,1,0:T(8,128)(2,1)} %param.13), kind=kOutput, calls=%fused_computation.56 | convolution fusion | flops 67108864 | bytes 7340032 | tf_op jit(solution)/shard_map/tok,trk->tro/dot_general | solution.py:19
  246.2 2.9 %copy.87 = f32[512,16,32]{0,2,1:T(8,128)S(1)} copy(f32[512,16,32]{2,1,0:T(8,128)} %fusion.37) | data formatting | bytes 2097152 | tf_op jit(solution)/shard_map/tok,trk->tro/dot_general | solution.py:19
  249.2 1.5 fusion.2
  (59 shorter events, 16.3 us)
Async XLA Ops:
  7.2 51.1 %copy-start = (bf16[256,32,128]{2,1,0:T(8,128)(2,1)S(1)}, bf16[256,32,128]{2,1,0:T(8,128)(2,1)}, u32[]{:S(2)}) copy-start(bf16[256,32,128]{2,1,0:T(8,128)(2,1)} %param.16) | copy-start | bytes 6291460
  7.2 45.9 %all-gather.4.cloned.1.call-start = ((), (), s32[]{:S(2)}) async-start(), calls=%async_computation.3 | async-start | bytes 1310720 | tf_op jit(solution)/shard_map/all_gather | solution.py:50
  20.1 2.8 %copy-start.5 = (s32[512]{0:T(512)S(1)}, s32[512]{0:T(512)}, u32[]{:S(2)}) copy-start(s32[512]{0:T(512)} %param.14) | copy-start | bytes 6148
  22.9 1.6 copy-start.4
  22.9 2.6 %copy-start.7 = (s32[256]{0:T(256)S(1)}, s32[256]{0:T(256)}, u32[]{:S(2)}) copy-start(s32[256]{0:T(256)} %param.20) | copy-start | bytes 3076
  22.9 16.4 %copy-start.6 = (s32[256]{0:T(256)S(1)}, s32[256]{0:T(256)}, u32[]{:S(2)}) copy-start(s32[256]{0:T(256)} %param.18) | copy-start | bytes 3076
  26.4 45.0 %all-to-all-start = ((s32[64,1,8]{2,1,0:T(1,128)}), s32[64,1,8]{2,1,0:T(1,128)S(1)}, u32[]{:S(2)}, u32[]{:S(2)}) async-start(s32[64,1,8]{2,1,0:T(1,128)} %bitcast.6), calls=%async_computation | async-start | bytes 65536 | tf_op jit(solution)/shard_map/all_to_all | solution.py:75
  71.4 40.9 %all-to-all-start.1 = ((f32[64,1,4096]{2,1,0:T(1,128)}), f32[64,1,4096]{2,1,0:T(1,128)S(1)}, u32[]{:S(2)}, u32[]{:S(2)}) async-start(f32[64,1,4096]{2,1,0:T(1,128)} %reshape.169), calls=%async_computation.1 | async-start | bytes 2097152 | tf_op jit(solution)/shard_map/all_to_all | solution.py:74
  84.1 114.1 %all-gather.6.cloned.1.call-start = ((), (), s32[]{:S(2)}) async-start(), calls=%async_computation.4 | async-start | bytes 1310720 | tf_op jit(solution)/shard_map/all_gather | solution.py:93
  127.4 1.0 copy-start.3
  127.4 13.7 %copy-start.2 = (bf16[32,32,128]{2,1,0:T(8,128)(2,1)S(1)}, bf16[32,32,128]{2,1,0:T(8,128)(2,1)}, u32[]{:S(2)}) copy-start(bf16[32,32,128]{2,1,0:T(8,128)(2,1)} %param.21) | copy-start | bytes 786436
  178.6 55.4 %all-gather.8.cloned.1.call-start = ((), (), s32[]{:S(2)}) async-start(), calls=%async_computation.5 | async-start | bytes 1310720 | tf_op jit(solution)/shard_map/all_gather | solution.py:96
  246.2 4.4 %copy-start.1 = (bf16[256,32,128]{2,1,0:T(8,128)(2,1)S(1)}, bf16[256,32,128]{2,1,0:T(8,128)(2,1)}, u32[]{:S(2)}) copy-start(bf16[256,32,128]{2,1,0:T(8,128)(2,1)} %param.16) | copy-start | bytes 6291460
Sparse Core Ops, SparseCore 0:
  24.6 28.3 all-gather.3
  178.7 19.4 all-gather.5
  206.9 27.0 all-gather.7
where the time goes:
time: 259 us; the launch traced here: 257 us
  waiting for transfers between devices  86.1 us (33%)
  local copies, waits for them, and re-layouts  60 us (23%)
  blocking collectives  37 us (14%)
  matrix products  28.3 us (11%)
  starting transfers between devices  26 us (10%)
  between operations  14.1 us (5%)
  other arithmetic  5.77 us (2%)
    all_to_all x1, waiting for transfers between devices, on_device(): lax.all_to_all(send_values, 'sub', split_axis=0, concat_axis=0, tiled=True)  26.5 us
    all_gather x1, waiting for transfers between devices, on_device(): update_full = lax.all_gather(update_low, 'harm', axis=2, tiled=True)  26.3 us
    all_to_all x1, blocking collectives, on_device(): lax.all_to_all(replies, 'sub', split_axis=0, concat_axis=0, tiled=True)  26.2 us
    all_gather x1, waiting for transfers between devices, on_device(): touch_full = lax.all_gather(touch_low, 'harm', axis=2, tiled=True)  19.6 us
    dot_general x3, matrix products, tile_product(): jnp.einsum('tok,trk->tro', tile_set, columns, preferred_element_type=jnp....  16.9 us
    unnamed x22, local copies, waits for them, and re-layouts  15.9 us
    all_gather x1, waiting for transfers between devices, on_device(): first_full = lax.all_gather(first_pass, 'harm', axis=2, tiled=True)  13.7 us
    all_to_all x1, starting transfers between devices, on_device(): lax.all_to_all(send_rows, 'sub', split_axis=0, concat_axis=0, tiled=True)  13 us
  transfers between devices with their start and end apart: 5, of which 4 were waited for; matrix products, arithmetic and copies ran while one was open for 8% of the time, Pallas kernels for 0%

commit v1 on v0

--- a/solution.py
+++ b/solution.py
@@ -18,6 +18,20 @@
 def tile_product(tile_set, columns, targets, segment_total):
     product = jnp.einsum("tok,trk->tro", tile_set, columns, preferred_element_type=jnp.float32)
     return collect(product, targets, segment_total)
+
+
+def harm_gather(values, axis):
+    count = lax.axis_size("harm")
+    own = lax.axis_index("harm")
+    parts = [values] + [
+        lax.ppermute(values, "harm", [(i, (i + s) % count) for i in range(count)])
+        for s in range(1, count)
+    ]
+    ahead = jnp.stack([parts[(-m) % count] for m in range(count)] * 2, 0)
+    ordered = lax.dynamic_slice_in_dim(ahead, (count - own) % count, count, 0)
+    ordered = jnp.moveaxis(ordered, 0, axis)
+    shape = values.shape[:axis] + (count * values.shape[axis],) + values.shape[axis + 1 :]
+    return ordered.reshape(shape)
 
 
 def on_device(
@@ -47,7 +61,7 @@
     first_pass = tile_product(precond_tiles, side_low[tile_in], tile_out, node_count).astype(
         jnp.bfloat16
     )
-    first_full = lax.all_gather(first_pass, "harm", axis=2, tiled=True)
+    first_full = harm_gather(first_pass, 2)
     partials = jnp.einsum(
         "tok,trk->tro", couple_tiles, first_full[couple_node], preferred_element_type=jnp.float32
     )
@@ -71,14 +85,16 @@
     send_values = send_values.reshape((sub_count, capacity) + value_shape)
     send_rows = send_rows.reshape((sub_count, capacity))
     arrived, arrived_rows = (
-        lax.all_to_all(send_values, "sub", split_axis=0, concat_axis=0, tiled=True),
+        lax.all_to_all(
+            send_values.astype(jnp.bfloat16), "sub", split_axis=0, concat_axis=0, tiled=True
+        ).astype(jnp.float32),
         lax.all_to_all(send_rows, "sub", split_axis=0, concat_axis=0, tiled=True),
     )
     incoming = collect(
         arrived.reshape((sub_count * capacity,) + value_shape), arrived_rows.reshape(-1), row_count
     )
     residual_low = (own_border - incoming).astype(jnp.bfloat16)
-    residual_full = lax.all_gather(residual_low, "harm", axis=2, tiled=True)
+    residual_full = harm_gather(residual_low, 2)
     solved = jnp.einsum(
         "bok,brk->bro", border_inverse, residual_full, preferred_element_type=jnp.float32
     )
@@ -90,10 +106,10 @@
         slot_place.astype(jnp.bfloat16).T, returned_flat, preferred_element_type=jnp.float32
     )
     touch_low = touch_low.astype(jnp.bfloat16).reshape((touch_count,) + value_shape)
-    touch_full = lax.all_gather(touch_low, "harm", axis=2, tiled=True)
+    touch_full = harm_gather(touch_low, 2)
     correction = tile_product(return_tiles, touch_full, couple_node, node_count)
     update_low = (own_side - correction).astype(jnp.bfloat16)
-    update_full = lax.all_gather(update_low, "harm", axis=2, tiled=True)
+    update_full = harm_gather(update_low, 2)
     second_pass = tile_product(precond_tiles, update_full[tile_in], tile_out, node_count)
     return (jnp.transpose(second_pass, (1, 2, 0)), jnp.transpose(solved, (1, 2, 0)))
 

time: 259 us -> 201 us (0.78)
  waiting for transfers between devices: 86.1 us -> 55 us
  between operations: 14.1 us -> 1.11 us
  blocking collectives: 37 us -> 24.1 us
  starting transfers between devices: 26 us -> 31.1 us
  other arithmetic: 5.77 us -> 2.51 us
    all_gather x3 -> x0, waiting for transfers between devices: 59.5 us -> none  [the longest x1 26.3 us: on_device(): update_full = lax.all_gather(update_low, 'harm', axis=2, tiled=True)]
    ppermute x0 -> x12, waiting for transfers between devices: none -> 29.3 us  [harm_gather(): lax.ppermute(values, 'harm', [(i, (i + s) % count) for i in range(count)])]
    ppermute x0 -> x12, starting transfers between devices: none -> 13.4 us  [harm_gather(): lax.ppermute(values, 'harm', [(i, (i + s) % count) for i in range(count)])]
    all_gather x1 -> x0, blocking collectives: 10.7 us -> none  [on_device(): residual_full = lax.all_gather(residual_low, 'harm', axis=2, tiled=True)]
    all_to_all x1, waiting for transfers between devices: 26.5 us -> 16.5 us  [on_device(): lax.all_to_all(send_values.astype(jnp.bfloat16), 'sub', split_axis=0, con...]
    all_to_all x1, waiting for transfers between devices: 0.01 us -> 9.27 us  [on_device(): lax.all_to_all(send_rows, 'sub', split_axis=0, concat_axis=0, tiled=True)]
    all_gather x4 -> x0, local copies, waits for them, and re-layouts: 8.58 us -> none  [the longest x1 3.17 us: on_device(): first_full = lax.all_gather(first_pass, 'harm', axis=2, tiled=True)]
    all_to_all x1, starting transfers between devices: 12.7 us -> 4.74 us  [on_device(): lax.all_to_all(send_values.astype(jnp.bfloat16), 'sub', split_axis=0, con...]
  transfers between devices with their start and end apart: 5 -> 14, of which waited for: 4 -> 9; matrix products, arithmetic and copies ran while one was open for 8% -> 3% of each run, Pallas kernels for 0% -> 0%
where the time goes in v1:
time: 201 us; the launch traced here: 200 us
  local copies, waits for them, and re-layouts  58.6 us (29%)
  waiting for transfers between devices  55 us (27%)
  starting transfers between devices  31.1 us (15%)
  matrix products  27.7 us (14%)
  blocking collectives  24.1 us (12%)
  other arithmetic  2.51 us (1%)
    ppermute x12, waiting for transfers between devices, harm_gather(): lax.ppermute(values, 'harm', [(i, (i + s) % count) for i in range(count)])  29.3 us
    all_to_all x1, blocking collectives, on_device(): lax.all_to_all(replies, 'sub', split_axis=0, concat_axis=0, tiled=True)  24.1 us
    unnamed x47, local copies, waits for them, and re-layouts  20.6 us
    dot_general x3, matrix products, tile_product(): jnp.einsum('tok,trk->tro', tile_set, columns, preferred_element_type=jnp....  16.9 us
    all_to_all x1, waiting for transfers between devices, on_device(): lax.all_to_all(send_values.astype(jnp.bfloat16), 'sub', split_axis=0, con...  16.5 us
    ppermute x12, starting transfers between devices, harm_gather(): lax.ppermute(values, 'harm', [(i, (i + s) % count) for i in range(count)])  13.4 us
    all_to_all x1, starting transfers between devices, on_device(): lax.all_to_all(send_rows, 'sub', split_axis=0, concat_axis=0, tiled=True)  13 us
    all_to_all x1, waiting for transfers between devices, on_device(): lax.all_to_all(send_rows, 'sub', split_axis=0, concat_axis=0, tiled=True)  9.27 us
  transfers between devices with their start and end apart: 14, of which 9 were waited for; matrix products, arithmetic and copies ran while one was open for 3% of the time, Pallas kernels for 0%

profile of v1, /device:TPU:1, one launch (start us, length us, event | category | flops | bytes accessed | tf_op | source)
XLA Modules:
  0.0 200.2 jit_solution(4529429594785687866)
XLA Ops:
  1.5 2.2 %copy.77 = bf16[16,128,256]{1,0,2:T(8,128)(2,1)S(1)} copy(f32[16,128,256]{2,1,0:T(8,128)} %param.11) | data formatting | bytes 3145728 | tf_op args[0]
  3.7 2.7 %gather_fusion = bf16[512,16,128]{2,1,0:T(8,128)(2,1)} fusion(bf16[256,16,128]{2,1,0:T(8,128)(2,1)S(1)} %bitcast.172, s32[1024]{0:T(1024)S(1)} %pad_clamp_fusion.2), kind=kCustom, calls=%fused_computation | custom fusion | bytes 4196352 | tf_op jit(solution)/shard_map/gather | solution.py:61
  6.4 7.1 %fusion.33 = f32[512,16,32]{2,1,0:T(8,128)} fusion(bf16[512,16,128]{2,1,0:T(8,128)(2,1)} %gather_fusion, bf16[512,32,128]{2,1,0:T(8,128)(2,1)} %param.13), kind=kOutput, calls=%fused_computation.89 | convolution fusion | flops 67108864 | bytes 7340032 | tf_op jit(solution)/shard_map/tok,trk->tro/dot_general | solution.py:19
  13.5 2.8 %copy.78 = f32[512,16,32]{0,2,1:T(8,128)S(1)} copy(f32[512,16,32]{2,1,0:T(8,128)} %fusion.33) | data formatting | bytes 2097152 | tf_op jit(solution)/shard_map/tok,trk->tro/dot_general | solution.py:19
  17.8 2.1 %collective-permute-start.2 = (bf16[256,16,32]{0,2,1:T(8,128)(2,1)S(1)}, bf16[256,16,32]{0,2,1:T(8,128)(2,1)S(1)}, u32[]{:S(2)}, u32[]{:S(2)}) collective-permute-start(bf16[256,16,32]{0,2,1:T(8,128)(2,1)S(1)} %get-tuple-element.13), channel_id=1, source_target_pairs={{0,1},{1,2},{2,3},{3,0},{4,5},{5,6},{6,7},{7,4},{8,9},{9,10},{10,1... | collective-permute-start | bytes 786440 | tf_op jit(solution)/shard_map/ppermute | solution.py:27
  19.9 2.6 %collective-permute-start.1 = (bf16[256,16,32]{0,2,1:T(8,128)(2,1)S(1)}, bf16[256,16,32]{0,2,1:T(8,128)(2,1)S(1)}, u32[]{:S(2)}, u32[]{:S(2)}) collective-permute-start(bf16[256,16,32]{0,2,1:T(8,128)(2,1)S(1)} %get-tuple-element.13), channel_id=1, source_target_pairs={{0,2},{1,3},{2,0},{3,1},{4,6},{5,7},{6,4},{7,5},{8,10},{9,11},{10,... | collective-permute-start | bytes 786440 | tf_op jit(solution)/shard_map/ppermute | solution.py:27
  25.4 13.0 %all-to-all-start = ((s32[64,1,8]{2,1,0:T(1,128)}), s32[64,1,8]{2,1,0:T(1,128)S(1)}, u32[]{:S(2)}, u32[]{:S(2)}) async-start(s32[64,1,8]{2,1,0:T(1,128)} %bitcast.6), calls=%async_computation | async-start | bytes 65536 | tf_op jit(solution)/shard_map/all_to_all | solution.py:91
  38.5 9.3 %all-to-all-done = s32[64,1,8]{2,1,0:T(1,128)S(1)} async-done(((s32[64,1,8]{2,1,0:T(1,128)}), s32[64,1,8]{2,1,0:T(1,128)S(1)}, u32[]{:S(2)}, u32[]{:S(2)}) %all-to-all-start) | async-done | bytes 2080 | tf_op jit(solution)/shard_map/all_to_all | solution.py:91
  56.1 2.1 %gather_fusion.1 = bf16[256,16,128]{2,1,0:T(8,128)(2,1)S(1)} fusion(bf16[256,16,128]{2,1,0:T(8,128)(2,1)} %copy.80, s32[1024]{0:T(1024)S(1)} %get-tuple-element.21), kind=kCustom, calls=%fused_computation.1 | custom fusion | bytes 2098176 | tf_op jit(solution)/shard_map/gather | solution.py:66
  58.2 2.5 %fusion.34 = f32[256,16,32]{2,1,0:T(8,128)} fusion(bf16[256,16,128]{2,1,0:T(8,128)(2,1)S(1)} %gather_fusion.1, bf16[256,32,128]{2,1,0:T(8,128)(2,1)S(1)} %copy-done), kind=kOutput, calls=%fused_computation.90 | convolution fusion | flops 33554432 | bytes 3670016 | tf_op jit(solution)/shard_map/tok,trk->tro/dot_general | solution.py:65
  60.7 2.5 %copy.81 = f32[256,16,32]{0,2,1:T(8,128)S(1)} copy(f32[256,16,32]{2,1,0:T(8,128)} %fusion.34) | data formatting | bytes 1048576 | tf_op jit(solution)/shard_map/tok,trk->tro/dot_general | solution.py:65
  63.2 2.1 %fusion.28 = bf16[64,16,8,32]{3,2,1,0:T(8,128)(2,1)S(1)} fusion(f32[256,16,32]{0,2,1:T(8,128)S(1)} %copy.81, s32[256]{0:T(256)S(1)} %multiply_add_fusion.1, s32[64,8]{1,0:T(8,128)S(1)} %multiply_add_fusion), kind=kOutput, calls=%fused_computation.88 | convolution fusion | flops 805699584 | bytes 1051648 | tf_op jit(solution)/shard_map/dot_general | solution.py:78
  65.3 2.8 %reshape.185 = bf16[64,2,2048]{2,1,0:T(2,128)(2,1)} reshape(bf16[64,16,8,32]{3,2,1,0:T(8,128)(2,1)S(1)} %fusion.28) | data formatting | bytes 1048576
  68.1 4.7 %all-to-all-start.1 = ((bf16[64,2,2048]{2,1,0:T(2,128)(2,1)}), bf16[64,2,2048]{2,1,0:T(2,128)(2,1)S(1)}, u32[]{:S(2)}, u32[]{:S(2)}) async-start(bf16[64,2,2048]{2,1,0:T(2,128)(2,1)} %reshape.185), calls=%async_computation.1 | async-start | bytes 1048576 | tf_op jit(solution)/shard_map/all_to_all | solution.py:88
  74.2 16.5 %all-to-all-done.1 = bf16[64,2,2048]{2,1,0:T(2,128)(2,1)S(1)} async-done(((bf16[64,2,2048]{2,1,0:T(2,128)(2,1)}), bf16[64,2,2048]{2,1,0:T(2,128)(2,1)S(1)}, u32[]{:S(2)}, u32[]{:S(2)}) %all-to-all-start.1) | async-done | bytes 524320 | tf_op jit(solution)/shard_map/all_to_all | solution.py:88
  93.7 3.4 %reshape_reshape.3 = bf16[512,512]{1,0:T(8,128)(2,1)S(1)} reshape(bf16[64,8,16,32]{3,2,1,0:T(8,128)(2,1)} %copy.82) | data formatting | bytes 1048576 | tf_op jit(solution)/shard_map/reshape;reshape | solution.py:11
  100.1 2.5 %collective-permute-done.3 = bf16[32,16,32]{2,0,1:T(8,128)(2,1)S(1)} collective-permute-done((bf16[32,16,32]{2,0,1:T(8,128)(2,1)S(1)}, bf16[32,16,32]{2,0,1:T(8,128)(2,1)S(1)}, u32[]{:S(2)}, u32[]{:S(2)}) %collective-permute-start.3) | collective-permute-done | bytes 32800 | tf_op jit(solution)/shard_map/ppermute | solution.py:27
  102.6 3.6 %collective-permute-done.4 = bf16[32,16,32]{2,0,1:T(8,128)(2,1)S(1)} collective-permute-done((bf16[32,16,32]{2,0,1:T(8,128)(2,1)S(1)}, bf16[32,16,32]{2,0,1:T(8,128)(2,1)S(1)}, u32[]{:S(2)}, u32[]{:S(2)}) %collective-permute-start.4) | collective-permute-done | bytes 32800 | tf_op jit(solution)/shard_map/ppermute | solution.py:27
  107.4 2.7 %gather_fusion.2 = bf16[512,16,32]{2,1,0:T(8,128)(2,1)} fusion(bf16[32,16,32]{2,1,0:T(8,128)(2,1)S(1)} %get-tuple-element.16, s32[1024]{0:T(1024)S(1)} %get-tuple-element.20), kind=kCustom, calls=%fused_computation.2 | custom fusion | bytes 1050624 | tf_op jit(solution)/shard_map/gather | solution.py:102
  110.1 3.7 %reshape.187 = bf16[64,2,2048]{2,1,0:T(2,128)(2,1)S(1)} reshape(bf16[64,8,16,32]{3,2,1,0:T(8,128)(2,1)} %bitcast.173) | data formatting | bytes 1048576
  113.8 24.1 %all_to_all.22 = bf16[64,2,2048]{2,1,0:T(2,128)(2,1)S(1)} all-to-all(bf16[64,2,2048]{2,1,0:T(2,128)(2,1)S(1)} %reshape.187), channel_id=1, replica_groups=mesh['sub'=64,'harm'=4] {'sub'}, dimensions={0} | all-to-all | bytes 1048576 | tf_op jit(solution)/shard_map/all_to_all | solution.py:103
  139.0 2.1 %reshape.128 = bf16[512,512]{1,0:T(8,128)(2,1)S(1)} reshape(bf16[64,8,16,32]{3,2,1,0:T(8,128)(2,1)S(1)} %reshape.188) | data formatting | bytes 1048576 | tf_op jit(solution)/shard_map/reshape | solution.py:104
  144.9 4.2 %collective-permute-done.6 = bf16[256,16,32]{0,2,1:T(8,128)(2,1)S(1)} collective-permute-done((bf16[256,16,32]{0,2,1:T(8,128)(2,1)S(1)}, bf16[256,16,32]{0,2,1:T(8,128)(2,1)S(1)}, u32[]{:S(2)}, u32[]{:S(2)}) %collective-permute-start.6) | collective-permute-done | bytes 262176 | tf_op jit(solution)/shard_map/ppermute | solution.py:27
  149.1 7.1 %collective-permute-done.7 = bf16[256,16,32]{0,2,1:T(8,128)(2,1)S(1)} collective-permute-done((bf16[256,16,32]{0,2,1:T(8,128)(2,1)S(1)}, bf16[256,16,32]{0,2,1:T(8,128)(2,1)S(1)}, u32[]{:S(2)}, u32[]{:S(2)}) %collective-permute-start.7) | collective-permute-done | bytes 262176 | tf_op jit(solution)/shard_map/ppermute | solution.py:27
  157.7 2.8 %fusion.35 = f32[256,16,32]{2,1,0:T(8,128)S(1)} fusion(bf16[256,16,128]{2,1,0:T(8,128)(2,1)S(1)} %copy.88, bf16[256,32,128]{2,1,0:T(8,128)(2,1)} %param.17), kind=kOutput, calls=%fused_computation.91 | convolution fusion | flops 33554432 | bytes 3670016 | tf_op jit(solution)/shard_map/tok,trk->tro/dot_general | solution.py:19
  161.5 2.2 %bitcast_dynamic-update-slice_fusion.6 = (bf16[8,256,16,32]{1,3,2,0:T(8,128)(2,1)}, bf16[256,16,32]{0,2,1:T(8,128)(2,1)S(1)}) fusion(f32[256,16,32]{0,2,1:T(8,128)S(1)} %copy.89, s32[256]{0:T(256)S(1)} %copy-done.6, f32[16,128,256]{2,1,0:T(8,128)} %param.11, s32[]{:T(128)S(6)} %select_n.40), kind=kOutput, calls=%fused_computation.33 | convolution fusion | flops 402980864 | bytes 1573892 | tf_op jit(solution)/shard_map/dot_general | solution.py:12
  166.6 2.9 %collective-permute-done.9 = bf16[256,16,32]{0,2,1:T(8,128)(2,1)S(1)} collective-permute-done((bf16[256,16,32]{0,2,1:T(8,128)(2,1)S(1)}, bf16[256,16,32]{0,2,1:T(8,128)(2,1)S(1)}, u32[]{:S(2)}, u32[]{:S(2)}) %collective-permute-start.9) | collective-permute-done | bytes 262176 | tf_op jit(solution)/shard_map/ppermute | solution.py:27
  170.2 2.3 %collective-permute-done.10 = bf16[256,16,32]{0,2,1:T(8,128)(2,1)S(1)} collective-permute-done((bf16[256,16,32]{0,2,1:T(8,128)(2,1)S(1)}, bf16[256,16,32]{0,2,1:T(8,128)(2,1)S(1)}, u32[]{:S(2)}, u32[]{:S(2)}) %collective-permute-start.10) | collective-permute-done | bytes 262176 | tf_op jit(solution)/shard_map/ppermute | solution.py:27
  173.2 6.7 %collective-permute-done.11 = bf16[256,16,32]{0,2,1:T(8,128)(2,1)S(1)} collective-permute-done((bf16[256,16,32]{0,2,1:T(8,128)(2,1)S(1)}, bf16[256,16,32]{0,2,1:T(8,128)(2,1)S(1)}, u32[]{:S(2)}, u32[]{:S(2)}) %collective-permute-start.11) | collective-permute-done | bytes 262176 | tf_op jit(solution)/shard_map/ppermute | solution.py:27
  186.0 2.7 %gather_fusion.3 = bf16[512,16,128]{2,1,0:T(8,128)(2,1)} fusion(bf16[256,16,128]{2,1,0:T(8,128)(2,1)S(1)} %copy.91, s32[1024]{0:T(1024)S(1)} %pad_clamp_fusion.2), kind=kCustom, calls=%fused_computation.3 | custom fusion | bytes 4196352 | tf_op jit(solution)/shard_map/gather | solution.py:113
  188.7 7.1 %fusion.36 = f32[512,16,32]{2,1,0:T(8,128)} fusion(bf16[512,16,128]{2,1,0:T(8,128)(2,1)} %gather_fusion.3, bf16[512,32,128]{2,1,0:T(8,128)(2,1)} %param.13), kind=kOutput, calls=%fused_computation.92 | convolution fusion | flops 67108864 | bytes 7340032 | tf_op jit(solution)/shard_map/tok,trk->tro/dot_general | solution.py:19
  195.8 2.9 %copy.92 = f32[512,16,32]{0,2,1:T(8,128)S(1)} copy(f32[512,16,32]{2,1,0:T(8,128)} %fusion.36) | data formatting | bytes 2097152 | tf_op jit(solution)/shard_map/tok,trk->tro/dot_general | solution.py:19
  (103 shorter events, 41.0 us)
Async XLA Ops:
  0.6 57.6 %copy-start = (bf16[256,32,128]{2,1,0:T(8,128)(2,1)S(1)}, bf16[256,32,128]{2,1,0:T(8,128)(2,1)}, u32[]{:S(2)}) copy-start(bf16[256,32,128]{2,1,0:T(8,128)(2,1)} %param.16) | copy-start | bytes 6291460
  13.5 2.9 %copy-start.5 = (s32[512]{0:T(512)S(1)}, s32[512]{0:T(512)}, u32[]{:S(2)}) copy-start(s32[512]{0:T(512)} %param.14) | copy-start | bytes 6148
  13.5 10.1 %copy-start.4 = (s32[256,1]{0,1:T(1,128)S(1)}, s32[256,1]{0,1:T(1,128)}, u32[]{:S(2)}) copy-start(s32[256,1]{0,1:T(1,128)} %param.19) | copy-start | bytes 3076
  13.5 11.0 %copy-start.7 = (s32[256]{0:T(256)S(1)}, s32[256]{0:T(256)}, u32[]{:S(2)}) copy-start(s32[256]{0:T(256)} %param.20) | copy-start | bytes 3076
  13.5 24.9 %copy-start.6 = (s32[256]{0:T(256)S(1)}, s32[256]{0:T(256)}, u32[]{:S(2)}) copy-start(s32[256]{0:T(256)} %param.18) | copy-start | bytes 3076
  17.8 31.5 %collective-permute-start.2 = (bf16[256,16,32]{0,2,1:T(8,128)(2,1)S(1)}, bf16[256,16,32]{0,2,1:T(8,128)(2,1)S(1)}, u32[]{:S(2)}, u32[]{:S(2)}) collective-permute-start(bf16[256,16,32]{0,2,1:T(8,128)(2,1)S(1)} %get-tuple-element.13), channel_id=1, source_target_pairs={{0,1},{1,2},{2,3},{3,0},{4,5},{5,6},{6,7},{7,4},{8,9},{9,10},{10,1... | collective-permute-start | bytes 786440 | tf_op jit(solution)/shard_map/ppermute | solution.py:27
  19.9 28.7 %collective-permute-start.1 = (bf16[256,16,32]{0,2,1:T(8,128)(2,1)S(1)}, bf16[256,16,32]{0,2,1:T(8,128)(2,1)S(1)}, u32[]{:S(2)}, u32[]{:S(2)}) collective-permute-start(bf16[256,16,32]{0,2,1:T(8,128)(2,1)S(1)} %get-tuple-element.13), channel_id=1, source_target_pairs={{0,2},{1,3},{2,0},{3,1},{4,6},{5,7},{6,4},{7,5},{8,10},{9,11},{10,... | collective-permute-start | bytes 786440 | tf_op jit(solution)/shard_map/ppermute | solution.py:27
  22.5 25.4 %collective-permute-start = (bf16[256,16,32]{0,2,1:T(8,128)(2,1)S(1)}, bf16[256,16,32]{0,2,1:T(8,128)(2,1)S(1)}, u32[]{:S(2)}, u32[]{:S(2)}) collective-permute-start(bf16[256,16,32]{0,2,1:T(8,128)(2,1)S(1)} %get-tuple-element.13), channel_id=1, source_target_pairs={{0,3},{1,0},{2,1},{3,2},{4,7},{5,4},{6,5},{7,6},{8,11},{9,8},{10,9... | collective-permute-start | bytes 786440 | tf_op jit(solution)/shard_map/ppermute | solution.py:27
  25.4 22.3 %all-to-all-start = ((s32[64,1,8]{2,1,0:T(1,128)}), s32[64,1,8]{2,1,0:T(1,128)S(1)}, u32[]{:S(2)}, u32[]{:S(2)}) async-start(s32[64,1,8]{2,1,0:T(1,128)} %bitcast.6), calls=%async_computation | async-start | bytes 65536 | tf_op jit(solution)/shard_map/all_to_all | solution.py:91
  68.1 22.6 %all-to-all-start.1 = ((bf16[64,2,2048]{2,1,0:T(2,128)(2,1)}), bf16[64,2,2048]{2,1,0:T(2,128)(2,1)S(1)}, u32[]{:S(2)}, u32[]{:S(2)}) async-start(bf16[64,2,2048]{2,1,0:T(2,128)(2,1)} %reshape.185), calls=%async_computation.1 | async-start | bytes 1048576 | tf_op jit(solution)/shard_map/all_to_all | solution.py:88
  93.7 3.6 %copy-start.3 = (f32[16,128,32]{1,2,0:T(8,128)S(1)}, f32[16,128,32]{1,2,0:T(8,128)}, u32[]{:S(2)}) copy-start(f32[16,128,32]{1,2,0:T(8,128)} %param.12) | copy-start | bytes 786436
  97.8 4.7 %collective-permute-start.3 = (bf16[32,16,32]{2,0,1:T(8,128)(2,1)S(1)}, bf16[32,16,32]{2,0,1:T(8,128)(2,1)S(1)}, u32[]{:S(2)}, u32[]{:S(2)}) collective-permute-start(bf16[32,16,32]{2,0,1:T(8,128)(2,1)S(1)} %get-tuple-element.15), channel_id=1, source_target_pairs={{0,3},{1,0},{2,1},{3,2},{4,7},{5,4},{6,5},{7,6},{8,11},{9,8},{10,9... | collective-permute-start | bytes 98312 | tf_op jit(solution)/shard_map/ppermute | solution.py:27
  97.9 8.3 %collective-permute-start.5 = (bf16[32,16,32]{2,0,1:T(8,128)(2,1)S(1)}, bf16[32,16,32]{2,0,1:T(8,128)(2,1)S(1)}, u32[]{:S(2)}, u32[]{:S(2)}) collective-permute-start(bf16[32,16,32]{2,0,1:T(8,128)(2,1)S(1)} %get-tuple-element.15), channel_id=1, source_target_pairs={{0,1},{1,2},{2,3},{3,0},{4,5},{5,6},{6,7},{7,4},{8,9},{9,10},{10,1... | collective-permute-start | bytes 98312 | tf_op jit(solution)/shard_map/ppermute | solution.py:27
  99.4 6.8 %collective-permute-start.4 = (bf16[32,16,32]{2,0,1:T(8,128)(2,1)S(1)}, bf16[32,16,32]{2,0,1:T(8,128)(2,1)S(1)}, u32[]{:S(2)}, u32[]{:S(2)}) collective-permute-start(bf16[32,16,32]{2,0,1:T(8,128)(2,1)S(1)} %get-tuple-element.15), channel_id=1, source_target_pairs={{0,2},{1,3},{2,0},{3,1},{4,6},{5,7},{6,4},{7,5},{8,10},{9,11},{10,... | collective-permute-start | bytes 98312 | tf_op jit(solution)/shard_map/ppermute | solution.py:27
  106.2 1.0 copy-start.2
  141.6 7.5 %collective-permute-start.6 = (bf16[256,16,32]{0,2,1:T(8,128)(2,1)S(1)}, bf16[256,16,32]{0,2,1:T(8,128)(2,1)S(1)}, u32[]{:S(2)}, u32[]{:S(2)}) collective-permute-start(bf16[256,16,32]{0,2,1:T(8,128)(2,1)S(1)} %bitcast.178), channel_id=1, source_target_pairs={{0,3},{1,0},{2,1},{3,2},{4,7},{5,4},{6,5},{7,6},{8,11},{9,8},{10,9... | collective-permute-start | bytes 786440 | tf_op jit(solution)/shard_map/ppermute | solution.py:27
  142.8 13.5 %collective-permute-start.8 = (bf16[256,16,32]{0,2,1:T(8,128)(2,1)S(1)}, bf16[256,16,32]{0,2,1:T(8,128)(2,1)S(1)}, u32[]{:S(2)}, u32[]{:S(2)}) collective-permute-start(bf16[256,16,32]{0,2,1:T(8,128)(2,1)S(1)} %bitcast.179), channel_id=1, source_target_pairs={{0,1},{1,2},{2,3},{3,0},{4,5},{5,6},{6,7},{7,4},{8,9},{9,10},{10,1... | collective-permute-start | bytes 786440 | tf_op jit(solution)/shard_map/ppermute | solution.py:27
  143.1 13.1 %collective-permute-start.7 = (bf16[256,16,32]{0,2,1:T(8,128)(2,1)S(1)}, bf16[256,16,32]{0,2,1:T(8,128)(2,1)S(1)}, u32[]{:S(2)}, u32[]{:S(2)}) collective-permute-start(bf16[256,16,32]{0,2,1:T(8,128)(2,1)S(1)} %bitcast.180), channel_id=1, source_target_pairs={{0,2},{1,3},{2,0},{3,1},{4,6},{5,7},{6,4},{7,5},{8,10},{9,11},{10,... | collective-permute-start | bytes 786440 | tf_op jit(solution)/shard_map/ppermute | solution.py:27
  163.7 5.8 %collective-permute-start.9 = (bf16[256,16,32]{0,2,1:T(8,128)(2,1)S(1)}, bf16[256,16,32]{0,2,1:T(8,128)(2,1)S(1)}, u32[]{:S(2)}, u32[]{:S(2)}) collective-permute-start(bf16[256,16,32]{0,2,1:T(8,128)(2,1)S(1)} %get-tuple-element.19), channel_id=1, source_target_pairs={{0,3},{1,0},{2,1},{3,2},{4,7},{5,4},{6,5},{7,6},{8,11},{9,8},{10,9... | collective-permute-start | bytes 786440 | tf_op jit(solution)/shard_map/ppermute | solution.py:27
  164.6 7.9 %collective-permute-start.10 = (bf16[256,16,32]{0,2,1:T(8,128)(2,1)S(1)}, bf16[256,16,32]{0,2,1:T(8,128)(2,1)S(1)}, u32[]{:S(2)}, u32[]{:S(2)}) collective-permute-start(bf16[256,16,32]{0,2,1:T(8,128)(2,1)S(1)} %get-tuple-element.19), channel_id=1, source_target_pairs={{0,2},{1,3},{2,0},{3,1},{4,6},{5,7},{6,4},{7,5},{8,10},{9,11},{10,... | collective-permute-start | bytes 786440 | tf_op jit(solution)/shard_map/ppermute | solution.py:27
  166.0 14.0 %collective-permute-start.11 = (bf16[256,16,32]{0,2,1:T(8,128)(2,1)S(1)}, bf16[256,16,32]{0,2,1:T(8,128)(2,1)S(1)}, u32[]{:S(2)}, u32[]{:S(2)}) collective-permute-start(bf16[256,16,32]{0,2,1:T(8,128)(2,1)S(1)} %get-tuple-element.19), channel_id=1, source_target_pairs={{0,1},{1,2},{2,3},{3,0},{4,5},{5,6},{6,7},{7,4},{8,9},{9,10},{10,1... | collective-permute-start | bytes 786440 | tf_op jit(solution)/shard_map/ppermute | solution.py:27
  195.8 4.4 %copy-start.1 = (bf16[256,32,128]{2,1,0:T(8,128)(2,1)S(1)}, bf16[256,32,128]{2,1,0:T(8,128)(2,1)}, u32[]{:S(2)}) copy-start(bf16[256,32,128]{2,1,0:T(8,128)(2,1)} %param.16) | copy-start | bytes 6291460

commit v2 on v1

--- a/solution.py
+++ b/solution.py
@@ -82,24 +82,24 @@
         preferred_element_type=jnp.float32,
     )
     send_rows = jnp.sum(slot_place.astype(jnp.int32) * border_row[None, :], axis=1)
-    send_values = send_values.reshape((sub_count, capacity) + value_shape)
-    send_rows = send_rows.reshape((sub_count, capacity))
-    arrived, arrived_rows = (
-        lax.all_to_all(
-            send_values.astype(jnp.bfloat16), "sub", split_axis=0, concat_axis=0, tiled=True
-        ).astype(jnp.float32),
-        lax.all_to_all(send_rows, "sub", split_axis=0, concat_axis=0, tiled=True),
+    row_block = jnp.zeros((sub_count, 128), jnp.float32)
+    row_block = row_block.at[:, :capacity].set(
+        send_rows.astype(jnp.float32).reshape(sub_count, capacity)
     )
-    incoming = collect(
-        arrived.reshape((sub_count * capacity,) + value_shape), arrived_rows.reshape(-1), row_count
-    )
+    packet = jnp.concatenate([send_values.reshape(sub_count, -1), row_block], axis=1)
+    arrived_packet = lax.all_to_all(packet, "sub", split_axis=0, concat_axis=0, tiled=True)
+    value_width = send_values.shape[1]
+    arrived = arrived_packet[:, : capacity * value_width].reshape(sub_count * capacity, value_width)
+    arrived_rows = arrived_packet[:, capacity * value_width : capacity * value_width + capacity]
+    arrived_rows = arrived_rows.astype(jnp.int32).reshape(-1)
+    incoming = collect(arrived, arrived_rows, row_count).reshape((row_count,) + value_shape)
     residual_low = (own_border - incoming).astype(jnp.bfloat16)
     residual_full = harm_gather(residual_low, 2)
     solved = jnp.einsum(
         "bok,brk->bro", border_inverse, residual_full, preferred_element_type=jnp.float32
     )
     solved, solved_low = (solved, solved.astype(jnp.bfloat16))
-    replies = solved_low[arrived_rows]
+    replies = solved_low[arrived_rows].reshape((sub_count, capacity) + value_shape)
     returned = lax.all_to_all(replies, "sub", split_axis=0, concat_axis=0, tiled=True)
     returned_flat = returned.reshape(sub_count * capacity, -1)
     touch_low = jnp.dot(

time: 201 us -> 202 us (level)
  waiting for transfers between devices: 55 us -> 62.7 us
  local copies, waits for them, and re-layouts: 58.6 us -> 51 us
    ppermute x12, waiting for transfers between devices: 29.3 us -> 33.9 us  [harm_gather(): lax.ppermute(values, 'harm', [(i, (i + s) % count) for i in range(count)])]
    all_to_all x2 -> x1, starting transfers between devices: 17.7 us -> 13.2 us  [on_device(): lax.all_to_all(packet, 'sub', split_axis=0, concat_axis=0, tiled=True)]
    ppermute x12, starting transfers between devices: 13.4 us -> 17.3 us  [harm_gather(): lax.ppermute(values, 'harm', [(i, (i + s) % count) for i in range(count)])]
    unnamed x47 -> x46, local copies, waits for them, and re-layouts: 20.6 us -> 17.2 us
    another operation x2 -> x3, local copies, waits for them, and re-layouts: 3.41 us -> 0.27 us  [the longest x1 3.4 us: collect(): flat_rows = values.reshape(values.shape[0], -1)]
    all_to_all x2 -> x1, waiting for transfers between devices: 25.7 us -> 28.8 us  [on_device(): lax.all_to_all(packet, 'sub', split_axis=0, concat_axis=0, tiled=True)]
  transfers between devices with their start and end apart: 14 -> 13, of which waited for: 9 -> 9; matrix products, arithmetic and copies ran while one was open for 3% -> 3% of each run, Pallas kernels for 0% -> 0%
where the time goes in v2:
time: 202 us; the launch traced here: 201 us
  waiting for transfers between devices  62.7 us (31%)
  local copies, waits for them, and re-layouts  51 us (25%)
  starting transfers between devices  30.5 us (15%)
  matrix products  27 us (13%)
  blocking collectives  25.1 us (12%)
  other arithmetic  3.83 us (2%)
    ppermute x12, waiting for transfers between devices, harm_gather(): lax.ppermute(values, 'harm', [(i, (i + s) % count) for i in range(count)])  33.9 us
    all_to_all x1, waiting for transfers between devices, on_device(): lax.all_to_all(packet, 'sub', split_axis=0, concat_axis=0, tiled=True)  28.8 us
    all_to_all x1, blocking collectives, on_device(): lax.all_to_all(replies, 'sub', split_axis=0, concat_axis=0, tiled=True)  25.1 us
    ppermute x12, starting transfers between devices, harm_gather(): lax.ppermute(values, 'harm', [(i, (i + s) % count) for i in range(count)])  17.3 us
    unnamed x46, local copies, waits for them, and re-layouts  17.2 us
    dot_general x3, matrix products, tile_product(): jnp.einsum('tok,trk->tro', tile_set, columns, preferred_element_type=jnp....  16.9 us
    all_to_all x1, starting transfers between devices, on_device(): lax.all_to_all(packet, 'sub', split_axis=0, concat_axis=0, tiled=True)  13.2 us
    dot_general x3, local copies, waits for them, and re-layouts, tile_product(): jnp.einsum('tok,trk->tro', tile_set, columns, preferred_element_type=jnp....  6.81 us
  transfers between devices with their start and end apart: 13, of which 9 were waited for; matrix products, arithmetic and copies ran while one was open for 3% of the time, Pallas kernels for 0%

profile of v2, /device:TPU:1, one launch (start us, length us, event | category | flops | bytes accessed | tf_op | source)
XLA Modules:
  0.0 201.3 jit_solution(3439293582154139572)
XLA Ops:
  2.2 2.2 %copy.72 = bf16[16,128,256]{1,0,2:T(8,128)(2,1)S(1)} copy(f32[16,128,256]{2,1,0:T(8,128)} %param.13) | data formatting | bytes 3145728 | tf_op args[0]
  4.4 2.7 %gather_fusion = bf16[512,16,128]{2,1,0:T(8,128)(2,1)} fusion(bf16[256,16,128]{2,1,0:T(8,128)(2,1)S(1)} %bitcast.152, s32[1024]{0:T(1024)S(1)} %get-tuple-element.33), kind=kCustom, calls=%fused_computation | custom fusion | bytes 4196352 | tf_op jit(solution)/shard_map/gather | solution.py:61
  7.1 7.1 %fusion.25 = f32[512,16,32]{2,1,0:T(8,128)} fusion(bf16[512,16,128]{2,1,0:T(8,128)(2,1)} %gather_fusion, bf16[512,32,128]{2,1,0:T(8,128)(2,1)} %param.15), kind=kOutput, calls=%fused_computation.89 | convolution fusion | flops 67108864 | bytes 7340032 | tf_op jit(solution)/shard_map/tok,trk->tro/dot_general | solution.py:19
  14.2 2.8 %copy.73 = f32[512,16,32]{0,2,1:T(8,128)S(1)} copy(f32[512,16,32]{2,1,0:T(8,128)} %fusion.25) | data formatting | bytes 2097152 | tf_op jit(solution)/shard_map/tok,trk->tro/dot_general | solution.py:19
  18.4 2.1 %collective-permute-start.2 = (bf16[256,16,32]{0,2,1:T(8,128)(2,1)S(1)}, bf16[256,16,32]{0,2,1:T(8,128)(2,1)S(1)}, u32[]{:S(2)}, u32[]{:S(2)}) collective-permute-start(bf16[256,16,32]{0,2,1:T(8,128)(2,1)S(1)} %get-tuple-element.25), channel_id=1, source_target_pairs={{0,1},{1,2},{2,3},{3,0},{4,5},{5,6},{6,7},{7,4},{8,9},{9,10},{10,1... | collective-permute-start | bytes 786440 | tf_op jit(solution)/shard_map/ppermute | solution.py:27
  20.6 2.6 %collective-permute-start.1 = (bf16[256,16,32]{0,2,1:T(8,128)(2,1)S(1)}, bf16[256,16,32]{0,2,1:T(8,128)(2,1)S(1)}, u32[]{:S(2)}, u32[]{:S(2)}) collective-permute-start(bf16[256,16,32]{0,2,1:T(8,128)(2,1)S(1)} %get-tuple-element.25), channel_id=1, source_target_pairs={{0,2},{1,3},{2,0},{3,1},{4,6},{5,7},{6,4},{7,5},{8,10},{9,11},{10,... | collective-permute-start | bytes 786440 | tf_op jit(solution)/shard_map/ppermute | solution.py:27
  26.8 6.7 %collective-permute-done = bf16[256,16,32]{0,2,1:T(8,128)(2,1)S(1)} collective-permute-done((bf16[256,16,32]{0,2,1:T(8,128)(2,1)S(1)}, bf16[256,16,32]{0,2,1:T(8,128)(2,1)S(1)}, u32[]{:S(2)}, u32[]{:S(2)}) %collective-permute-start) | collective-permute-done | bytes 262176 | tf_op jit(solution)/shard_map/ppermute | solution.py:27
  40.2 1.8 copy.75
  42.0 2.1 %gather_fusion.1 = bf16[256,16,128]{2,1,0:T(8,128)(2,1)S(1)} fusion(bf16[256,16,128]{2,1,0:T(8,128)(2,1)} %copy.75, s32[1024]{0:T(1024)S(1)} %get-tuple-element.32), kind=kCustom, calls=%fused_computation.1 | custom fusion | bytes 2098176 | tf_op jit(solution)/shard_map/gather | solution.py:66
  44.1 2.5 %fusion.26 = f32[256,16,32]{2,1,0:T(8,128)} fusion(bf16[256,16,128]{2,1,0:T(8,128)(2,1)S(1)} %gather_fusion.1, bf16[256,32,128]{2,1,0:T(8,128)(2,1)S(1)} %copy-done), kind=kOutput, calls=%fused_computation.90 | convolution fusion | flops 33554432 | bytes 3670016 | tf_op jit(solution)/shard_map/tok,trk->tro/dot_general | solution.py:65
  46.6 2.5 %copy.76 = f32[256,16,32]{0,2,1:T(8,128)S(1)} copy(f32[256,16,32]{2,1,0:T(8,128)} %fusion.26) | data formatting | bytes 1048576 | tf_op jit(solution)/shard_map/tok,trk->tro/dot_general | solution.py:65
  50.1 1.7 all_to_all.11
  51.8 13.2 %all-to-all-start = ((f32[64,1,4224]{2,1,0:T(1,128)}), f32[64,1,4224]{2,1,0:T(1,128)S(1)}, u32[]{:S(2)}, u32[]{:S(2)}) async-start(f32[64,1,4224]{2,1,0:T(1,128)} %all_to_all.11), calls=%async_computation | async-start | bytes 2162688 | tf_op jit(solution)/shard_map/all_to_all | solution.py:90
  65.0 28.8 %all-to-all-done = f32[64,1,4224]{2,1,0:T(1,128)S(1)} async-done(((f32[64,1,4224]{2,1,0:T(1,128)}), f32[64,1,4224]{2,1,0:T(1,128)S(1)}, u32[]{:S(2)}, u32[]{:S(2)}) %all-to-all-start) | async-done | bytes 1081376 | tf_op jit(solution)/shard_map/all_to_all | solution.py:90
  97.9 2.1 %collective-permute-start.4 = (bf16[32,16,32]{2,0,1:T(8,128)(2,1)S(1)}, bf16[32,16,32]{2,0,1:T(8,128)(2,1)S(1)}, u32[]{:S(2)}, u32[]{:S(2)}) collective-permute-start(bf16[32,16,32]{2,0,1:T(8,128)(2,1)S(1)} %get-tuple-element.27), channel_id=1, source_target_pairs={{0,2},{1,3},{2,0},{3,1},{4,6},{5,7},{6,4},{7,5},{8,10},{9,11},{10,... | collective-permute-start | bytes 98312 | tf_op jit(solution)/shard_map/ppermute | solution.py:27
  101.4 3.6 %collective-permute-done.3 = bf16[32,16,32]{2,0,1:T(8,128)(2,1)S(1)} collective-permute-done((bf16[32,16,32]{2,0,1:T(8,128)(2,1)S(1)}, bf16[32,16,32]{2,0,1:T(8,128)(2,1)S(1)}, u32[]{:S(2)}, u32[]{:S(2)}) %collective-permute-start.3) | collective-permute-done | bytes 32800 | tf_op jit(solution)/shard_map/ppermute | solution.py:27
  106.3 2.8 %gather_fusion.2 = bf16[512,16,32]{2,1,0:T(8,128)(2,1)} fusion(bf16[32,16,32]{2,1,0:T(8,128)(2,1)S(1)} %get-tuple-element.28, s32[1024]{0:T(1024)S(1)} %pad_clamp_fusion), kind=kCustom, calls=%fused_computation.2 | custom fusion | bytes 1050624 | tf_op jit(solution)/shard_map/gather | solution.py:102
  109.1 3.7 %reshape.201 = bf16[64,2,2048]{2,1,0:T(2,128)(2,1)S(1)} reshape(bf16[64,8,16,32]{3,2,1,0:T(8,128)(2,1)} %bitcast.153) | data formatting | bytes 1048576
  112.8 25.1 %all_to_all.17 = bf16[64,2,2048]{2,1,0:T(2,128)(2,1)S(1)} all-to-all(bf16[64,2,2048]{2,1,0:T(2,128)(2,1)S(1)} %reshape.201), channel_id=1, replica_groups=mesh['sub'=64,'harm'=4] {'sub'}, dimensions={0} | all-to-all | bytes 1048576 | tf_op jit(solution)/shard_map/all_to_all | solution.py:103
  138.9 2.1 %reshape.156 = bf16[512,512]{1,0:T(8,128)(2,1)S(1)} reshape(bf16[64,8,16,32]{3,2,1,0:T(8,128)(2,1)S(1)} %reshape.202) | data formatting | bytes 1048576 | tf_op jit(solution)/shard_map/reshape | solution.py:104
  141.5 2.5 %collective-permute-start.6 = (bf16[256,16,32]{0,2,1:T(8,128)(2,1)S(1)}, bf16[256,16,32]{0,2,1:T(8,128)(2,1)S(1)}, u32[]{:S(2)}, u32[]{:S(2)}) collective-permute-start(bf16[256,16,32]{0,2,1:T(8,128)(2,1)S(1)} %bitcast.160), channel_id=1, source_target_pairs={{0,3},{1,0},{2,1},{3,2},{4,7},{5,4},{6,5},{7,6},{8,11},{9,8},{10,9... | collective-permute-start | bytes 786440 | tf_op jit(solution)/shard_map/ppermute | solution.py:27
  143.9 1.8 collective-permute-start.7
  145.7 4.2 %collective-permute-done.6 = bf16[256,16,32]{0,2,1:T(8,128)(2,1)S(1)} collective-permute-done((bf16[256,16,32]{0,2,1:T(8,128)(2,1)S(1)}, bf16[256,16,32]{0,2,1:T(8,128)(2,1)S(1)}, u32[]{:S(2)}, u32[]{:S(2)}) %collective-permute-start.6) | collective-permute-done | bytes 262176 | tf_op jit(solution)/shard_map/ppermute | solution.py:27
  149.9 7.2 %collective-permute-done.7 = bf16[256,16,32]{0,2,1:T(8,128)(2,1)S(1)} collective-permute-done((bf16[256,16,32]{0,2,1:T(8,128)(2,1)S(1)}, bf16[256,16,32]{0,2,1:T(8,128)(2,1)S(1)}, u32[]{:S(2)}, u32[]{:S(2)}) %collective-permute-start.7) | collective-permute-done | bytes 262176 | tf_op jit(solution)/shard_map/ppermute | solution.py:27
  158.5 2.8 %fusion.27 = f32[256,16,32]{2,1,0:T(8,128)S(1)} fusion(bf16[256,16,128]{2,1,0:T(8,128)(2,1)S(1)} %copy.82, bf16[256,32,128]{2,1,0:T(8,128)(2,1)} %param.19), kind=kOutput, calls=%fused_computation.91 | convolution fusion | flops 33554432 | bytes 3670016 | tf_op jit(solution)/shard_map/tok,trk->tro/dot_general | solution.py:19
  162.3 2.2 %bitcast_dynamic-update-slice_fusion.6 = (bf16[8,256,16,32]{1,3,2,0:T(8,128)(2,1)}, bf16[256,16,32]{0,2,1:T(8,128)(2,1)S(1)}) fusion(f32[256,16,32]{0,2,1:T(8,128)S(1)} %copy.83, s32[256]{0:T(256)S(1)} %copy-done.6, f32[16,128,256]{2,1,0:T(8,128)} %param.13, s32[]{:T(128)S(6)} %select_n.40), kind=kOutput, calls=%fused_computation.33 | convolution fusion | flops 402980864 | bytes 1573892 | tf_op jit(solution)/shard_map/dot_general | solution.py:12
  167.7 3.0 %collective-permute-done.9 = bf16[256,16,32]{0,2,1:T(8,128)(2,1)S(1)} collective-permute-done((bf16[256,16,32]{0,2,1:T(8,128)(2,1)S(1)}, bf16[256,16,32]{0,2,1:T(8,128)(2,1)S(1)}, u32[]{:S(2)}, u32[]{:S(2)}) %collective-permute-start.9) | collective-permute-done | bytes 262176 | tf_op jit(solution)/shard_map/ppermute | solution.py:27
  171.5 2.1 %collective-permute-done.10 = bf16[256,16,32]{0,2,1:T(8,128)(2,1)S(1)} collective-permute-done((bf16[256,16,32]{0,2,1:T(8,128)(2,1)S(1)}, bf16[256,16,32]{0,2,1:T(8,128)(2,1)S(1)}, u32[]{:S(2)}, u32[]{:S(2)}) %collective-permute-start.10) | collective-permute-done | bytes 262176 | tf_op jit(solution)/shard_map/ppermute | solution.py:27
  174.3 6.7 %collective-permute-done.11 = bf16[256,16,32]{0,2,1:T(8,128)(2,1)S(1)} collective-permute-done((bf16[256,16,32]{0,2,1:T(8,128)(2,1)S(1)}, bf16[256,16,32]{0,2,1:T(8,128)(2,1)S(1)}, u32[]{:S(2)}, u32[]{:S(2)}) %collective-permute-start.11) | collective-permute-done | bytes 262176 | tf_op jit(solution)/shard_map/ppermute | solution.py:27
  187.1 2.7 %gather_fusion.3 = bf16[512,16,128]{2,1,0:T(8,128)(2,1)} fusion(bf16[256,16,128]{2,1,0:T(8,128)(2,1)S(1)} %copy.85, s32[1024]{0:T(1024)S(1)} %get-tuple-element.33), kind=kCustom, calls=%fused_computation.3 | custom fusion | bytes 4196352 | tf_op jit(solution)/shard_map/gather | solution.py:113
  189.8 7.1 %fusion.28 = f32[512,16,32]{2,1,0:T(8,128)} fusion(bf16[512,16,128]{2,1,0:T(8,128)(2,1)} %gather_fusion.3, bf16[512,32,128]{2,1,0:T(8,128)(2,1)} %param.15), kind=kOutput, calls=%fused_computation.92 | convolution fusion | flops 67108864 | bytes 7340032 | tf_op jit(solution)/shard_map/tok,trk->tro/dot_general | solution.py:19
  196.9 2.9 %copy.86 = f32[512,16,32]{0,2,1:T(8,128)S(1)} copy(f32[512,16,32]{2,1,0:T(8,128)} %fusion.28) | data formatting | bytes 2097152 | tf_op jit(solution)/shard_map/tok,trk->tro/dot_general | solution.py:19
  (103 shorter events, 36.8 us)
Async XLA Ops:
  0.6 43.4 %copy-start = (bf16[256,32,128]{2,1,0:T(8,128)(2,1)S(1)}, bf16[256,32,128]{2,1,0:T(8,128)(2,1)}, u32[]{:S(2)}) copy-start(bf16[256,32,128]{2,1,0:T(8,128)(2,1)} %param.18) | copy-start | bytes 6291460
  14.2 2.9 %copy-start.5 = (s32[512]{0:T(512)S(1)}, s32[512]{0:T(512)}, u32[]{:S(2)}) copy-start(s32[512]{0:T(512)} %param.16) | copy-start | bytes 6148
  14.2 10.0 %copy-start.4 = (s32[256,1]{0,1:T(1,128)S(1)}, s32[256,1]{0,1:T(1,128)}, u32[]{:S(2)}) copy-start(s32[256,1]{0,1:T(1,128)} %param.21) | copy-start | bytes 3076
  14.2 11.0 %copy-start.7 = (s32[256]{0:T(256)S(1)}, s32[256]{0:T(256)}, u32[]{:S(2)}) copy-start(s32[256]{0:T(256)} %param.22) | copy-start | bytes 3076
  18.4 16.8 %collective-permute-start.2 = (bf16[256,16,32]{0,2,1:T(8,128)(2,1)S(1)}, bf16[256,16,32]{0,2,1:T(8,128)(2,1)S(1)}, u32[]{:S(2)}, u32[]{:S(2)}) collective-permute-start(bf16[256,16,32]{0,2,1:T(8,128)(2,1)S(1)} %get-tuple-element.25), channel_id=1, source_target_pairs={{0,1},{1,2},{2,3},{3,0},{4,5},{5,6},{6,7},{7,4},{8,9},{9,10},{10,1... | collective-permute-start | bytes 786440 | tf_op jit(solution)/shard_map/ppermute | solution.py:27
  20.6 14.0 %collective-permute-start.1 = (bf16[256,16,32]{0,2,1:T(8,128)(2,1)S(1)}, bf16[256,16,32]{0,2,1:T(8,128)(2,1)S(1)}, u32[]{:S(2)}, u32[]{:S(2)}) collective-permute-start(bf16[256,16,32]{0,2,1:T(8,128)(2,1)S(1)} %get-tuple-element.25), channel_id=1, source_target_pairs={{0,2},{1,3},{2,0},{3,1},{4,6},{5,7},{6,4},{7,5},{8,10},{9,11},{10,... | collective-permute-start | bytes 786440 | tf_op jit(solution)/shard_map/ppermute | solution.py:27
  23.2 10.3 %collective-permute-start = (bf16[256,16,32]{0,2,1:T(8,128)(2,1)S(1)}, bf16[256,16,32]{0,2,1:T(8,128)(2,1)S(1)}, u32[]{:S(2)}, u32[]{:S(2)}) collective-permute-start(bf16[256,16,32]{0,2,1:T(8,128)(2,1)S(1)} %get-tuple-element.25), channel_id=1, source_target_pairs={{0,3},{1,0},{2,1},{3,2},{4,7},{5,4},{6,5},{7,6},{8,11},{9,8},{10,9... | collective-permute-start | bytes 786440 | tf_op jit(solution)/shard_map/ppermute | solution.py:27
  51.8 42.0 %all-to-all-start = ((f32[64,1,4224]{2,1,0:T(1,128)}), f32[64,1,4224]{2,1,0:T(1,128)S(1)}, u32[]{:S(2)}, u32[]{:S(2)}) async-start(f32[64,1,4224]{2,1,0:T(1,128)} %all_to_all.11), calls=%async_computation | async-start | bytes 2162688 | tf_op jit(solution)/shard_map/all_to_all | solution.py:90
  94.1 1.0 copy-start.3
  96.4 8.7 %collective-permute-start.5 = (bf16[32,16,32]{2,0,1:T(8,128)(2,1)S(1)}, bf16[32,16,32]{2,0,1:T(8,128)(2,1)S(1)}, u32[]{:S(2)}, u32[]{:S(2)}) collective-permute-start(bf16[32,16,32]{2,0,1:T(8,128)(2,1)S(1)} %get-tuple-element.27), channel_id=1, source_target_pairs={{0,1},{1,2},{2,3},{3,0},{4,5},{5,6},{6,7},{7,4},{8,9},{9,10},{10,1... | collective-permute-start | bytes 98312 | tf_op jit(solution)/shard_map/ppermute | solution.py:27
  97.9 7.2 %collective-permute-start.4 = (bf16[32,16,32]{2,0,1:T(8,128)(2,1)S(1)}, bf16[32,16,32]{2,0,1:T(8,128)(2,1)S(1)}, u32[]{:S(2)}, u32[]{:S(2)}) collective-permute-start(bf16[32,16,32]{2,0,1:T(8,128)(2,1)S(1)} %get-tuple-element.27), channel_id=1, source_target_pairs={{0,2},{1,3},{2,0},{3,1},{4,6},{5,7},{6,4},{7,5},{8,10},{9,11},{10,... | collective-permute-start | bytes 98312 | tf_op jit(solution)/shard_map/ppermute | solution.py:27
  100.0 5.0 %collective-permute-start.3 = (bf16[32,16,32]{2,0,1:T(8,128)(2,1)S(1)}, bf16[32,16,32]{2,0,1:T(8,128)(2,1)S(1)}, u32[]{:S(2)}, u32[]{:S(2)}) collective-permute-start(bf16[32,16,32]{2,0,1:T(8,128)(2,1)S(1)} %get-tuple-element.27), channel_id=1, source_target_pairs={{0,3},{1,0},{2,1},{3,2},{4,7},{5,4},{6,5},{7,6},{8,11},{9,8},{10,9... | collective-permute-start | bytes 98312 | tf_op jit(solution)/shard_map/ppermute | solution.py:27
  105.1 1.0 copy-start.2
  141.5 8.4 %collective-permute-start.6 = (bf16[256,16,32]{0,2,1:T(8,128)(2,1)S(1)}, bf16[256,16,32]{0,2,1:T(8,128)(2,1)S(1)}, u32[]{:S(2)}, u32[]{:S(2)}) collective-permute-start(bf16[256,16,32]{0,2,1:T(8,128)(2,1)S(1)} %bitcast.160), channel_id=1, source_target_pairs={{0,3},{1,0},{2,1},{3,2},{4,7},{5,4},{6,5},{7,6},{8,11},{9,8},{10,9... | collective-permute-start | bytes 786440 | tf_op jit(solution)/shard_map/ppermute | solution.py:27
  143.9 13.2 %collective-permute-start.8 = (bf16[256,16,32]{0,2,1:T(8,128)(2,1)S(1)}, bf16[256,16,32]{0,2,1:T(8,128)(2,1)S(1)}, u32[]{:S(2)}, u32[]{:S(2)}) collective-permute-start(bf16[256,16,32]{0,2,1:T(8,128)(2,1)S(1)} %bitcast.161), channel_id=1, source_target_pairs={{0,1},{1,2},{2,3},{3,0},{4,5},{5,6},{6,7},{7,4},{8,9},{9,10},{10,1... | collective-permute-start | bytes 786440 | tf_op jit(solution)/shard_map/ppermute | solution.py:27
  143.9 13.1 %collective-permute-start.7 = (bf16[256,16,32]{0,2,1:T(8,128)(2,1)S(1)}, bf16[256,16,32]{0,2,1:T(8,128)(2,1)S(1)}, u32[]{:S(2)}, u32[]{:S(2)}) collective-permute-start(bf16[256,16,32]{0,2,1:T(8,128)(2,1)S(1)} %bitcast.162), channel_id=1, source_target_pairs={{0,2},{1,3},{2,0},{3,1},{4,6},{5,7},{6,4},{7,5},{8,10},{9,11},{10,... | collective-permute-start | bytes 786440 | tf_op jit(solution)/shard_map/ppermute | solution.py:27
  161.3 1.0 copy-start.6
  164.5 6.2 %collective-permute-start.9 = (bf16[256,16,32]{0,2,1:T(8,128)(2,1)S(1)}, bf16[256,16,32]{0,2,1:T(8,128)(2,1)S(1)}, u32[]{:S(2)}, u32[]{:S(2)}) collective-permute-start(bf16[256,16,32]{0,2,1:T(8,128)(2,1)S(1)} %get-tuple-element.31), channel_id=1, source_target_pairs={{0,3},{1,0},{2,1},{3,2},{4,7},{5,4},{6,5},{7,6},{8,11},{9,8},{10,9... | collective-permute-start | bytes 786440 | tf_op jit(solution)/shard_map/ppermute | solution.py:27
  165.7 7.9 %collective-permute-start.10 = (bf16[256,16,32]{0,2,1:T(8,128)(2,1)S(1)}, bf16[256,16,32]{0,2,1:T(8,128)(2,1)S(1)}, u32[]{:S(2)}, u32[]{:S(2)}) collective-permute-start(bf16[256,16,32]{0,2,1:T(8,128)(2,1)S(1)} %get-tuple-element.31), channel_id=1, source_target_pairs={{0,2},{1,3},{2,0},{3,1},{4,6},{5,7},{6,4},{7,5},{8,10},{9,11},{10,... | collective-permute-start | bytes 786440 | tf_op jit(solution)/shard_map/ppermute | solution.py:27
  166.8 14.2 %collective-permute-start.11 = (bf16[256,16,32]{0,2,1:T(8,128)(2,1)S(1)}, bf16[256,16,32]{0,2,1:T(8,128)(2,1)S(1)}, u32[]{:S(2)}, u32[]{:S(2)}) collective-permute-start(bf16[256,16,32]{0,2,1:T(8,128)(2,1)S(1)} %get-tuple-element.31), channel_id=1, source_target_pairs={{0,1},{1,2},{2,3},{3,0},{4,5},{5,6},{6,7},{7,4},{8,9},{9,10},{10,1... | collective-permute-start | bytes 786440 | tf_op jit(solution)/shard_map/ppermute | solution.py:27
  196.9 4.4 %copy-start.1 = (bf16[256,32,128]{2,1,0:T(8,128)(2,1)S(1)}, bf16[256,32,128]{2,1,0:T(8,128)(2,1)}, u32[]{:S(2)}) copy-start(bf16[256,32,128]{2,1,0:T(8,128)(2,1)} %param.18) | copy-start | bytes 6291460

commit v3 on v2

--- a/solution.py
+++ b/solution.py
@@ -27,12 +27,14 @@
         lax.ppermute(values, "harm", [(i, (i + s) % count) for i in range(count)])
         for s in range(1, count)
     ]
-    ahead = jnp.stack([parts[(-m) % count] for m in range(count)] * 2, 0)
-    ordered = lax.dynamic_slice_in_dim(ahead, (count - own) % count, count, 0)
-    ordered = jnp.moveaxis(ordered, 0, axis)
-    shape = values.shape[:axis] + (count * values.shape[axis],) + values.shape[axis + 1 :]
-    return ordered.reshape(shape)
-
+    blocks = []
+    for block in range(count):
+        source = (own - block) % count
+        chosen = parts[0]
+        for s in range(1, count):
+            chosen = jnp.where(source == s, parts[s], chosen)
+        blocks.append(chosen)
+    return jnp.concatenate(blocks, axis)
 
 def on_device(
     right_side,

time: 202 us -> 200 us (0.990)
  local copies, waits for them, and re-layouts: 51 us -> 45.4 us
  other arithmetic: 3.83 us -> 5.94 us
    unnamed x46 -> x19, local copies, waits for them, and re-layouts: 17.2 us -> 8.97 us
    concatenate x0 -> x3, local copies, waits for them, and re-layouts: none -> 5.64 us  [harm_gather(): return jnp.concatenate(blocks, axis)]
    reshape x4 -> x0, local copies, waits for them, and re-layouts: 4.22 us -> none  [harm_gather(): return ordered.reshape(shape)]
    transpose x8 -> x0, local copies, waits for them, and re-layouts: 3.37 us -> none  [harm_gather(): ordered = jnp.moveaxis(ordered, 0, axis)]
    concatenate x0 -> x4, other arithmetic: none -> 2.34 us  [harm_gather(): return jnp.concatenate(blocks, axis)]
    reshape x2, local copies, waits for them, and re-layouts: 0.52 us -> 2.71 us  [on_device(): arrived_packet[:, :capacity * value_width]]
  transfers between devices with their start and end apart: 13 -> 13, of which waited for: 9 -> 9; matrix products, arithmetic and copies ran while one was open for 3% -> 2% of each run, Pallas kernels for 0% -> 0%
where the time goes in v3:
time: 200 us; the launch traced here: 199 us
  waiting for transfers between devices  61.7 us (31%)
  local copies, waits for them, and re-layouts  45.4 us (23%)
  starting transfers between devices  32 us (16%)
  matrix products  28 us (14%)
  blocking collectives  25.2 us (13%)
  other arithmetic  5.94 us (3%)
    ppermute x12, waiting for transfers between devices, harm_gather(): lax.ppermute(values, 'harm', [(i, (i + s) % count) for i in range(count)])  32.8 us
    all_to_all x1, waiting for transfers between devices, on_device(): lax.all_to_all(packet, 'sub', split_axis=0, concat_axis=0, tiled=True)  28.8 us
    all_to_all x1, blocking collectives, on_device(): lax.all_to_all(replies, 'sub', split_axis=0, concat_axis=0, tiled=True)  25.2 us
    ppermute x12, starting transfers between devices, harm_gather(): lax.ppermute(values, 'harm', [(i, (i + s) % count) for i in range(count)])  19 us
    dot_general x3, matrix products, tile_product(): jnp.einsum('tok,trk->tro', tile_set, columns, preferred_element_type=jnp....  18.3 us
    all_to_all x1, starting transfers between devices, on_device(): lax.all_to_all(packet, 'sub', split_axis=0, concat_axis=0, tiled=True)  13 us
    unnamed x19, local copies, waits for them, and re-layouts  8.97 us
    dot_general x3, local copies, waits for them, and re-layouts, tile_product(): jnp.einsum('tok,trk->tro', tile_set, columns, preferred_element_type=jnp....  8.14 us
  transfers between devices with their start and end apart: 13, of which 9 were waited for; matrix products, arithmetic and copies ran while one was open for 2% of the time, Pallas kernels for 0%

profile of v3, /device:TPU:1, one launch (start us, length us, event | category | flops | bytes accessed | tf_op | source)
XLA Modules:
  0.0 199.2 jit_solution(3623306569708942531)
XLA Ops:
  1.5 2.2 %copy.51 = bf16[16,128,256]{1,0,2:T(8,128)(2,1)S(1)} copy(f32[16,128,256]{2,1,0:T(8,128)} %param.13) | data formatting | bytes 3145728 | tf_op args[0]
  3.7 2.7 %gather_fusion = bf16[512,16,128]{2,1,0:T(8,128)(2,1)} fusion(bf16[256,16,128]{2,1,0:T(8,128)(2,1)S(1)} %bitcast.84, s32[1024]{0:T(1024)S(1)} %pad_clamp_fusion.2), kind=kCustom, calls=%fused_computation | custom fusion | bytes 4196352 | tf_op jit(solution)/shard_map/gather | solution.py:63
  6.4 7.1 %fusion.27 = f32[512,16,32]{2,1,0:T(8,128)} fusion(bf16[512,16,128]{2,1,0:T(8,128)(2,1)} %gather_fusion, bf16[512,32,128]{2,1,0:T(8,128)(2,1)} %param.15), kind=kOutput, calls=%fused_computation.75 | convolution fusion | flops 67108864 | bytes 7340032 | tf_op jit(solution)/shard_map/tok,trk->tro/dot_general | solution.py:19
  13.5 2.8 %copy.52 = f32[512,16,32]{0,2,1:T(8,128)S(1)} copy(f32[512,16,32]{2,1,0:T(8,128)} %fusion.27) | data formatting | bytes 2097152 | tf_op jit(solution)/shard_map/tok,trk->tro/dot_general | solution.py:19
  17.1 2.2 %collective-permute-start.2 = (bf16[256,16,32]{0,2,1:T(8,128)(2,1)S(1)}, bf16[256,16,32]{0,2,1:T(8,128)(2,1)S(1)}, u32[]{:S(2)}, u32[]{:S(2)}) collective-permute-start(bf16[256,16,32]{0,2,1:T(8,128)(2,1)S(1)} %convolution_convert_fusion.1), channel_id=1, source_target_pairs={{0,1},{1,2},{2,3},{3,0},{4,5},{5,6},{6,7},{7,4},{8,9},{9,10},{10,1... | collective-permute-start | bytes 786440 | tf_op jit(solution)/shard_map/ppermute | solution.py:27
  19.3 2.6 %collective-permute-start.1 = (bf16[256,16,32]{0,2,1:T(8,128)(2,1)S(1)}, bf16[256,16,32]{0,2,1:T(8,128)(2,1)S(1)}, u32[]{:S(2)}, u32[]{:S(2)}) collective-permute-start(bf16[256,16,32]{0,2,1:T(8,128)(2,1)S(1)} %convolution_convert_fusion.1), channel_id=1, source_target_pairs={{0,2},{1,3},{2,0},{3,1},{4,6},{5,7},{6,4},{7,5},{8,10},{9,11},{10,... | collective-permute-start | bytes 786440 | tf_op jit(solution)/shard_map/ppermute | solution.py:27
  25.5 7.7 %collective-permute-done.1 = bf16[256,16,32]{0,2,1:T(8,128)(2,1)S(1)} collective-permute-done((bf16[256,16,32]{0,2,1:T(8,128)(2,1)S(1)}, bf16[256,16,32]{0,2,1:T(8,128)(2,1)S(1)}, u32[]{:S(2)}, u32[]{:S(2)}) %collective-permute-start.1) | collective-permute-done | bytes 262176 | tf_op jit(solution)/shard_map/ppermute | solution.py:27
  35.2 2.1 %gather_fusion.1 = bf16[256,16,128]{2,1,0:T(8,128)(2,1)S(1)} fusion(bf16[256,16,128]{2,1,0:T(8,128)(2,1)} %copy.53, s32[1024]{0:T(1024)S(1)} %pad_clamp_fusion.1), kind=kCustom, calls=%fused_computation.1 | custom fusion | bytes 2098176 | tf_op jit(solution)/shard_map/gather | solution.py:68
  37.3 2.6 %fusion.28 = f32[256,16,32]{2,1,0:T(8,128)} fusion(bf16[256,16,128]{2,1,0:T(8,128)(2,1)S(1)} %gather_fusion.1, bf16[256,32,128]{2,1,0:T(8,128)(2,1)S(1)} %copy-done), kind=kOutput, calls=%fused_computation.76 | convolution fusion | flops 33554432 | bytes 3670016 | tf_op jit(solution)/shard_map/tok,trk->tro/dot_general | solution.py:67
  39.9 2.5 %copy.54 = f32[256,16,32]{0,2,1:T(8,128)S(1)} copy(f32[256,16,32]{2,1,0:T(8,128)} %fusion.28) | data formatting | bytes 1048576 | tf_op jit(solution)/shard_map/tok,trk->tro/dot_general | solution.py:67
  47.2 13.0 %all-to-all-start = ((f32[64,1,4224]{2,1,0:T(1,128)}), f32[64,1,4224]{2,1,0:T(1,128)S(1)}, u32[]{:S(2)}, u32[]{:S(2)}) async-start(f32[64,1,4224]{2,1,0:T(1,128)} %all_to_all.11), calls=%async_computation | async-start | bytes 2162688 | tf_op jit(solution)/shard_map/all_to_all | solution.py:92
  60.2 28.8 %all-to-all-done = f32[64,1,4224]{2,1,0:T(1,128)S(1)} async-done(((f32[64,1,4224]{2,1,0:T(1,128)}), f32[64,1,4224]{2,1,0:T(1,128)S(1)}, u32[]{:S(2)}, u32[]{:S(2)}) %all-to-all-start) | async-done | bytes 1081376 | tf_op jit(solution)/shard_map/all_to_all | solution.py:92
  94.5 2.1 %collective-permute-start.4 = (bf16[32,16,32]{2,0,1:T(8,128)(2,1)S(1)}, bf16[32,16,32]{2,0,1:T(8,128)(2,1)S(1)}, u32[]{:S(2)}, u32[]{:S(2)}) collective-permute-start(bf16[32,16,32]{2,0,1:T(8,128)(2,1)S(1)} %fusion.1), channel_id=1, source_target_pairs={{0,2},{1,3},{2,0},{3,1},{4,6},{5,7},{6,4},{7,5},{8,10},{9,11},{10,... | collective-permute-start | bytes 98312 | tf_op jit(solution)/shard_map/ppermute | solution.py:27
  98.6 2.9 %collective-permute-done.4 = bf16[32,16,32]{2,0,1:T(8,128)(2,1)S(1)} collective-permute-done((bf16[32,16,32]{2,0,1:T(8,128)(2,1)S(1)}, bf16[32,16,32]{2,0,1:T(8,128)(2,1)S(1)}, u32[]{:S(2)}, u32[]{:S(2)}) %collective-permute-start.4) | collective-permute-done | bytes 32800 | tf_op jit(solution)/shard_map/ppermute | solution.py:27
  102.2 2.8 %gather_fusion.2 = bf16[512,16,32]{2,1,0:T(8,128)(2,1)} fusion(bf16[32,16,32]{2,1,0:T(8,128)(2,1)S(1)} %get-tuple-element.38, s32[1024]{0:T(1024)S(1)} %pad_clamp_fusion), kind=kCustom, calls=%fused_computation.2 | custom fusion | bytes 1050624 | tf_op jit(solution)/shard_map/gather | solution.py:104
  105.0 3.7 %reshape.185 = bf16[64,2,2048]{2,1,0:T(2,128)(2,1)S(1)} reshape(bf16[64,8,16,32]{3,2,1,0:T(8,128)(2,1)} %bitcast.85) | data formatting | bytes 1048576
  108.8 25.2 %all_to_all.17 = bf16[64,2,2048]{2,1,0:T(2,128)(2,1)S(1)} all-to-all(bf16[64,2,2048]{2,1,0:T(2,128)(2,1)S(1)} %reshape.185), channel_id=1, replica_groups=mesh['sub'=64,'harm'=4] {'sub'}, dimensions={0} | all-to-all | bytes 1048576 | tf_op jit(solution)/shard_map/all_to_all | solution.py:105
  134.0 2.0 %reshape.186 = bf16[64,8,16,32]{3,2,1,0:T(8,128)(2,1)} reshape(bf16[64,2,2048]{2,1,0:T(2,128)(2,1)S(1)} %all_to_all.17) | data formatting | bytes 1048576
  136.0 3.4 %reshape.142 = bf16[512,512]{1,0:T(8,128)(2,1)S(1)} reshape(bf16[64,8,16,32]{3,2,1,0:T(8,128)(2,1)} %reshape.186) | data formatting | bytes 1048576 | tf_op jit(solution)/shard_map/reshape | solution.py:106
  141.4 2.1 %collective-permute-start.7 = (bf16[256,16,32]{0,2,1:T(8,128)(2,1)S(1)}, bf16[256,16,32]{0,2,1:T(8,128)(2,1)S(1)}, u32[]{:S(2)}, u32[]{:S(2)}) collective-permute-start(bf16[256,16,32]{0,2,1:T(8,128)(2,1)S(1)} %bitcast.92), channel_id=1, source_target_pairs={{0,2},{1,3},{2,0},{3,1},{4,6},{5,7},{6,4},{7,5},{8,10},{9,11},{10,... | collective-permute-start | bytes 786440 | tf_op jit(solution)/shard_map/ppermute | solution.py:27
  144.4 4.3 %collective-permute-done.8 = bf16[256,16,32]{0,2,1:T(8,128)(2,1)S(1)} collective-permute-done((bf16[256,16,32]{0,2,1:T(8,128)(2,1)S(1)}, bf16[256,16,32]{0,2,1:T(8,128)(2,1)S(1)}, u32[]{:S(2)}, u32[]{:S(2)}) %collective-permute-start.8) | collective-permute-done | bytes 262176 | tf_op jit(solution)/shard_map/ppermute | solution.py:27
  148.7 6.5 %collective-permute-done.7 = bf16[256,16,32]{0,2,1:T(8,128)(2,1)S(1)} collective-permute-done((bf16[256,16,32]{0,2,1:T(8,128)(2,1)S(1)}, bf16[256,16,32]{0,2,1:T(8,128)(2,1)S(1)}, u32[]{:S(2)}, u32[]{:S(2)}) %collective-permute-start.7) | collective-permute-done | bytes 262176 | tf_op jit(solution)/shard_map/ppermute | solution.py:27
  156.3 1.9 copy.58
  158.3 4.1 %fusion.29 = f32[256,16,32]{2,1,0:T(8,128)} fusion(bf16[256,16,128]{2,1,0:T(8,128)(2,1)S(1)} %copy.58, bf16[256,32,128]{2,1,0:T(8,128)(2,1)} %param.19), kind=kOutput, calls=%fused_computation.77 | convolution fusion | flops 33554432 | bytes 3670016 | tf_op jit(solution)/shard_map/tok,trk->tro/dot_general | solution.py:19
  162.4 2.5 %copy.59 = f32[256,16,32]{0,2,1:T(8,128)S(1)} copy(f32[256,16,32]{2,1,0:T(8,128)} %fusion.29) | data formatting | bytes 1048576 | tf_op jit(solution)/shard_map/tok,trk->tro/dot_general | solution.py:19
  168.1 2.4 %collective-permute-start.10 = (bf16[256,16,32]{0,2,1:T(8,128)(2,1)S(1)}, bf16[256,16,32]{0,2,1:T(8,128)(2,1)S(1)}, u32[]{:S(2)}, u32[]{:S(2)}) collective-permute-start(bf16[256,16,32]{0,2,1:T(8,128)(2,1)S(1)} %fusion), channel_id=1, source_target_pairs={{0,2},{1,3},{2,0},{3,1},{4,6},{5,7},{6,4},{7,5},{8,10},{9,11},{10,... | collective-permute-start | bytes 786440 | tf_op jit(solution)/shard_map/ppermute | solution.py:27
  171.5 3.1 %collective-permute-done.11 = bf16[256,16,32]{0,2,1:T(8,128)(2,1)S(1)} collective-permute-done((bf16[256,16,32]{0,2,1:T(8,128)(2,1)S(1)}, bf16[256,16,32]{0,2,1:T(8,128)(2,1)S(1)}, u32[]{:S(2)}, u32[]{:S(2)}) %collective-permute-start.11) | collective-permute-done | bytes 262176 | tf_op jit(solution)/shard_map/ppermute | solution.py:27
  174.6 7.4 %collective-permute-done.10 = bf16[256,16,32]{0,2,1:T(8,128)(2,1)S(1)} collective-permute-done((bf16[256,16,32]{0,2,1:T(8,128)(2,1)S(1)}, bf16[256,16,32]{0,2,1:T(8,128)(2,1)S(1)}, u32[]{:S(2)}, u32[]{:S(2)}) %collective-permute-start.10) | collective-permute-done | bytes 262176 | tf_op jit(solution)/shard_map/ppermute | solution.py:27
  183.2 1.9 copy.60
  185.1 2.7 %gather_fusion.3 = bf16[512,16,128]{2,1,0:T(8,128)(2,1)} fusion(bf16[256,16,128]{2,1,0:T(8,128)(2,1)S(1)} %copy.60, s32[1024]{0:T(1024)S(1)} %pad_clamp_fusion.2), kind=kCustom, calls=%fused_computation.3 | custom fusion | bytes 4196352 | tf_op jit(solution)/shard_map/gather | solution.py:115
  187.8 7.1 %fusion.30 = f32[512,16,32]{2,1,0:T(8,128)} fusion(bf16[512,16,128]{2,1,0:T(8,128)(2,1)} %gather_fusion.3, bf16[512,32,128]{2,1,0:T(8,128)(2,1)} %param.15), kind=kOutput, calls=%fused_computation.78 | convolution fusion | flops 67108864 | bytes 7340032 | tf_op jit(solution)/shard_map/tok,trk->tro/dot_general | solution.py:19
  194.9 2.8 %copy.61 = f32[512,16,32]{0,2,1:T(8,128)S(1)} copy(f32[512,16,32]{2,1,0:T(8,128)} %fusion.30) | data formatting | bytes 2097152 | tf_op jit(solution)/shard_map/tok,trk->tro/dot_general | solution.py:19
  (72 shorter events, 30.8 us)
Async XLA Ops:
  0.6 36.7 %copy-start = (bf16[256,32,128]{2,1,0:T(8,128)(2,1)S(1)}, bf16[256,32,128]{2,1,0:T(8,128)(2,1)}, u32[]{:S(2)}) copy-start(bf16[256,32,128]{2,1,0:T(8,128)(2,1)} %param.18) | copy-start | bytes 6291460
  13.5 2.9 %copy-start.4 = (s32[512]{0:T(512)S(1)}, s32[512]{0:T(512)}, u32[]{:S(2)}) copy-start(s32[512]{0:T(512)} %param.16) | copy-start | bytes 6148
  13.5 10.1 %copy-start.3 = (s32[256,1]{0,1:T(1,128)S(1)}, s32[256,1]{0,1:T(1,128)}, u32[]{:S(2)}) copy-start(s32[256,1]{0,1:T(1,128)} %param.21) | copy-start | bytes 3076
  13.5 11.1 %copy-start.6 = (s32[256]{0:T(256)S(1)}, s32[256]{0:T(256)}, u32[]{:S(2)}) copy-start(s32[256]{0:T(256)} %param.22) | copy-start | bytes 3076
  13.5 12.0 %copy-start.5 = (s32[256]{0:T(256)S(1)}, s32[256]{0:T(256)}, u32[]{:S(2)}) copy-start(s32[256]{0:T(256)} %param.20) | copy-start | bytes 3076
  17.1 8.4 %collective-permute-start.2 = (bf16[256,16,32]{0,2,1:T(8,128)(2,1)S(1)}, bf16[256,16,32]{0,2,1:T(8,128)(2,1)S(1)}, u32[]{:S(2)}, u32[]{:S(2)}) collective-permute-start(bf16[256,16,32]{0,2,1:T(8,128)(2,1)S(1)} %convolution_convert_fusion.1), channel_id=1, source_target_pairs={{0,1},{1,2},{2,3},{3,0},{4,5},{5,6},{6,7},{7,4},{8,9},{9,10},{10,1... | collective-permute-start | bytes 786440 | tf_op jit(solution)/shard_map/ppermute | solution.py:27
  19.3 14.0 %collective-permute-start.1 = (bf16[256,16,32]{0,2,1:T(8,128)(2,1)S(1)}, bf16[256,16,32]{0,2,1:T(8,128)(2,1)S(1)}, u32[]{:S(2)}, u32[]{:S(2)}) collective-permute-start(bf16[256,16,32]{0,2,1:T(8,128)(2,1)S(1)} %convolution_convert_fusion.1), channel_id=1, source_target_pairs={{0,2},{1,3},{2,0},{3,1},{4,6},{5,7},{6,4},{7,5},{8,10},{9,11},{10,... | collective-permute-start | bytes 786440 | tf_op jit(solution)/shard_map/ppermute | solution.py:27
  21.9 11.3 %collective-permute-start = (bf16[256,16,32]{0,2,1:T(8,128)(2,1)S(1)}, bf16[256,16,32]{0,2,1:T(8,128)(2,1)S(1)}, u32[]{:S(2)}, u32[]{:S(2)}) collective-permute-start(bf16[256,16,32]{0,2,1:T(8,128)(2,1)S(1)} %convolution_convert_fusion.1), channel_id=1, source_target_pairs={{0,3},{1,0},{2,1},{3,2},{4,7},{5,4},{6,5},{7,6},{8,11},{9,8},{10,9... | collective-permute-start | bytes 786440 | tf_op jit(solution)/shard_map/ppermute | solution.py:27
  47.2 41.8 %all-to-all-start = ((f32[64,1,4224]{2,1,0:T(1,128)}), f32[64,1,4224]{2,1,0:T(1,128)S(1)}, u32[]{:S(2)}, u32[]{:S(2)}) async-start(f32[64,1,4224]{2,1,0:T(1,128)} %all_to_all.11), calls=%async_computation | async-start | bytes 2162688 | tf_op jit(solution)/shard_map/all_to_all | solution.py:92
  89.4 2.7 %copy-start.2 = (f32[16,128,32]{1,2,0:T(8,128)S(1)}, f32[16,128,32]{1,2,0:T(8,128)}, u32[]{:S(2)}) copy-start(f32[16,128,32]{1,2,0:T(8,128)} %param.14) | copy-start | bytes 786436
  92.1 9.9 %copy-start.1 = (bf16[32,32,128]{2,1,0:T(8,128)(2,1)S(1)}, bf16[32,32,128]{2,1,0:T(8,128)(2,1)}, u32[]{:S(2)}) copy-start(bf16[32,32,128]{2,1,0:T(8,128)(2,1)} %param.23) | copy-start | bytes 786436
  93.5 5.1 %collective-permute-start.5 = (bf16[32,16,32]{2,0,1:T(8,128)(2,1)S(1)}, bf16[32,16,32]{2,0,1:T(8,128)(2,1)S(1)}, u32[]{:S(2)}, u32[]{:S(2)}) collective-permute-start(bf16[32,16,32]{2,0,1:T(8,128)(2,1)S(1)} %fusion.1), channel_id=1, source_target_pairs={{0,1},{1,2},{2,3},{3,0},{4,5},{5,6},{6,7},{7,4},{8,9},{9,10},{10,1... | collective-permute-start | bytes 98312 | tf_op jit(solution)/shard_map/ppermute | solution.py:27
  94.5 7.0 %collective-permute-start.4 = (bf16[32,16,32]{2,0,1:T(8,128)(2,1)S(1)}, bf16[32,16,32]{2,0,1:T(8,128)(2,1)S(1)}, u32[]{:S(2)}, u32[]{:S(2)}) collective-permute-start(bf16[32,16,32]{2,0,1:T(8,128)(2,1)S(1)} %fusion.1), channel_id=1, source_target_pairs={{0,2},{1,3},{2,0},{3,1},{4,6},{5,7},{6,4},{7,5},{8,10},{9,11},{10,... | collective-permute-start | bytes 98312 | tf_op jit(solution)/shard_map/ppermute | solution.py:27
  96.6 5.1 %collective-permute-start.3 = (bf16[32,16,32]{2,0,1:T(8,128)(2,1)S(1)}, bf16[32,16,32]{2,0,1:T(8,128)(2,1)S(1)}, u32[]{:S(2)}, u32[]{:S(2)}) collective-permute-start(bf16[32,16,32]{2,0,1:T(8,128)(2,1)S(1)} %fusion.1), channel_id=1, source_target_pairs={{0,3},{1,0},{2,1},{3,2},{4,7},{5,4},{6,5},{7,6},{8,11},{9,8},{10,9... | collective-permute-start | bytes 98312 | tf_op jit(solution)/shard_map/ppermute | solution.py:27
  139.9 8.8 %collective-permute-start.8 = (bf16[256,16,32]{0,2,1:T(8,128)(2,1)S(1)}, bf16[256,16,32]{0,2,1:T(8,128)(2,1)S(1)}, u32[]{:S(2)}, u32[]{:S(2)}) collective-permute-start(bf16[256,16,32]{0,2,1:T(8,128)(2,1)S(1)} %bitcast.91), channel_id=1, source_target_pairs={{0,1},{1,2},{2,3},{3,0},{4,5},{5,6},{6,7},{7,4},{8,9},{9,10},{10,1... | collective-permute-start | bytes 786440 | tf_op jit(solution)/shard_map/ppermute | solution.py:27
  141.4 13.7 %collective-permute-start.7 = (bf16[256,16,32]{0,2,1:T(8,128)(2,1)S(1)}, bf16[256,16,32]{0,2,1:T(8,128)(2,1)S(1)}, u32[]{:S(2)}, u32[]{:S(2)}) collective-permute-start(bf16[256,16,32]{0,2,1:T(8,128)(2,1)S(1)} %bitcast.92), channel_id=1, source_target_pairs={{0,2},{1,3},{2,0},{3,1},{4,6},{5,7},{6,4},{7,5},{8,10},{9,11},{10,... | collective-permute-start | bytes 786440 | tf_op jit(solution)/shard_map/ppermute | solution.py:27
  143.5 11.6 %collective-permute-start.6 = (bf16[256,16,32]{0,2,1:T(8,128)(2,1)S(1)}, bf16[256,16,32]{0,2,1:T(8,128)(2,1)S(1)}, u32[]{:S(2)}, u32[]{:S(2)}) collective-permute-start(bf16[256,16,32]{0,2,1:T(8,128)(2,1)S(1)} %bitcast.93), channel_id=1, source_target_pairs={{0,3},{1,0},{2,1},{3,2},{4,7},{5,4},{6,5},{7,6},{8,11},{9,8},{10,9... | collective-permute-start | bytes 786440 | tf_op jit(solution)/shard_map/ppermute | solution.py:27
  166.4 8.2 %collective-permute-start.11 = (bf16[256,16,32]{0,2,1:T(8,128)(2,1)S(1)}, bf16[256,16,32]{0,2,1:T(8,128)(2,1)S(1)}, u32[]{:S(2)}, u32[]{:S(2)}) collective-permute-start(bf16[256,16,32]{0,2,1:T(8,128)(2,1)S(1)} %fusion), channel_id=1, source_target_pairs={{0,1},{1,2},{2,3},{3,0},{4,5},{5,6},{6,7},{7,4},{8,9},{9,10},{10,1... | collective-permute-start | bytes 786440 | tf_op jit(solution)/shard_map/ppermute | solution.py:27
  168.1 13.9 %collective-permute-start.10 = (bf16[256,16,32]{0,2,1:T(8,128)(2,1)S(1)}, bf16[256,16,32]{0,2,1:T(8,128)(2,1)S(1)}, u32[]{:S(2)}, u32[]{:S(2)}) collective-permute-start(bf16[256,16,32]{0,2,1:T(8,128)(2,1)S(1)} %fusion), channel_id=1, source_target_pairs={{0,2},{1,3},{2,0},{3,1},{4,6},{5,7},{6,4},{7,5},{8,10},{9,11},{10,... | collective-permute-start | bytes 786440 | tf_op jit(solution)/shard_map/ppermute | solution.py:27
  170.5 11.5 %collective-permute-start.9 = (bf16[256,16,32]{0,2,1:T(8,128)(2,1)S(1)}, bf16[256,16,32]{0,2,1:T(8,128)(2,1)S(1)}, u32[]{:S(2)}, u32[]{:S(2)}) collective-permute-start(bf16[256,16,32]{0,2,1:T(8,128)(2,1)S(1)} %fusion), channel_id=1, source_target_pairs={{0,3},{1,0},{2,1},{3,2},{4,7},{5,4},{6,5},{7,6},{8,11},{9,8},{10,9... | collective-permute-start | bytes 786440 | tf_op jit(solution)/shard_map/ppermute | solution.py:27

commit v4 on v3

--- a/solution.py
+++ b/solution.py
@@ -8,11 +8,7 @@
     marks = (
         first_row + jnp.arange(row_total, dtype=jnp.int32)[:, None] == targets[None, :]
     ).astype(jnp.float32)
-    flat_rows = values.reshape(values.shape[0], -1)
-    summed = jnp.dot(
-        marks, flat_rows, precision=lax.Precision.HIGHEST, preferred_element_type=jnp.float32
-    )
-    return summed.reshape((row_total,) + values.shape[1:])
+    return jnp.tensordot(marks, values, axes=1, precision=lax.Precision.HIGHEST)
 
 
 def tile_product(tile_set, columns, targets, segment_total):

time: 200 us -> 202 us (1.010)
  other arithmetic: 5.94 us -> 9.44 us
  waiting for transfers between devices: 61.7 us -> 59.6 us
    unnamed x0 -> x2, matrix products: none -> 2.32 us
    ppermute x12, waiting for transfers between devices: 32.8 us -> 30.8 us  [harm_gather(): lax.ppermute(values, 'harm', [(i, (i + s) % count) for i in range(count)])]
    dot_general x3 -> x2, local copies, waits for them, and re-layouts: 8.14 us -> 6.12 us  [tile_product(): jnp.einsum('tok,trk->tro', tile_set, columns, preferred_element_type=jnp....]
    dot_general x4 -> x2, matrix products: 4.94 us -> 6.01 us  [collect(): return jnp.tensordot(marks, values, axes=1, precision=lax.Precision.HIGHEST)]
  transfers between devices with their start and end apart: 13 -> 13, of which waited for: 9 -> 9; matrix products, arithmetic and copies ran while one was open for 2% -> 3% of each run, Pallas kernels for 0% -> 0%
where the time goes in v4:
time: 202 us; the launch traced here: 201 us
  waiting for transfers between devices  59.6 us (30%)
  local copies, waits for them, and re-layouts  44 us (22%)
  starting transfers between devices  32.1 us (16%)
  matrix products  29.4 us (15%)
  blocking collectives  25.2 us (12%)
  other arithmetic  9.44 us (5%)
    ppermute x12, waiting for transfers between devices, harm_gather(): lax.ppermute(values, 'harm', [(i, (i + s) % count) for i in range(count)])  30.8 us
    all_to_all x1, waiting for transfers between devices, on_device(): lax.all_to_all(packet, 'sub', split_axis=0, concat_axis=0, tiled=True)  28.8 us
    all_to_all x1, blocking collectives, on_device(): lax.all_to_all(replies, 'sub', split_axis=0, concat_axis=0, tiled=True)  25.2 us
    ppermute x12, starting transfers between devices, harm_gather(): lax.ppermute(values, 'harm', [(i, (i + s) % count) for i in range(count)])  19.1 us
    dot_general x3, matrix products, tile_product(): jnp.einsum('tok,trk->tro', tile_set, columns, preferred_element_type=jnp....  16.3 us
    all_to_all x1, starting transfers between devices, on_device(): lax.all_to_all(packet, 'sub', split_axis=0, concat_axis=0, tiled=True)  13 us
    unnamed x19, local copies, waits for them, and re-layouts  8.97 us
    dot_general x2, local copies, waits for them, and re-layouts, tile_product(): jnp.einsum('tok,trk->tro', tile_set, columns, preferred_element_type=jnp....  6.12 us
  transfers between devices with their start and end apart: 13, of which 9 were waited for; matrix products, arithmetic and copies ran while one was open for 3% of the time, Pallas kernels for 0%

profile of v4, /device:TPU:1, one launch (start us, length us, event | category | flops | bytes accessed | tf_op | source)
XLA Modules:
  0.0 200.7 jit_solution(14621546380984501085)
XLA Ops:
  1.5 2.2 %copy.41 = bf16[16,128,256]{1,0,2:T(8,128)(2,1)S(1)} copy(f32[16,128,256]{2,1,0:T(8,128)} %param.13) | data formatting | bytes 3145728 | tf_op args[0]
  3.7 2.7 %gather_fusion = bf16[512,16,128]{2,1,0:T(8,128)(2,1)} fusion(bf16[256,16,128]{2,1,0:T(8,128)(2,1)S(1)} %bitcast.67, s32[1024]{0:T(1024)S(1)} %pad_clamp_fusion.2), kind=kCustom, calls=%fused_computation | custom fusion | bytes 4196352 | tf_op jit(solution)/shard_map/gather | solution.py:59
  6.4 7.1 %fusion.24 = f32[512,16,32]{2,1,0:T(8,128)} fusion(bf16[512,16,128]{2,1,0:T(8,128)(2,1)} %gather_fusion, bf16[512,32,128]{2,1,0:T(8,128)(2,1)} %param.15), kind=kOutput, calls=%fused_computation.73 | convolution fusion | flops 67108864 | bytes 7340032 | tf_op jit(solution)/shard_map/tok,trk->tro/dot_general | solution.py:15
  13.5 3.6 %copy.42 = f32[512,16,32]{0,2,1:T(8,128)} copy(f32[512,16,32]{2,1,0:T(8,128)} %fusion.24) | data formatting | bytes 2097152 | tf_op jit(solution)/shard_map/tok,trk->tro/dot_general | solution.py:15
  19.1 2.2 %collective-permute-start.2 = (bf16[256,16,32]{0,2,1:T(8,128)(2,1)S(1)}, bf16[256,16,32]{0,2,1:T(8,128)(2,1)S(1)}, u32[]{:S(2)}, u32[]{:S(2)}) collective-permute-start(bf16[256,16,32]{0,2,1:T(8,128)(2,1)S(1)} %convert_element_type.47), channel_id=1, source_target_pairs={{0,1},{1,2},{2,3},{3,0},{4,5},{5,6},{6,7},{7,4},{8,9},{9,10},{10,1... | collective-permute-start | bytes 786440 | tf_op jit(solution)/shard_map/ppermute | solution.py:23
  21.3 2.6 %collective-permute-start.1 = (bf16[256,16,32]{0,2,1:T(8,128)(2,1)S(1)}, bf16[256,16,32]{0,2,1:T(8,128)(2,1)S(1)}, u32[]{:S(2)}, u32[]{:S(2)}) collective-permute-start(bf16[256,16,32]{0,2,1:T(8,128)(2,1)S(1)} %convert_element_type.47), channel_id=1, source_target_pairs={{0,2},{1,3},{2,0},{3,1},{4,6},{5,7},{6,4},{7,5},{8,10},{9,11},{10,... | collective-permute-start | bytes 786440 | tf_op jit(solution)/shard_map/ppermute | solution.py:23
  29.5 5.8 %collective-permute-done.1 = bf16[256,16,32]{0,2,1:T(8,128)(2,1)S(1)} collective-permute-done((bf16[256,16,32]{0,2,1:T(8,128)(2,1)S(1)}, bf16[256,16,32]{0,2,1:T(8,128)(2,1)S(1)}, u32[]{:S(2)}, u32[]{:S(2)}) %collective-permute-start.1) | collective-permute-done | bytes 262176 | tf_op jit(solution)/shard_map/ppermute | solution.py:23
  38.2 2.1 %gather_fusion.1 = bf16[256,16,128]{2,1,0:T(8,128)(2,1)S(1)} fusion(bf16[256,16,128]{2,1,0:T(8,128)(2,1)} %copy.43, s32[1024]{0:T(1024)S(1)} %pad_clamp_fusion.1), kind=kCustom, calls=%fused_computation.1 | custom fusion | bytes 2098176 | tf_op jit(solution)/shard_map/gather | solution.py:64
  40.3 2.6 %fusion.25 = f32[256,16,32]{2,1,0:T(8,128)} fusion(bf16[256,16,128]{2,1,0:T(8,128)(2,1)S(1)} %gather_fusion.1, bf16[256,32,128]{2,1,0:T(8,128)(2,1)S(1)} %copy-done), kind=kOutput, calls=%fused_computation.74 | convolution fusion | flops 33554432 | bytes 3670016 | tf_op jit(solution)/shard_map/tok,trk->tro/dot_general | solution.py:63
  42.8 2.5 %copy.44 = f32[256,16,32]{0,2,1:T(8,128)S(1)} copy(f32[256,16,32]{2,1,0:T(8,128)} %fusion.25) | data formatting | bytes 1048576 | tf_op jit(solution)/shard_map/tok,trk->tro/dot_general | solution.py:63
  50.2 13.0 %all-to-all-start = ((f32[64,1,4224]{2,1,0:T(1,128)}), f32[64,1,4224]{2,1,0:T(1,128)S(1)}, u32[]{:S(2)}, u32[]{:S(2)}) async-start(f32[64,1,4224]{2,1,0:T(1,128)} %all_to_all.11), calls=%async_computation | async-start | bytes 2162688 | tf_op jit(solution)/shard_map/all_to_all | solution.py:88
  63.2 28.8 %all-to-all-done = f32[64,1,4224]{2,1,0:T(1,128)S(1)} async-done(((f32[64,1,4224]{2,1,0:T(1,128)}), f32[64,1,4224]{2,1,0:T(1,128)S(1)}, u32[]{:S(2)}, u32[]{:S(2)}) %all-to-all-start) | async-done | bytes 1081376 | tf_op jit(solution)/shard_map/all_to_all | solution.py:88
  97.6 2.1 %collective-permute-start.4 = (bf16[32,16,32]{2,0,1:T(8,128)(2,1)S(1)}, bf16[32,16,32]{2,0,1:T(8,128)(2,1)S(1)}, u32[]{:S(2)}, u32[]{:S(2)}) collective-permute-start(bf16[32,16,32]{2,0,1:T(8,128)(2,1)S(1)} %fusion.2), channel_id=1, source_target_pairs={{0,2},{1,3},{2,0},{3,1},{4,6},{5,7},{6,4},{7,5},{8,10},{9,11},{10,... | collective-permute-start | bytes 98312 | tf_op jit(solution)/shard_map/ppermute | solution.py:23
  101.6 3.1 %collective-permute-done.4 = bf16[32,16,32]{2,0,1:T(8,128)(2,1)S(1)} collective-permute-done((bf16[32,16,32]{2,0,1:T(8,128)(2,1)S(1)}, bf16[32,16,32]{2,0,1:T(8,128)(2,1)S(1)}, u32[]{:S(2)}, u32[]{:S(2)}) %collective-permute-start.4) | collective-permute-done | bytes 32800 | tf_op jit(solution)/shard_map/ppermute | solution.py:23
  105.2 2.8 %gather_fusion.2 = bf16[512,16,32]{2,1,0:T(8,128)(2,1)} fusion(bf16[32,16,32]{2,1,0:T(8,128)(2,1)S(1)} %get-tuple-element.38, s32[1024]{0:T(1024)S(1)} %pad_clamp_fusion), kind=kCustom, calls=%fused_computation.2 | custom fusion | bytes 1050624 | tf_op jit(solution)/shard_map/gather | solution.py:100
  108.0 3.7 %reshape.170 = bf16[64,2,2048]{2,1,0:T(2,128)(2,1)S(1)} reshape(bf16[64,8,16,32]{3,2,1,0:T(8,128)(2,1)} %bitcast.68) | data formatting | bytes 1048576
  111.7 25.2 %all_to_all.17 = bf16[64,2,2048]{2,1,0:T(2,128)(2,1)S(1)} all-to-all(bf16[64,2,2048]{2,1,0:T(2,128)(2,1)S(1)} %reshape.170), channel_id=1, replica_groups=mesh['sub'=64,'harm'=4] {'sub'}, dimensions={0} | all-to-all | bytes 1048576 | tf_op jit(solution)/shard_map/all_to_all | solution.py:101
  137.0 2.0 %reshape.171 = bf16[64,8,16,32]{3,2,1,0:T(8,128)(2,1)} reshape(bf16[64,2,2048]{2,1,0:T(2,128)(2,1)S(1)} %all_to_all.17) | data formatting | bytes 1048576
  139.0 3.4 %reshape.126 = bf16[512,512]{1,0:T(8,128)(2,1)S(1)} reshape(bf16[64,8,16,32]{3,2,1,0:T(8,128)(2,1)} %reshape.171) | data formatting | bytes 1048576 | tf_op jit(solution)/shard_map/reshape | solution.py:102
  144.4 2.1 %collective-permute-start.7 = (bf16[256,16,32]{0,2,1:T(8,128)(2,1)S(1)}, bf16[256,16,32]{0,2,1:T(8,128)(2,1)S(1)}, u32[]{:S(2)}, u32[]{:S(2)}) collective-permute-start(bf16[256,16,32]{0,2,1:T(8,128)(2,1)S(1)} %bitcast.80), channel_id=1, source_target_pairs={{0,2},{1,3},{2,0},{3,1},{4,6},{5,7},{6,4},{7,5},{8,10},{9,11},{10,... | collective-permute-start | bytes 786440 | tf_op jit(solution)/shard_map/ppermute | solution.py:23
  147.5 4.2 %collective-permute-done.8 = bf16[256,16,32]{0,2,1:T(8,128)(2,1)S(1)} collective-permute-done((bf16[256,16,32]{0,2,1:T(8,128)(2,1)S(1)}, bf16[256,16,32]{0,2,1:T(8,128)(2,1)S(1)}, u32[]{:S(2)}, u32[]{:S(2)}) %collective-permute-start.8) | collective-permute-done | bytes 262176 | tf_op jit(solution)/shard_map/ppermute | solution.py:23
  151.6 6.5 %collective-permute-done.7 = bf16[256,16,32]{0,2,1:T(8,128)(2,1)S(1)} collective-permute-done((bf16[256,16,32]{0,2,1:T(8,128)(2,1)S(1)}, bf16[256,16,32]{0,2,1:T(8,128)(2,1)S(1)}, u32[]{:S(2)}, u32[]{:S(2)}) %collective-permute-start.7) | collective-permute-done | bytes 262176 | tf_op jit(solution)/shard_map/ppermute | solution.py:23
  159.3 1.9 copy.48
  161.3 4.1 %fusion.26 = f32[256,16,32]{2,1,0:T(8,128)} fusion(bf16[256,16,128]{2,1,0:T(8,128)(2,1)S(1)} %copy.48, bf16[256,32,128]{2,1,0:T(8,128)(2,1)} %param.19), kind=kOutput, calls=%fused_computation.75 | convolution fusion | flops 33554432 | bytes 3670016 | tf_op jit(solution)/shard_map/tok,trk->tro/dot_general | solution.py:15
  165.4 2.5 %copy.49 = f32[256,16,32]{0,2,1:T(8,128)S(1)} copy(f32[256,16,32]{2,1,0:T(8,128)} %fusion.26) | data formatting | bytes 1048576 | tf_op jit(solution)/shard_map/tok,trk->tro/dot_general | solution.py:15
  171.1 2.5 %collective-permute-start.10 = (bf16[256,16,32]{0,2,1:T(8,128)(2,1)S(1)}, bf16[256,16,32]{0,2,1:T(8,128)(2,1)S(1)}, u32[]{:S(2)}, u32[]{:S(2)}) collective-permute-start(bf16[256,16,32]{0,2,1:T(8,128)(2,1)S(1)} %fusion.3), channel_id=1, source_target_pairs={{0,2},{1,3},{2,0},{3,1},{4,6},{5,7},{6,4},{7,5},{8,10},{9,11},{10,... | collective-permute-start | bytes 786440 | tf_op jit(solution)/shard_map/ppermute | solution.py:23
  174.4 3.2 %collective-permute-done.11 = bf16[256,16,32]{0,2,1:T(8,128)(2,1)S(1)} collective-permute-done((bf16[256,16,32]{0,2,1:T(8,128)(2,1)S(1)}, bf16[256,16,32]{0,2,1:T(8,128)(2,1)S(1)}, u32[]{:S(2)}, u32[]{:S(2)}) %collective-permute-start.11) | collective-permute-done | bytes 262176 | tf_op jit(solution)/shard_map/ppermute | solution.py:23
  177.7 7.4 %collective-permute-done.10 = bf16[256,16,32]{0,2,1:T(8,128)(2,1)S(1)} collective-permute-done((bf16[256,16,32]{0,2,1:T(8,128)(2,1)S(1)}, bf16[256,16,32]{0,2,1:T(8,128)(2,1)S(1)}, u32[]{:S(2)}, u32[]{:S(2)}) %collective-permute-start.10) | collective-permute-done | bytes 262176 | tf_op jit(solution)/shard_map/ppermute | solution.py:23
  186.3 1.9 copy.50
  188.2 2.8 %gather_fusion.3 = bf16[512,16,128]{2,1,0:T(8,128)(2,1)} fusion(bf16[256,16,128]{2,1,0:T(8,128)(2,1)S(1)} %copy.50, s32[1024]{0:T(1024)S(1)} %pad_clamp_fusion.2), kind=kCustom, calls=%fused_computation.3 | custom fusion | bytes 4196352 | tf_op jit(solution)/shard_map/gather | solution.py:111
  190.9 5.1 %fusion.27 = f32[512,16,32]{2,1,0:T(8,128)S(1)} fusion(bf16[512,16,128]{2,1,0:T(8,128)(2,1)} %gather_fusion.3, bf16[512,32,128]{2,1,0:T(8,128)(2,1)} %param.15), kind=kOutput, calls=%fused_computation.76 | convolution fusion | flops 67108864 | bytes 7340032 | tf_op jit(solution)/shard_map/tok,trk->tro/dot_general | solution.py:15
  196.0 4.7 %fusion = f32[16,32,256]{2,1,0:T(8,128)} fusion(f32[512,16,32]{2,1,0:T(8,128)S(1)} %fusion.27, s32[512]{0:T(512)S(1)} %copy-done.5), kind=kOutput, calls=%fused_computation.4 | convolution fusion | flops 805437440 | bytes 1574912 | tf_op jit(solution)/shard_map/dot_general | solution.py:11
  (73 shorter events, 33.4 us)
Async XLA Ops:
  0.6 39.6 %copy-start = (bf16[256,32,128]{2,1,0:T(8,128)(2,1)S(1)}, bf16[256,32,128]{2,1,0:T(8,128)(2,1)}, u32[]{:S(2)}) copy-start(bf16[256,32,128]{2,1,0:T(8,128)(2,1)} %param.18) | copy-start | bytes 6291460
  13.5 3.6 %copy-start.5 = (s32[512]{0:T(512)S(1)}, s32[512]{0:T(512)}, u32[]{:S(2)}) copy-start(s32[512]{0:T(512)} %param.16) | copy-start | bytes 6148
  17.1 8.5 %copy-start.4 = (s32[256,1]{0,1:T(1,128)S(1)}, s32[256,1]{0,1:T(1,128)}, u32[]{:S(2)}) copy-start(s32[256,1]{0,1:T(1,128)} %param.21) | copy-start | bytes 3076
  19.1 10.4 %collective-permute-start.2 = (bf16[256,16,32]{0,2,1:T(8,128)(2,1)S(1)}, bf16[256,16,32]{0,2,1:T(8,128)(2,1)S(1)}, u32[]{:S(2)}, u32[]{:S(2)}) collective-permute-start(bf16[256,16,32]{0,2,1:T(8,128)(2,1)S(1)} %convert_element_type.47), channel_id=1, source_target_pairs={{0,1},{1,2},{2,3},{3,0},{4,5},{5,6},{6,7},{7,4},{8,9},{9,10},{10,1... | collective-permute-start | bytes 786440 | tf_op jit(solution)/shard_map/ppermute | solution.py:23
  21.3 14.0 %collective-permute-start.1 = (bf16[256,16,32]{0,2,1:T(8,128)(2,1)S(1)}, bf16[256,16,32]{0,2,1:T(8,128)(2,1)S(1)}, u32[]{:S(2)}, u32[]{:S(2)}) collective-permute-start(bf16[256,16,32]{0,2,1:T(8,128)(2,1)S(1)} %convert_element_type.47), channel_id=1, source_target_pairs={{0,2},{1,3},{2,0},{3,1},{4,6},{5,7},{6,4},{7,5},{8,10},{9,11},{10,... | collective-permute-start | bytes 786440 | tf_op jit(solution)/shard_map/ppermute | solution.py:23
  23.9 11.3 %collective-permute-start = (bf16[256,16,32]{0,2,1:T(8,128)(2,1)S(1)}, bf16[256,16,32]{0,2,1:T(8,128)(2,1)}, u32[]{:S(2)}, u32[]{:S(2)}) collective-permute-start(bf16[256,16,32]{0,2,1:T(8,128)(2,1)S(1)} %convert_element_type.47), channel_id=1, source_target_pairs={{0,3},{1,0},{2,1},{3,2},{4,7},{5,4},{6,5},{7,6},{8,11},{9,8},{10,9... | collective-permute-start | bytes 786440 | tf_op jit(solution)/shard_map/ppermute | solution.py:23
  45.3 3.0 %copy-start.3 = (f32[64,8]{1,0:T(8,128)S(1)}, f32[64,8]{1,0:T(8,128)}, u32[]{:S(2)}) copy-start(f32[64,8]{1,0:T(8,128)} %reshape.122) | copy-start | bytes 6148
  50.2 41.8 %all-to-all-start = ((f32[64,1,4224]{2,1,0:T(1,128)}), f32[64,1,4224]{2,1,0:T(1,128)S(1)}, u32[]{:S(2)}, u32[]{:S(2)}) async-start(f32[64,1,4224]{2,1,0:T(1,128)} %all_to_all.11), calls=%async_computation | async-start | bytes 2162688 | tf_op jit(solution)/shard_map/all_to_all | solution.py:88
  92.4 2.7 %copy-start.2 = (f32[16,128,32]{1,2,0:T(8,128)S(1)}, f32[16,128,32]{1,2,0:T(8,128)}, u32[]{:S(2)}) copy-start(f32[16,128,32]{1,2,0:T(8,128)} %param.14) | copy-start | bytes 786436
  95.1 9.9 %copy-start.1 = (bf16[32,32,128]{2,1,0:T(8,128)(2,1)S(1)}, bf16[32,32,128]{2,1,0:T(8,128)(2,1)}, u32[]{:S(2)}) copy-start(bf16[32,32,128]{2,1,0:T(8,128)(2,1)} %param.23) | copy-start | bytes 786436
  96.5 5.1 %collective-permute-start.5 = (bf16[32,16,32]{2,0,1:T(8,128)(2,1)S(1)}, bf16[32,16,32]{2,0,1:T(8,128)(2,1)S(1)}, u32[]{:S(2)}, u32[]{:S(2)}) collective-permute-start(bf16[32,16,32]{2,0,1:T(8,128)(2,1)S(1)} %fusion.2), channel_id=1, source_target_pairs={{0,1},{1,2},{2,3},{3,0},{4,5},{5,6},{6,7},{7,4},{8,9},{9,10},{10,1... | collective-permute-start | bytes 98312 | tf_op jit(solution)/shard_map/ppermute | solution.py:23
  97.6 7.0 %collective-permute-start.4 = (bf16[32,16,32]{2,0,1:T(8,128)(2,1)S(1)}, bf16[32,16,32]{2,0,1:T(8,128)(2,1)S(1)}, u32[]{:S(2)}, u32[]{:S(2)}) collective-permute-start(bf16[32,16,32]{2,0,1:T(8,128)(2,1)S(1)} %fusion.2), channel_id=1, source_target_pairs={{0,2},{1,3},{2,0},{3,1},{4,6},{5,7},{6,4},{7,5},{8,10},{9,11},{10,... | collective-permute-start | bytes 98312 | tf_op jit(solution)/shard_map/ppermute | solution.py:23
  99.7 5.0 %collective-permute-start.3 = (bf16[32,16,32]{2,0,1:T(8,128)(2,1)S(1)}, bf16[32,16,32]{2,0,1:T(8,128)(2,1)S(1)}, u32[]{:S(2)}, u32[]{:S(2)}) collective-permute-start(bf16[32,16,32]{2,0,1:T(8,128)(2,1)S(1)} %fusion.2), channel_id=1, source_target_pairs={{0,3},{1,0},{2,1},{3,2},{4,7},{5,4},{6,5},{7,6},{8,11},{9,8},{10,9... | collective-permute-start | bytes 98312 | tf_op jit(solution)/shard_map/ppermute | solution.py:23
  142.9 8.8 %collective-permute-start.8 = (bf16[256,16,32]{0,2,1:T(8,128)(2,1)S(1)}, bf16[256,16,32]{0,2,1:T(8,128)(2,1)S(1)}, u32[]{:S(2)}, u32[]{:S(2)}) collective-permute-start(bf16[256,16,32]{0,2,1:T(8,128)(2,1)S(1)} %bitcast.79), channel_id=1, source_target_pairs={{0,1},{1,2},{2,3},{3,0},{4,5},{5,6},{6,7},{7,4},{8,9},{9,10},{10,1... | collective-permute-start | bytes 786440 | tf_op jit(solution)/shard_map/ppermute | solution.py:23
  144.4 13.7 %collective-permute-start.7 = (bf16[256,16,32]{0,2,1:T(8,128)(2,1)S(1)}, bf16[256,16,32]{0,2,1:T(8,128)(2,1)S(1)}, u32[]{:S(2)}, u32[]{:S(2)}) collective-permute-start(bf16[256,16,32]{0,2,1:T(8,128)(2,1)S(1)} %bitcast.80), channel_id=1, source_target_pairs={{0,2},{1,3},{2,0},{3,1},{4,6},{5,7},{6,4},{7,5},{8,10},{9,11},{10,... | collective-permute-start | bytes 786440 | tf_op jit(solution)/shard_map/ppermute | solution.py:23
  146.5 11.6 %collective-permute-start.6 = (bf16[256,16,32]{0,2,1:T(8,128)(2,1)S(1)}, bf16[256,16,32]{0,2,1:T(8,128)(2,1)S(1)}, u32[]{:S(2)}, u32[]{:S(2)}) collective-permute-start(bf16[256,16,32]{0,2,1:T(8,128)(2,1)S(1)} %bitcast.81), channel_id=1, source_target_pairs={{0,3},{1,0},{2,1},{3,2},{4,7},{5,4},{6,5},{7,6},{8,11},{9,8},{10,9... | collective-permute-start | bytes 786440 | tf_op jit(solution)/shard_map/ppermute | solution.py:23
  165.4 2.5 %copy-start.6 = (s32[256]{0:T(256)S(1)}, s32[256]{0:T(256)}, u32[]{:S(2)}) copy-start(s32[256]{0:T(256)} %param.20) | copy-start | bytes 3076
  169.5 8.2 %collective-permute-start.11 = (bf16[256,16,32]{0,2,1:T(8,128)(2,1)S(1)}, bf16[256,16,32]{0,2,1:T(8,128)(2,1)S(1)}, u32[]{:S(2)}, u32[]{:S(2)}) collective-permute-start(bf16[256,16,32]{0,2,1:T(8,128)(2,1)S(1)} %fusion.3), channel_id=1, source_target_pairs={{0,1},{1,2},{2,3},{3,0},{4,5},{5,6},{6,7},{7,4},{8,9},{9,10},{10,1... | collective-permute-start | bytes 786440 | tf_op jit(solution)/shard_map/ppermute | solution.py:23
  171.1 14.0 %collective-permute-start.10 = (bf16[256,16,32]{0,2,1:T(8,128)(2,1)S(1)}, bf16[256,16,32]{0,2,1:T(8,128)(2,1)S(1)}, u32[]{:S(2)}, u32[]{:S(2)}) collective-permute-start(bf16[256,16,32]{0,2,1:T(8,128)(2,1)S(1)} %fusion.3), channel_id=1, source_target_pairs={{0,2},{1,3},{2,0},{3,1},{4,6},{5,7},{6,4},{7,5},{8,10},{9,11},{10,... | collective-permute-start | bytes 786440 | tf_op jit(solution)/shard_map/ppermute | solution.py:23
  173.6 11.5 %collective-permute-start.9 = (bf16[256,16,32]{0,2,1:T(8,128)(2,1)S(1)}, bf16[256,16,32]{0,2,1:T(8,128)(2,1)S(1)}, u32[]{:S(2)}, u32[]{:S(2)}) collective-permute-start(bf16[256,16,32]{0,2,1:T(8,128)(2,1)S(1)} %fusion.3), channel_id=1, source_target_pairs={{0,3},{1,0},{2,1},{3,2},{4,7},{5,4},{6,5},{7,6},{8,11},{9,8},{10,9... | collective-permute-start | bytes 786440 | tf_op jit(solution)/shard_map/ppermute | solution.py:23

commit v5 on v3

--- a/solution.py
+++ b/solution.py
@@ -18,6 +18,14 @@
 def tile_product(tile_set, columns, targets, segment_total):
     product = jnp.einsum("tok,trk->tro", tile_set, columns, preferred_element_type=jnp.float32)
     return collect(product, targets, segment_total)
+
+
+def pick_rows(table, rows):
+    marks = (rows[:, None] == jnp.arange(table.shape[0], dtype=jnp.int32)[None, :]).astype(
+        table.dtype
+    )
+    picked = jnp.einsum("tn,nrk->trk", marks, table, preferred_element_type=jnp.float32)
+    return picked.astype(table.dtype)
 
 
 def harm_gather(values, axis):
@@ -60,12 +68,12 @@
     own_border = lax.dynamic_slice_in_dim(border_nodes, harm_offset, harm_block, 2)
     own_side = lax.dynamic_slice_in_dim(side_nodes, harm_offset, harm_block, 2)
     side_low = side_nodes.astype(jnp.bfloat16)
-    first_pass = tile_product(precond_tiles, side_low[tile_in], tile_out, node_count).astype(
+    first_pass = tile_product(precond_tiles, pick_rows(side_low, tile_in), tile_out, node_count).astype(
         jnp.bfloat16
     )
     first_full = harm_gather(first_pass, 2)
     partials = jnp.einsum(
-        "tok,trk->tro", couple_tiles, first_full[couple_node], preferred_element_type=jnp.float32
+        "tok,trk->tro", couple_tiles, pick_rows(first_full, couple_node), preferred_element_type=jnp.float32
     )
     owner_list = border_owner[:, 0]
     value_shape = partials.shape[1:]
@@ -112,7 +120,7 @@
     correction = tile_product(return_tiles, touch_full, couple_node, node_count)
     update_low = (own_side - correction).astype(jnp.bfloat16)
     update_full = harm_gather(update_low, 2)
-    second_pass = tile_product(precond_tiles, update_full[tile_in], tile_out, node_count)
+    second_pass = tile_product(precond_tiles, pick_rows(update_full, tile_in), tile_out, node_count)
     return (jnp.transpose(second_pass, (1, 2, 0)), jnp.transpose(solved, (1, 2, 0)))
 
 

time: 200 us -> 184 us (0.920)
  local copies, waits for them, and re-layouts: 45.4 us -> 33.8 us
    gather x3 -> x0, local copies, waits for them, and re-layouts: 7.53 us -> none  [the longest x1 2.73 us: on_device(): side_low[tile_in]]
    dot_general x3, matrix products: 18.3 us -> 12.7 us  [tile_product(): jnp.einsum('tok,trk->tro', tile_set, columns, preferred_element_type=jnp....]
    dot_general x1 -> x4, matrix products: 2.55 us -> 6.33 us  [the longest x3 3.76 us: pick_rows(): jnp.einsum('tn,nrk->trk', marks, table, preferred_element_type=jnp.float32)]
    concatenate x3 -> x1, local copies, waits for them, and re-layouts: 5.64 us -> 1.92 us  [harm_gather(): return jnp.concatenate(blocks, axis)]
    unnamed x19 -> x24, local copies, waits for them, and re-layouts: 8.97 us -> 8.6 us
where the time goes in v5:
time: 184 us
  waiting for transfers between devices  61.6 us (33%)
  local copies, waits for them, and re-layouts  33.8 us (18%)
  starting transfers between devices  32 us (17%)
  matrix products  26.2 us (14%)
  blocking collectives  25.2 us (14%)
  other arithmetic  3.98 us (2%)
    ppermute x12, waiting for transfers between devices, harm_gather(): lax.ppermute(values, 'harm', [(i, (i + s) % count) for i in range(count)])  32.8 us
    all_to_all x1, waiting for transfers between devices, on_device(): lax.all_to_all(packet, 'sub', split_axis=0, concat_axis=0, tiled=True)  28.8 us
    all_to_all x1, blocking collectives, on_device(): lax.all_to_all(replies, 'sub', split_axis=0, concat_axis=0, tiled=True)  25.2 us
    ppermute x12, starting transfers between devices, harm_gather(): lax.ppermute(values, 'harm', [(i, (i + s) % count) for i in range(count)])  19 us
    all_to_all x1, starting transfers between devices, on_device(): lax.all_to_all(packet, 'sub', split_axis=0, concat_axis=0, tiled=True)  13 us
    dot_general x3, matrix products, tile_product(): jnp.einsum('tok,trk->tro', tile_set, columns, preferred_element_type=jnp....  12.7 us
    unnamed x24, local copies, waits for them, and re-layouts  8.6 us
    dot_general x3, local copies, waits for them, and re-layouts, tile_product(): jnp.einsum('tok,trk->tro', tile_set, columns, preferred_element_type=jnp....  8.13 us
  transfers between devices with their start and end apart: 13, of which 9 were waited for; matrix products, arithmetic and copies ran while one was open for 2% of the time, Pallas kernels for 0%

profile of v5, /device:TPU:1, one launch (start us, length us, event | category | flops | bytes accessed | tf_op | source)
XLA Modules:
  0.0 183.8 jit_solution(9864400990670682613)
XLA Ops:
  0.7 2.5 %convolution_convert_fusion.1 = bf16[512,16,128]{2,0,1:T(8,128)(2,1)S(1)} fusion(f32[16,128,256]{2,1,0:T(8,128)} %param.13, s32[512]{0:T(512)} %param.17), kind=kOutput, calls=%fused_computation.6 | convolution fusion | flops 538574848 | bytes 4196352 | tf_op jit(solution)/shard_map/tn,nrk->trk/dot_general | solution.py:27
  3.6 4.3 %fusion.2 = f32[512,16,32]{2,1,0:T(8,128)} fusion(bf16[512,32,128]{2,1,0:T(8,128)(2,1)S(1)} %copy-done.1, bf16[512,16,128]{2,0,1:T(8,128)(2,1)S(1)} %convolution_convert_fusion.1), kind=kOutput, calls=%fused_computation.3 | convolution fusion | flops 67108864 | bytes 7340032 | tf_op jit(solution)/shard_map/tok,trk->tro/dot_general | solution.py:19
  7.9 2.8 %copy.50 = f32[512,16,32]{0,2,1:T(8,128)S(1)} copy(f32[512,16,32]{2,1,0:T(8,128)} %fusion.2) | data formatting | bytes 2097152 | tf_op jit(solution)/shard_map/tok,trk->tro/dot_general | solution.py:19
  11.5 2.2 %collective-permute-start.2 = (bf16[256,16,32]{0,2,1:T(8,128)(2,1)S(1)}, bf16[256,16,32]{0,2,1:T(8,128)(2,1)S(1)}, u32[]{:S(2)}, u32[]{:S(2)}) collective-permute-start(bf16[256,16,32]{0,2,1:T(8,128)(2,1)S(1)} %convolution_convert_fusion.4), channel_id=1, source_target_pairs={{0,1},{1,2},{2,3},{3,0},{4,5},{5,6},{6,7},{7,4},{8,9},{9,10},{10,1... | collective-permute-start | bytes 786440 | tf_op jit(solution)/shard_map/ppermute | solution.py:35
  13.7 2.6 %collective-permute-start.1 = (bf16[256,16,32]{0,2,1:T(8,128)(2,1)S(1)}, bf16[256,16,32]{0,2,1:T(8,128)(2,1)S(1)}, u32[]{:S(2)}, u32[]{:S(2)}) collective-permute-start(bf16[256,16,32]{0,2,1:T(8,128)(2,1)S(1)} %convolution_convert_fusion.4), channel_id=1, source_target_pairs={{0,2},{1,3},{2,0},{3,1},{4,6},{5,7},{6,4},{7,5},{8,10},{9,11},{10,... | collective-permute-start | bytes 786440 | tf_op jit(solution)/shard_map/ppermute | solution.py:35
  20.0 7.7 %collective-permute-done.1 = bf16[256,16,32]{0,2,1:T(8,128)(2,1)S(1)} collective-permute-done((bf16[256,16,32]{0,2,1:T(8,128)(2,1)S(1)}, bf16[256,16,32]{0,2,1:T(8,128)(2,1)S(1)}, u32[]{:S(2)}, u32[]{:S(2)}) %collective-permute-start.1) | collective-permute-done | bytes 262176 | tf_op jit(solution)/shard_map/ppermute | solution.py:35
  28.3 2.6 %fusion.24 = f32[256,16,32]{2,1,0:T(8,128)} fusion(bf16[256,32,128]{2,1,0:T(8,128)(2,1)S(1)} %copy-done, bf16[256,16,128]{2,0,1:T(8,128)(2,1)S(1)} %convolution_convert_fusion.2), kind=kOutput, calls=%fused_computation.36 | convolution fusion | flops 33554432 | bytes 3670016 | tf_op jit(solution)/shard_map/tok,trk->tro/dot_general | solution.py:75
  30.8 2.5 %copy.53 = f32[256,16,32]{0,2,1:T(8,128)S(1)} copy(f32[256,16,32]{2,1,0:T(8,128)} %fusion.24) | data formatting | bytes 1048576 | tf_op jit(solution)/shard_map/tok,trk->tro/dot_general | solution.py:75
  33.3 1.6 fusion.28
  36.4 1.7 all_to_all.11
  38.2 13.0 %all-to-all-start = ((f32[64,1,4224]{2,1,0:T(1,128)}), f32[64,1,4224]{2,1,0:T(1,128)S(1)}, u32[]{:S(2)}, u32[]{:S(2)}) async-start(f32[64,1,4224]{2,1,0:T(1,128)} %all_to_all.11), calls=%async_computation | async-start | bytes 2162688 | tf_op jit(solution)/shard_map/all_to_all | solution.py:100
  51.2 28.8 %all-to-all-done = f32[64,1,4224]{2,1,0:T(1,128)S(1)} async-done(((f32[64,1,4224]{2,1,0:T(1,128)}), f32[64,1,4224]{2,1,0:T(1,128)S(1)}, u32[]{:S(2)}, u32[]{:S(2)}) %all-to-all-start) | async-done | bytes 1081376 | tf_op jit(solution)/shard_map/all_to_all | solution.py:100
  81.5 1.6 copy.54
  85.5 2.1 %collective-permute-start.4 = (bf16[32,16,32]{2,0,1:T(8,128)(2,1)S(1)}, bf16[32,16,32]{2,0,1:T(8,128)(2,1)S(1)}, u32[]{:S(2)}, u32[]{:S(2)}) collective-permute-start(bf16[32,16,32]{2,0,1:T(8,128)(2,1)S(1)} %fusion.5), channel_id=1, source_target_pairs={{0,2},{1,3},{2,0},{3,1},{4,6},{5,7},{6,4},{7,5},{8,10},{9,11},{10,... | collective-permute-start | bytes 98312 | tf_op jit(solution)/shard_map/ppermute | solution.py:35
  89.5 2.9 %collective-permute-done.4 = bf16[32,16,32]{2,0,1:T(8,128)(2,1)S(1)} collective-permute-done((bf16[32,16,32]{2,0,1:T(8,128)(2,1)S(1)}, bf16[32,16,32]{2,0,1:T(8,128)(2,1)S(1)}, u32[]{:S(2)}, u32[]{:S(2)}) %collective-permute-start.4) | collective-permute-done | bytes 32800 | tf_op jit(solution)/shard_map/ppermute | solution.py:35
  93.2 2.8 %gather_fusion = bf16[512,16,32]{2,1,0:T(8,128)(2,1)} fusion(bf16[32,16,32]{2,1,0:T(8,128)(2,1)S(1)} %get-tuple-element.38, s32[1024]{0:T(1024)S(1)} %pad_clamp_fusion), kind=kCustom, calls=%fused_computation | custom fusion | bytes 1050624 | tf_op jit(solution)/shard_map/gather | solution.py:112
  96.0 3.7 %reshape.162 = bf16[64,2,2048]{2,1,0:T(2,128)(2,1)S(1)} reshape(bf16[64,8,16,32]{3,2,1,0:T(8,128)(2,1)} %bitcast.88) | data formatting | bytes 1048576
  99.7 25.2 %all_to_all.17 = bf16[64,2,2048]{2,1,0:T(2,128)(2,1)S(1)} all-to-all(bf16[64,2,2048]{2,1,0:T(2,128)(2,1)S(1)} %reshape.162), channel_id=1, replica_groups=mesh['sub'=64,'harm'=4] {'sub'}, dimensions={0} | all-to-all | bytes 1048576 | tf_op jit(solution)/shard_map/all_to_all | solution.py:113
  124.9 2.0 %reshape.163 = bf16[64,8,16,32]{3,2,1,0:T(8,128)(2,1)} reshape(bf16[64,2,2048]{2,1,0:T(2,128)(2,1)S(1)} %all_to_all.17) | data formatting | bytes 1048576
  126.9 3.4 %reshape.144 = bf16[512,512]{1,0:T(8,128)(2,1)S(1)} reshape(bf16[64,8,16,32]{3,2,1,0:T(8,128)(2,1)} %reshape.163) | data formatting | bytes 1048576 | tf_op jit(solution)/shard_map/reshape | solution.py:114
  132.4 2.1 %collective-permute-start.7 = (bf16[256,16,32]{0,2,1:T(8,128)(2,1)S(1)}, bf16[256,16,32]{0,2,1:T(8,128)(2,1)S(1)}, u32[]{:S(2)}, u32[]{:S(2)}) collective-permute-start(bf16[256,16,32]{0,2,1:T(8,128)(2,1)S(1)} %bitcast.95), channel_id=1, source_target_pairs={{0,2},{1,3},{2,0},{3,1},{4,6},{5,7},{6,4},{7,5},{8,10},{9,11},{10,... | collective-permute-start | bytes 786440 | tf_op jit(solution)/shard_map/ppermute | solution.py:35
  135.3 4.3 %collective-permute-done.8 = bf16[256,16,32]{0,2,1:T(8,128)(2,1)S(1)} collective-permute-done((bf16[256,16,32]{0,2,1:T(8,128)(2,1)S(1)}, bf16[256,16,32]{0,2,1:T(8,128)(2,1)S(1)}, u32[]{:S(2)}, u32[]{:S(2)}) %collective-permute-start.8) | collective-permute-done | bytes 262176 | tf_op jit(solution)/shard_map/ppermute | solution.py:35
  139.6 6.5 %collective-permute-done.7 = bf16[256,16,32]{0,2,1:T(8,128)(2,1)S(1)} collective-permute-done((bf16[256,16,32]{0,2,1:T(8,128)(2,1)S(1)}, bf16[256,16,32]{0,2,1:T(8,128)(2,1)S(1)}, u32[]{:S(2)}, u32[]{:S(2)}) %collective-permute-start.7) | collective-permute-done | bytes 262176 | tf_op jit(solution)/shard_map/ppermute | solution.py:35
  147.3 1.9 %copy.57 = bf16[256,16,128]{2,1,0:T(8,128)(2,1)S(1)} copy(bf16[256,16,128]{0,2,1:T(8,128)(2,1)} %pad_maximum_fusion) | data formatting | bytes 2097152 | tf_op jit(solution)/shard_map/concatenate | solution.py:45
  149.2 4.1 %fusion.59 = f32[256,16,32]{2,1,0:T(8,128)} fusion(bf16[256,16,128]{2,1,0:T(8,128)(2,1)S(1)} %copy.57, bf16[256,32,128]{2,1,0:T(8,128)(2,1)} %param.19), kind=kOutput, calls=%fused_computation.99 | convolution fusion | flops 33554432 | bytes 3670016 | tf_op jit(solution)/shard_map/tok,trk->tro/dot_general | solution.py:19
  153.3 2.5 %copy.58 = f32[256,16,32]{0,2,1:T(8,128)S(1)} copy(f32[256,16,32]{2,1,0:T(8,128)} %fusion.59) | data formatting | bytes 1048576 | tf_op jit(solution)/shard_map/tok,trk->tro/dot_general | solution.py:19
  157.3 1.7 collective-permute-start.11
  159.0 2.4 %collective-permute-start.10 = (bf16[256,16,32]{0,2,1:T(8,128)(2,1)S(1)}, bf16[256,16,32]{0,2,1:T(8,128)(2,1)S(1)}, u32[]{:S(2)}, u32[]{:S(2)}) collective-permute-start(bf16[256,16,32]{0,2,1:T(8,128)(2,1)S(1)} %fusion.4), channel_id=1, source_target_pairs={{0,2},{1,3},{2,0},{3,1},{4,6},{5,7},{6,4},{7,5},{8,10},{9,11},{10,... | collective-permute-start | bytes 786440 | tf_op jit(solution)/shard_map/ppermute | solution.py:35
  162.4 3.1 %collective-permute-done.11 = bf16[256,16,32]{0,2,1:T(8,128)(2,1)S(1)} collective-permute-done((bf16[256,16,32]{0,2,1:T(8,128)(2,1)S(1)}, bf16[256,16,32]{0,2,1:T(8,128)(2,1)S(1)}, u32[]{:S(2)}, u32[]{:S(2)}) %collective-permute-start.11) | collective-permute-done | bytes 262176 | tf_op jit(solution)/shard_map/ppermute | solution.py:35
  165.5 7.4 %collective-permute-done.10 = bf16[256,16,32]{0,2,1:T(8,128)(2,1)S(1)} collective-permute-done((bf16[256,16,32]{0,2,1:T(8,128)(2,1)S(1)}, bf16[256,16,32]{0,2,1:T(8,128)(2,1)S(1)}, u32[]{:S(2)}, u32[]{:S(2)}) %collective-permute-start.10) | collective-permute-done | bytes 262176 | tf_op jit(solution)/shard_map/ppermute | solution.py:35
  175.2 4.3 %fusion = f32[512,16,32]{2,1,0:T(8,128)} fusion(bf16[512,32,128]{2,1,0:T(8,128)(2,1)S(1)} %copy-done.2, bf16[512,16,128]{2,0,1:T(8,128)(2,1)S(1)} %convolution_convert_fusion), kind=kOutput, calls=%fused_computation.1 | convolution fusion | flops 67108864 | bytes 7340032 | tf_op jit(solution)/shard_map/tok,trk->tro/dot_general | solution.py:19
  179.5 2.8 %copy.61 = f32[512,16,32]{0,2,1:T(8,128)S(1)} copy(f32[512,16,32]{2,1,0:T(8,128)} %fusion) | data formatting | bytes 2097152 | tf_op jit(solution)/shard_map/tok,trk->tro/dot_general | solution.py:19
  (69 shorter events, 23.6 us)
Async XLA Ops:
  0.6 27.6 %copy-start = (bf16[256,32,128]{2,1,0:T(8,128)(2,1)S(1)}, bf16[256,32,128]{2,1,0:T(8,128)(2,1)}, u32[]{:S(2)}) copy-start(bf16[256,32,128]{2,1,0:T(8,128)(2,1)} %param.18) | copy-start | bytes 6291460
  0.6 3.0 %copy-start.1 = (bf16[512,32,128]{2,1,0:T(8,128)(2,1)S(1)}, bf16[512,32,128]{2,1,0:T(8,128)(2,1)}, u32[]{:S(2)}) copy-start(bf16[512,32,128]{2,1,0:T(8,128)(2,1)} %param.15) | copy-start | bytes 12582916
  7.9 2.9 %copy-start.6 = (s32[512]{0:T(512)S(1)}, s32[512]{0:T(512)}, u32[]{:S(2)}) copy-start(s32[512]{0:T(512)} %param.16) | copy-start | bytes 6148
  7.9 9.4 %copy-start.5 = (s32[256,1]{0,1:T(1,128)S(1)}, s32[256,1]{0,1:T(1,128)}, u32[]{:S(2)}) copy-start(s32[256,1]{0,1:T(1,128)} %param.21) | copy-start | bytes 3076
  7.9 10.4 %copy-start.8 = (s32[256]{0:T(256)S(1)}, s32[256]{0:T(256)}, u32[]{:S(2)}) copy-start(s32[256]{0:T(256)} %param.22) | copy-start | bytes 3076
  10.8 17.0 %copy-start.9 = (s32[256]{0:T(256)S(1)}, s32[256]{0:T(256)}, u32[]{:S(2)}) copy-start(s32[256]{0:T(256)} %param.20) | copy-start | bytes 3076
  11.5 8.5 %collective-permute-start.2 = (bf16[256,16,32]{0,2,1:T(8,128)(2,1)S(1)}, bf16[256,16,32]{0,2,1:T(8,128)(2,1)S(1)}, u32[]{:S(2)}, u32[]{:S(2)}) collective-permute-start(bf16[256,16,32]{0,2,1:T(8,128)(2,1)S(1)} %convolution_convert_fusion.4), channel_id=1, source_target_pairs={{0,1},{1,2},{2,3},{3,0},{4,5},{5,6},{6,7},{7,4},{8,9},{9,10},{10,1... | collective-permute-start | bytes 786440 | tf_op jit(solution)/shard_map/ppermute | solution.py:35
  13.7 14.0 %collective-permute-start.1 = (bf16[256,16,32]{0,2,1:T(8,128)(2,1)S(1)}, bf16[256,16,32]{0,2,1:T(8,128)(2,1)S(1)}, u32[]{:S(2)}, u32[]{:S(2)}) collective-permute-start(bf16[256,16,32]{0,2,1:T(8,128)(2,1)S(1)} %convolution_convert_fusion.4), channel_id=1, source_target_pairs={{0,2},{1,3},{2,0},{3,1},{4,6},{5,7},{6,4},{7,5},{8,10},{9,11},{10,... | collective-permute-start | bytes 786440 | tf_op jit(solution)/shard_map/ppermute | solution.py:35
  16.3 11.3 %collective-permute-start = (bf16[256,16,32]{0,2,1:T(8,128)(2,1)S(1)}, bf16[256,16,32]{0,2,1:T(8,128)(2,1)S(1)}, u32[]{:S(2)}, u32[]{:S(2)}) collective-permute-start(bf16[256,16,32]{0,2,1:T(8,128)(2,1)S(1)} %convolution_convert_fusion.4), channel_id=1, source_target_pairs={{0,3},{1,0},{2,1},{3,2},{4,7},{5,4},{6,5},{7,6},{8,11},{9,8},{10,9... | collective-permute-start | bytes 786440 | tf_op jit(solution)/shard_map/ppermute | solution.py:35
  38.2 41.8 %all-to-all-start = ((f32[64,1,4224]{2,1,0:T(1,128)}), f32[64,1,4224]{2,1,0:T(1,128)S(1)}, u32[]{:S(2)}, u32[]{:S(2)}) async-start(f32[64,1,4224]{2,1,0:T(1,128)} %all_to_all.11), calls=%async_computation | async-start | bytes 2162688 | tf_op jit(solution)/shard_map/all_to_all | solution.py:100
  80.3 2.7 %copy-start.4 = (f32[16,128,32]{1,2,0:T(8,128)S(1)}, f32[16,128,32]{1,2,0:T(8,128)}, u32[]{:S(2)}) copy-start(f32[16,128,32]{1,2,0:T(8,128)} %param.14) | copy-start | bytes 786436
  83.1 9.9 %copy-start.3 = (bf16[32,32,128]{2,1,0:T(8,128)(2,1)S(1)}, bf16[32,32,128]{2,1,0:T(8,128)(2,1)}, u32[]{:S(2)}) copy-start(bf16[32,32,128]{2,1,0:T(8,128)(2,1)} %param.23) | copy-start | bytes 786436
  84.4 5.1 %collective-permute-start.5 = (bf16[32,16,32]{2,0,1:T(8,128)(2,1)S(1)}, bf16[32,16,32]{2,0,1:T(8,128)(2,1)S(1)}, u32[]{:S(2)}, u32[]{:S(2)}) collective-permute-start(bf16[32,16,32]{2,0,1:T(8,128)(2,1)S(1)} %fusion.5), channel_id=1, source_target_pairs={{0,1},{1,2},{2,3},{3,0},{4,5},{5,6},{6,7},{7,4},{8,9},{9,10},{10,1... | collective-permute-start | bytes 98312 | tf_op jit(solution)/shard_map/ppermute | solution.py:35
  85.5 7.0 %collective-permute-start.4 = (bf16[32,16,32]{2,0,1:T(8,128)(2,1)S(1)}, bf16[32,16,32]{2,0,1:T(8,128)(2,1)S(1)}, u32[]{:S(2)}, u32[]{:S(2)}) collective-permute-start(bf16[32,16,32]{2,0,1:T(8,128)(2,1)S(1)} %fusion.5), channel_id=1, source_target_pairs={{0,2},{1,3},{2,0},{3,1},{4,6},{5,7},{6,4},{7,5},{8,10},{9,11},{10,... | collective-permute-start | bytes 98312 | tf_op jit(solution)/shard_map/ppermute | solution.py:35
  87.6 5.1 %collective-permute-start.3 = (bf16[32,16,32]{2,0,1:T(8,128)(2,1)S(1)}, bf16[32,16,32]{2,0,1:T(8,128)(2,1)S(1)}, u32[]{:S(2)}, u32[]{:S(2)}) collective-permute-start(bf16[32,16,32]{2,0,1:T(8,128)(2,1)S(1)} %fusion.5), channel_id=1, source_target_pairs={{0,3},{1,0},{2,1},{3,2},{4,7},{5,4},{6,5},{7,6},{8,11},{9,8},{10,9... | collective-permute-start | bytes 98312 | tf_op jit(solution)/shard_map/ppermute | solution.py:35
  130.8 8.8 %collective-permute-start.8 = (bf16[256,16,32]{0,2,1:T(8,128)(2,1)S(1)}, bf16[256,16,32]{0,2,1:T(8,128)(2,1)S(1)}, u32[]{:S(2)}, u32[]{:S(2)}) collective-permute-start(bf16[256,16,32]{0,2,1:T(8,128)(2,1)S(1)} %bitcast.94), channel_id=1, source_target_pairs={{0,1},{1,2},{2,3},{3,0},{4,5},{5,6},{6,7},{7,4},{8,9},{9,10},{10,1... | collective-permute-start | bytes 786440 | tf_op jit(solution)/shard_map/ppermute | solution.py:35
  132.4 13.7 %collective-permute-start.7 = (bf16[256,16,32]{0,2,1:T(8,128)(2,1)S(1)}, bf16[256,16,32]{0,2,1:T(8,128)(2,1)S(1)}, u32[]{:S(2)}, u32[]{:S(2)}) collective-permute-start(bf16[256,16,32]{0,2,1:T(8,128)(2,1)S(1)} %bitcast.95), channel_id=1, source_target_pairs={{0,2},{1,3},{2,0},{3,1},{4,6},{5,7},{6,4},{7,5},{8,10},{9,11},{10,... | collective-permute-start | bytes 786440 | tf_op jit(solution)/shard_map/ppermute | solution.py:35
  134.5 11.6 %collective-permute-start.6 = (bf16[256,16,32]{0,2,1:T(8,128)(2,1)S(1)}, bf16[256,16,32]{0,2,1:T(8,128)(2,1)S(1)}, u32[]{:S(2)}, u32[]{:S(2)}) collective-permute-start(bf16[256,16,32]{0,2,1:T(8,128)(2,1)S(1)} %bitcast.96), channel_id=1, source_target_pairs={{0,3},{1,0},{2,1},{3,2},{4,7},{5,4},{6,5},{7,6},{8,11},{9,8},{10,9... | collective-permute-start | bytes 786440 | tf_op jit(solution)/shard_map/ppermute | solution.py:35
  155.8 17.2 %copy-start.7 = (s32[512]{0:T(512)S(1)}, s32[512]{0:T(512)}, u32[]{:S(2)}) copy-start(s32[512]{0:T(512)} %param.17) | copy-start | bytes 6148
  157.3 8.2 %collective-permute-start.11 = (bf16[256,16,32]{0,2,1:T(8,128)(2,1)S(1)}, bf16[256,16,32]{0,2,1:T(8,128)(2,1)S(1)}, u32[]{:S(2)}, u32[]{:S(2)}) collective-permute-start(bf16[256,16,32]{0,2,1:T(8,128)(2,1)S(1)} %fusion.4), channel_id=1, source_target_pairs={{0,1},{1,2},{2,3},{3,0},{4,5},{5,6},{6,7},{7,4},{8,9},{9,10},{10,1... | collective-permute-start | bytes 786440 | tf_op jit(solution)/shard_map/ppermute | solution.py:35
  159.0 13.9 %collective-permute-start.10 = (bf16[256,16,32]{0,2,1:T(8,128)(2,1)S(1)}, bf16[256,16,32]{0,2,1:T(8,128)(2,1)S(1)}, u32[]{:S(2)}, u32[]{:S(2)}) collective-permute-start(bf16[256,16,32]{0,2,1:T(8,128)(2,1)S(1)} %fusion.4), channel_id=1, source_target_pairs={{0,2},{1,3},{2,0},{3,1},{4,6},{5,7},{6,4},{7,5},{8,10},{9,11},{10,... | collective-permute-start | bytes 786440 | tf_op jit(solution)/shard_map/ppermute | solution.py:35
  161.4 11.5 %collective-permute-start.9 = (bf16[256,16,32]{0,2,1:T(8,128)(2,1)S(1)}, bf16[256,16,32]{0,2,1:T(8,128)(2,1)S(1)}, u32[]{:S(2)}, u32[]{:S(2)}) collective-permute-start(bf16[256,16,32]{0,2,1:T(8,128)(2,1)S(1)} %fusion.4), channel_id=1, source_target_pairs={{0,3},{1,0},{2,1},{3,2},{4,7},{5,4},{6,5},{7,6},{8,11},{9,8},{10,9... | collective-permute-start | bytes 786440 | tf_op jit(solution)/shard_map/ppermute | solution.py:35
  173.1 2.2 %copy-start.2 = (bf16[512,32,128]{2,1,0:T(8,128)(2,1)S(1)}, bf16[512,32,128]{2,1,0:T(8,128)(2,1)}, u32[]{:S(2)}) copy-start(bf16[512,32,128]{2,1,0:T(8,128)(2,1)} %param.15) | copy-start | bytes 12582916

commit v6 on v5

--- a/solution.py
+++ b/solution.py
@@ -109,7 +109,7 @@
         "bok,brk->bro", border_inverse, residual_full, preferred_element_type=jnp.float32
     )
     solved, solved_low = (solved, solved.astype(jnp.bfloat16))
-    replies = solved_low[arrived_rows].reshape((sub_count, capacity) + value_shape)
+    replies = pick_rows(solved_low, arrived_rows).reshape((sub_count, capacity) + value_shape)
     returned = lax.all_to_all(replies, "sub", split_axis=0, concat_axis=0, tiled=True)
     returned_flat = returned.reshape(sub_count * capacity, -1)
     touch_low = jnp.dot(

time: 184 us -> 185 us (level)
    convert_element_type x0 -> x2, local copies, waits for them, and re-layouts: none -> 3.02 us  [the longest x1 2.83 us: pick_rows(): return picked.astype(table.dtype)]
    gather x1 -> x0, local copies, waits for them, and re-layouts: 2.75 us -> none  [on_device(): solved_low[arrived_rows].reshape((sub_count, capacity) + value_shape)]
where the time goes in v6:
time: 185 us; the launch traced here: 184 us
  waiting for transfers between devices  61.6 us (33%)
  local copies, waits for them, and re-layouts  34 us (18%)
  starting transfers between devices  32 us (17%)
  matrix products  26.4 us (14%)
  blocking collectives  25.2 us (14%)
  other arithmetic  4.04 us (2%)
    ppermute x12, waiting for transfers between devices, harm_gather(): lax.ppermute(values, 'harm', [(i, (i + s) % count) for i in range(count)])  32.8 us
    all_to_all x1, waiting for transfers between devices, on_device(): lax.all_to_all(packet, 'sub', split_axis=0, concat_axis=0, tiled=True)  28.8 us
    all_to_all x1, blocking collectives, on_device(): lax.all_to_all(replies, 'sub', split_axis=0, concat_axis=0, tiled=True)  25.2 us
    ppermute x12, starting transfers between devices, harm_gather(): lax.ppermute(values, 'harm', [(i, (i + s) % count) for i in range(count)])  19 us
    all_to_all x1, starting transfers between devices, on_device(): lax.all_to_all(packet, 'sub', split_axis=0, concat_axis=0, tiled=True)  13 us
    dot_general x3, matrix products, tile_product(): jnp.einsum('tok,trk->tro', tile_set, columns, preferred_element_type=jnp....  12.7 us
    unnamed x24, local copies, waits for them, and re-layouts  8.6 us
    dot_general x3, local copies, waits for them, and re-layouts, tile_product(): jnp.einsum('tok,trk->tro', tile_set, columns, preferred_element_type=jnp....  8.13 us
  transfers between devices with their start and end apart: 13, of which 9 were waited for; matrix products, arithmetic and copies ran while one was open for 2% of the time, Pallas kernels for 0%

profile of v6, /device:TPU:1, one launch (start us, length us, event | category | flops | bytes accessed | tf_op | source)
XLA Modules:
  0.0 184.3 jit_solution(5914926640715797970)
XLA Ops:
  0.7 2.5 %convolution_convert_fusion.1 = bf16[512,16,128]{2,0,1:T(8,128)(2,1)S(1)} fusion(f32[16,128,256]{2,1,0:T(8,128)} %param.13, s32[512]{0:T(512)} %param.17), kind=kOutput, calls=%fused_computation.5 | convolution fusion | flops 538574848 | bytes 4196352 | tf_op jit(solution)/shard_map/tn,nrk->trk/dot_general | solution.py:27
  3.6 4.3 %fusion.2 = f32[512,16,32]{2,1,0:T(8,128)} fusion(bf16[512,32,128]{2,1,0:T(8,128)(2,1)S(1)} %copy-done.1, bf16[512,16,128]{2,0,1:T(8,128)(2,1)S(1)} %convolution_convert_fusion.1), kind=kOutput, calls=%fused_computation.2 | convolution fusion | flops 67108864 | bytes 7340032 | tf_op jit(solution)/shard_map/tok,trk->tro/dot_general | solution.py:19
  7.9 2.8 %copy.55 = f32[512,16,32]{0,2,1:T(8,128)S(1)} copy(f32[512,16,32]{2,1,0:T(8,128)} %fusion.2) | data formatting | bytes 2097152 | tf_op jit(solution)/shard_map/tok,trk->tro/dot_general | solution.py:19
  11.5 2.2 %collective-permute-start.2 = (bf16[256,16,32]{0,2,1:T(8,128)(2,1)S(1)}, bf16[256,16,32]{0,2,1:T(8,128)(2,1)S(1)}, u32[]{:S(2)}, u32[]{:S(2)}) collective-permute-start(bf16[256,16,32]{0,2,1:T(8,128)(2,1)S(1)} %convolution_convert_fusion.4), channel_id=1, source_target_pairs={{0,1},{1,2},{2,3},{3,0},{4,5},{5,6},{6,7},{7,4},{8,9},{9,10},{10,1... | collective-permute-start | bytes 786440 | tf_op jit(solution)/shard_map/ppermute | solution.py:35
  13.7 2.6 %collective-permute-start.1 = (bf16[256,16,32]{0,2,1:T(8,128)(2,1)S(1)}, bf16[256,16,32]{0,2,1:T(8,128)(2,1)S(1)}, u32[]{:S(2)}, u32[]{:S(2)}) collective-permute-start(bf16[256,16,32]{0,2,1:T(8,128)(2,1)S(1)} %convolution_convert_fusion.4), channel_id=1, source_target_pairs={{0,2},{1,3},{2,0},{3,1},{4,6},{5,7},{6,4},{7,5},{8,10},{9,11},{10,... | collective-permute-start | bytes 786440 | tf_op jit(solution)/shard_map/ppermute | solution.py:35
  20.0 7.7 %collective-permute-done.1 = bf16[256,16,32]{0,2,1:T(8,128)(2,1)S(1)} collective-permute-done((bf16[256,16,32]{0,2,1:T(8,128)(2,1)S(1)}, bf16[256,16,32]{0,2,1:T(8,128)(2,1)S(1)}, u32[]{:S(2)}, u32[]{:S(2)}) %collective-permute-start.1) | collective-permute-done | bytes 262176 | tf_op jit(solution)/shard_map/ppermute | solution.py:35
  28.3 2.6 %fusion.24 = f32[256,16,32]{2,1,0:T(8,128)} fusion(bf16[256,32,128]{2,1,0:T(8,128)(2,1)S(1)} %copy-done, bf16[256,16,128]{2,0,1:T(8,128)(2,1)S(1)} %convolution_convert_fusion.2), kind=kOutput, calls=%fused_computation.35 | convolution fusion | flops 33554432 | bytes 3670016 | tf_op jit(solution)/shard_map/tok,trk->tro/dot_general | solution.py:75
  30.8 2.5 %copy.58 = f32[256,16,32]{0,2,1:T(8,128)S(1)} copy(f32[256,16,32]{2,1,0:T(8,128)} %fusion.24) | data formatting | bytes 1048576 | tf_op jit(solution)/shard_map/tok,trk->tro/dot_general | solution.py:75
  33.3 1.6 fusion.28
  36.4 1.7 all_to_all.11
  38.2 13.0 %all-to-all-start = ((f32[64,1,4224]{2,1,0:T(1,128)}), f32[64,1,4224]{2,1,0:T(1,128)S(1)}, u32[]{:S(2)}, u32[]{:S(2)}) async-start(f32[64,1,4224]{2,1,0:T(1,128)} %all_to_all.11), calls=%async_computation | async-start | bytes 2162688 | tf_op jit(solution)/shard_map/all_to_all | solution.py:100
  51.2 28.8 %all-to-all-done = f32[64,1,4224]{2,1,0:T(1,128)S(1)} async-done(((f32[64,1,4224]{2,1,0:T(1,128)}), f32[64,1,4224]{2,1,0:T(1,128)S(1)}, u32[]{:S(2)}, u32[]{:S(2)}) %all-to-all-start) | async-done | bytes 1081376 | tf_op jit(solution)/shard_map/all_to_all | solution.py:100
  81.4 1.6 copy.59
  85.4 2.1 %collective-permute-start.4 = (bf16[32,16,32]{2,0,1:T(8,128)(2,1)S(1)}, bf16[32,16,32]{2,0,1:T(8,128)(2,1)S(1)}, u32[]{:S(2)}, u32[]{:S(2)}) collective-permute-start(bf16[32,16,32]{2,0,1:T(8,128)(2,1)S(1)} %fusion.5), channel_id=1, source_target_pairs={{0,2},{1,3},{2,0},{3,1},{4,6},{5,7},{6,4},{7,5},{8,10},{9,11},{10,... | collective-permute-start | bytes 98312 | tf_op jit(solution)/shard_map/ppermute | solution.py:35
  89.4 2.9 %collective-permute-done.4 = bf16[32,16,32]{2,0,1:T(8,128)(2,1)S(1)} collective-permute-done((bf16[32,16,32]{2,0,1:T(8,128)(2,1)S(1)}, bf16[32,16,32]{2,0,1:T(8,128)(2,1)S(1)}, u32[]{:S(2)}, u32[]{:S(2)}) %collective-permute-start.4) | collective-permute-done | bytes 32800 | tf_op jit(solution)/shard_map/ppermute | solution.py:35
  93.7 2.8 %copy.62 = bf16[512,16,32]{2,1,0:T(8,128)(2,1)} copy(bf16[512,16,32]{0,2,1:T(8,128)(2,1)S(1)} %convert_element_type.70) | data formatting | bytes 1048576 | tf_op jit(solution)/shard_map/convert_element_type | solution.py:28
  96.5 3.7 %reshape.125 = bf16[64,2,2048]{2,1,0:T(2,128)(2,1)S(1)} reshape(bf16[64,8,16,32]{3,2,1,0:T(8,128)(2,1)} %bitcast.90) | data formatting | bytes 1048576
  100.2 25.2 %all_to_all.17 = bf16[64,2,2048]{2,1,0:T(2,128)(2,1)S(1)} all-to-all(bf16[64,2,2048]{2,1,0:T(2,128)(2,1)S(1)} %reshape.125), channel_id=1, replica_groups=mesh['sub'=64,'harm'=4] {'sub'}, dimensions={0} | all-to-all | bytes 1048576 | tf_op jit(solution)/shard_map/all_to_all | solution.py:113
  125.5 2.0 %reshape.126 = bf16[64,8,16,32]{3,2,1,0:T(8,128)(2,1)} reshape(bf16[64,2,2048]{2,1,0:T(2,128)(2,1)S(1)} %all_to_all.17) | data formatting | bytes 1048576
  127.5 3.4 %reshape.113 = bf16[512,512]{1,0:T(8,128)(2,1)S(1)} reshape(bf16[64,8,16,32]{3,2,1,0:T(8,128)(2,1)} %reshape.126) | data formatting | bytes 1048576 | tf_op jit(solution)/shard_map/reshape | solution.py:114
  132.9 2.1 %collective-permute-start.7 = (bf16[256,16,32]{0,2,1:T(8,128)(2,1)S(1)}, bf16[256,16,32]{0,2,1:T(8,128)(2,1)S(1)}, u32[]{:S(2)}, u32[]{:S(2)}) collective-permute-start(bf16[256,16,32]{0,2,1:T(8,128)(2,1)S(1)} %bitcast.98), channel_id=1, source_target_pairs={{0,2},{1,3},{2,0},{3,1},{4,6},{5,7},{6,4},{7,5},{8,10},{9,11},{10,... | collective-permute-start | bytes 786440 | tf_op jit(solution)/shard_map/ppermute | solution.py:35
  135.8 4.3 %collective-permute-done.8 = bf16[256,16,32]{0,2,1:T(8,128)(2,1)S(1)} collective-permute-done((bf16[256,16,32]{0,2,1:T(8,128)(2,1)S(1)}, bf16[256,16,32]{0,2,1:T(8,128)(2,1)S(1)}, u32[]{:S(2)}, u32[]{:S(2)}) %collective-permute-start.8) | collective-permute-done | bytes 262176 | tf_op jit(solution)/shard_map/ppermute | solution.py:35
  140.1 6.5 %collective-permute-done.7 = bf16[256,16,32]{0,2,1:T(8,128)(2,1)S(1)} collective-permute-done((bf16[256,16,32]{0,2,1:T(8,128)(2,1)S(1)}, bf16[256,16,32]{0,2,1:T(8,128)(2,1)S(1)}, u32[]{:S(2)}, u32[]{:S(2)}) %collective-permute-start.7) | collective-permute-done | bytes 262176 | tf_op jit(solution)/shard_map/ppermute | solution.py:35
  147.8 1.9 %copy.64 = bf16[256,16,128]{2,1,0:T(8,128)(2,1)S(1)} copy(bf16[256,16,128]{0,2,1:T(8,128)(2,1)} %pad_maximum_fusion) | data formatting | bytes 2097152 | tf_op jit(solution)/shard_map/concatenate | solution.py:45
  149.7 4.1 %fusion.61 = f32[256,16,32]{2,1,0:T(8,128)} fusion(bf16[256,16,128]{2,1,0:T(8,128)(2,1)S(1)} %copy.64, bf16[256,32,128]{2,1,0:T(8,128)(2,1)} %param.19), kind=kOutput, calls=%fused_computation.99 | convolution fusion | flops 33554432 | bytes 3670016 | tf_op jit(solution)/shard_map/tok,trk->tro/dot_general | solution.py:19
  153.9 2.5 %copy.65 = f32[256,16,32]{0,2,1:T(8,128)S(1)} copy(f32[256,16,32]{2,1,0:T(8,128)} %fusion.61) | data formatting | bytes 1048576 | tf_op jit(solution)/shard_map/tok,trk->tro/dot_general | solution.py:19
  157.9 1.7 collective-permute-start.11
  159.6 2.4 %collective-permute-start.10 = (bf16[256,16,32]{0,2,1:T(8,128)(2,1)S(1)}, bf16[256,16,32]{0,2,1:T(8,128)(2,1)S(1)}, u32[]{:S(2)}, u32[]{:S(2)}) collective-permute-start(bf16[256,16,32]{0,2,1:T(8,128)(2,1)S(1)} %fusion.4), channel_id=1, source_target_pairs={{0,2},{1,3},{2,0},{3,1},{4,6},{5,7},{6,4},{7,5},{8,10},{9,11},{10,... | collective-permute-start | bytes 786440 | tf_op jit(solution)/shard_map/ppermute | solution.py:35
  162.9 3.1 %collective-permute-done.11 = bf16[256,16,32]{0,2,1:T(8,128)(2,1)S(1)} collective-permute-done((bf16[256,16,32]{0,2,1:T(8,128)(2,1)S(1)}, bf16[256,16,32]{0,2,1:T(8,128)(2,1)S(1)}, u32[]{:S(2)}, u32[]{:S(2)}) %collective-permute-start.11) | collective-permute-done | bytes 262176 | tf_op jit(solution)/shard_map/ppermute | solution.py:35
  166.1 7.4 %collective-permute-done.10 = bf16[256,16,32]{0,2,1:T(8,128)(2,1)S(1)} collective-permute-done((bf16[256,16,32]{0,2,1:T(8,128)(2,1)S(1)}, bf16[256,16,32]{0,2,1:T(8,128)(2,1)S(1)}, u32[]{:S(2)}, u32[]{:S(2)}) %collective-permute-start.10) | collective-permute-done | bytes 262176 | tf_op jit(solution)/shard_map/ppermute | solution.py:35
  175.8 4.3 %fusion = f32[512,16,32]{2,1,0:T(8,128)} fusion(bf16[512,32,128]{2,1,0:T(8,128)(2,1)S(1)} %copy-done.2, bf16[512,16,128]{2,0,1:T(8,128)(2,1)S(1)} %convolution_convert_fusion), kind=kOutput, calls=%fused_computation | convolution fusion | flops 67108864 | bytes 7340032 | tf_op jit(solution)/shard_map/tok,trk->tro/dot_general | solution.py:19
  180.1 2.8 %copy.68 = f32[512,16,32]{0,2,1:T(8,128)S(1)} copy(f32[512,16,32]{2,1,0:T(8,128)} %fusion) | data formatting | bytes 2097152 | tf_op jit(solution)/shard_map/tok,trk->tro/dot_general | solution.py:19
  (69 shorter events, 24.1 us)
Async XLA Ops:
  0.6 27.6 %copy-start = (bf16[256,32,128]{2,1,0:T(8,128)(2,1)S(1)}, bf16[256,32,128]{2,1,0:T(8,128)(2,1)}, u32[]{:S(2)}) copy-start(bf16[256,32,128]{2,1,0:T(8,128)(2,1)} %param.18) | copy-start | bytes 6291460
  0.6 3.0 %copy-start.1 = (bf16[512,32,128]{2,1,0:T(8,128)(2,1)S(1)}, bf16[512,32,128]{2,1,0:T(8,128)(2,1)}, u32[]{:S(2)}) copy-start(bf16[512,32,128]{2,1,0:T(8,128)(2,1)} %param.15) | copy-start | bytes 12582916
  7.9 2.9 %copy-start.6 = (s32[512]{0:T(512)S(1)}, s32[512]{0:T(512)}, u32[]{:S(2)}) copy-start(s32[512]{0:T(512)} %param.16) | copy-start | bytes 6148
  7.9 9.4 %copy-start.5 = (s32[256,1]{0,1:T(1,128)S(1)}, s32[256,1]{0,1:T(1,128)}, u32[]{:S(2)}) copy-start(s32[256,1]{0,1:T(1,128)} %param.21) | copy-start | bytes 3076
  7.9 10.4 %copy-start.8 = (s32[256]{0:T(256)S(1)}, s32[256]{0:T(256)}, u32[]{:S(2)}) copy-start(s32[256]{0:T(256)} %param.22) | copy-start | bytes 3076
  10.8 17.0 %copy-start.9 = (s32[256]{0:T(256)S(1)}, s32[256]{0:T(256)}, u32[]{:S(2)}) copy-start(s32[256]{0:T(256)} %param.20) | copy-start | bytes 3076
  11.5 8.5 %collective-permute-start.2 = (bf16[256,16,32]{0,2,1:T(8,128)(2,1)S(1)}, bf16[256,16,32]{0,2,1:T(8,128)(2,1)S(1)}, u32[]{:S(2)}, u32[]{:S(2)}) collective-permute-start(bf16[256,16,32]{0,2,1:T(8,128)(2,1)S(1)} %convolution_convert_fusion.4), channel_id=1, source_target_pairs={{0,1},{1,2},{2,3},{3,0},{4,5},{5,6},{6,7},{7,4},{8,9},{9,10},{10,1... | collective-permute-start | bytes 786440 | tf_op jit(solution)/shard_map/ppermute | solution.py:35
  13.7 14.0 %collective-permute-start.1 = (bf16[256,16,32]{0,2,1:T(8,128)(2,1)S(1)}, bf16[256,16,32]{0,2,1:T(8,128)(2,1)S(1)}, u32[]{:S(2)}, u32[]{:S(2)}) collective-permute-start(bf16[256,16,32]{0,2,1:T(8,128)(2,1)S(1)} %convolution_convert_fusion.4), channel_id=1, source_target_pairs={{0,2},{1,3},{2,0},{3,1},{4,6},{5,7},{6,4},{7,5},{8,10},{9,11},{10,... | collective-permute-start | bytes 786440 | tf_op jit(solution)/shard_map/ppermute | solution.py:35
  16.3 11.3 %collective-permute-start = (bf16[256,16,32]{0,2,1:T(8,128)(2,1)S(1)}, bf16[256,16,32]{0,2,1:T(8,128)(2,1)S(1)}, u32[]{:S(2)}, u32[]{:S(2)}) collective-permute-start(bf16[256,16,32]{0,2,1:T(8,128)(2,1)S(1)} %convolution_convert_fusion.4), channel_id=1, source_target_pairs={{0,3},{1,0},{2,1},{3,2},{4,7},{5,4},{6,5},{7,6},{8,11},{9,8},{10,9... | collective-permute-start | bytes 786440 | tf_op jit(solution)/shard_map/ppermute | solution.py:35
  38.2 41.8 %all-to-all-start = ((f32[64,1,4224]{2,1,0:T(1,128)}), f32[64,1,4224]{2,1,0:T(1,128)S(1)}, u32[]{:S(2)}, u32[]{:S(2)}) async-start(f32[64,1,4224]{2,1,0:T(1,128)} %all_to_all.11), calls=%async_computation | async-start | bytes 2162688 | tf_op jit(solution)/shard_map/all_to_all | solution.py:100
  80.3 2.7 %copy-start.4 = (f32[16,128,32]{1,2,0:T(8,128)S(1)}, f32[16,128,32]{1,2,0:T(8,128)}, u32[]{:S(2)}) copy-start(f32[16,128,32]{1,2,0:T(8,128)} %param.14) | copy-start | bytes 786436
  83.0 9.9 %copy-start.3 = (bf16[32,32,128]{2,1,0:T(8,128)(2,1)S(1)}, bf16[32,32,128]{2,1,0:T(8,128)(2,1)}, u32[]{:S(2)}) copy-start(bf16[32,32,128]{2,1,0:T(8,128)(2,1)} %param.23) | copy-start | bytes 786436
  84.3 5.1 %collective-permute-start.5 = (bf16[32,16,32]{2,0,1:T(8,128)(2,1)S(1)}, bf16[32,16,32]{2,0,1:T(8,128)(2,1)S(1)}, u32[]{:S(2)}, u32[]{:S(2)}) collective-permute-start(bf16[32,16,32]{2,0,1:T(8,128)(2,1)S(1)} %fusion.5), channel_id=1, source_target_pairs={{0,1},{1,2},{2,3},{3,0},{4,5},{5,6},{6,7},{7,4},{8,9},{9,10},{10,1... | collective-permute-start | bytes 98312 | tf_op jit(solution)/shard_map/ppermute | solution.py:35
  85.4 7.0 %collective-permute-start.4 = (bf16[32,16,32]{2,0,1:T(8,128)(2,1)S(1)}, bf16[32,16,32]{2,0,1:T(8,128)(2,1)S(1)}, u32[]{:S(2)}, u32[]{:S(2)}) collective-permute-start(bf16[32,16,32]{2,0,1:T(8,128)(2,1)S(1)} %fusion.5), channel_id=1, source_target_pairs={{0,2},{1,3},{2,0},{3,1},{4,6},{5,7},{6,4},{7,5},{8,10},{9,11},{10,... | collective-permute-start | bytes 98312 | tf_op jit(solution)/shard_map/ppermute | solution.py:35
  87.5 5.1 %collective-permute-start.3 = (bf16[32,16,32]{2,0,1:T(8,128)(2,1)S(1)}, bf16[32,16,32]{2,0,1:T(8,128)(2,1)S(1)}, u32[]{:S(2)}, u32[]{:S(2)}) collective-permute-start(bf16[32,16,32]{2,0,1:T(8,128)(2,1)S(1)} %fusion.5), channel_id=1, source_target_pairs={{0,3},{1,0},{2,1},{3,2},{4,7},{5,4},{6,5},{7,6},{8,11},{9,8},{10,9... | collective-permute-start | bytes 98312 | tf_op jit(solution)/shard_map/ppermute | solution.py:35
  131.4 8.8 %collective-permute-start.8 = (bf16[256,16,32]{0,2,1:T(8,128)(2,1)S(1)}, bf16[256,16,32]{0,2,1:T(8,128)(2,1)S(1)}, u32[]{:S(2)}, u32[]{:S(2)}) collective-permute-start(bf16[256,16,32]{0,2,1:T(8,128)(2,1)S(1)} %bitcast.97), channel_id=1, source_target_pairs={{0,1},{1,2},{2,3},{3,0},{4,5},{5,6},{6,7},{7,4},{8,9},{9,10},{10,1... | collective-permute-start | bytes 786440 | tf_op jit(solution)/shard_map/ppermute | solution.py:35
  132.9 13.7 %collective-permute-start.7 = (bf16[256,16,32]{0,2,1:T(8,128)(2,1)S(1)}, bf16[256,16,32]{0,2,1:T(8,128)(2,1)S(1)}, u32[]{:S(2)}, u32[]{:S(2)}) collective-permute-start(bf16[256,16,32]{0,2,1:T(8,128)(2,1)S(1)} %bitcast.98), channel_id=1, source_target_pairs={{0,2},{1,3},{2,0},{3,1},{4,6},{5,7},{6,4},{7,5},{8,10},{9,11},{10,... | collective-permute-start | bytes 786440 | tf_op jit(solution)/shard_map/ppermute | solution.py:35
  135.0 11.6 %collective-permute-start.6 = (bf16[256,16,32]{0,2,1:T(8,128)(2,1)S(1)}, bf16[256,16,32]{0,2,1:T(8,128)(2,1)S(1)}, u32[]{:S(2)}, u32[]{:S(2)}) collective-permute-start(bf16[256,16,32]{0,2,1:T(8,128)(2,1)S(1)} %bitcast.99), channel_id=1, source_target_pairs={{0,3},{1,0},{2,1},{3,2},{4,7},{5,4},{6,5},{7,6},{8,11},{9,8},{10,9... | collective-permute-start | bytes 786440 | tf_op jit(solution)/shard_map/ppermute | solution.py:35
  156.4 17.2 %copy-start.7 = (s32[512]{0:T(512)S(1)}, s32[512]{0:T(512)}, u32[]{:S(2)}) copy-start(s32[512]{0:T(512)} %param.17) | copy-start | bytes 6148
  157.9 8.2 %collective-permute-start.11 = (bf16[256,16,32]{0,2,1:T(8,128)(2,1)S(1)}, bf16[256,16,32]{0,2,1:T(8,128)(2,1)S(1)}, u32[]{:S(2)}, u32[]{:S(2)}) collective-permute-start(bf16[256,16,32]{0,2,1:T(8,128)(2,1)S(1)} %fusion.4), channel_id=1, source_target_pairs={{0,1},{1,2},{2,3},{3,0},{4,5},{5,6},{6,7},{7,4},{8,9},{9,10},{10,1... | collective-permute-start | bytes 786440 | tf_op jit(solution)/shard_map/ppermute | solution.py:35
  159.6 13.9 %collective-permute-start.10 = (bf16[256,16,32]{0,2,1:T(8,128)(2,1)S(1)}, bf16[256,16,32]{0,2,1:T(8,128)(2,1)S(1)}, u32[]{:S(2)}, u32[]{:S(2)}) collective-permute-start(bf16[256,16,32]{0,2,1:T(8,128)(2,1)S(1)} %fusion.4), channel_id=1, source_target_pairs={{0,2},{1,3},{2,0},{3,1},{4,6},{5,7},{6,4},{7,5},{8,10},{9,11},{10,... | collective-permute-start | bytes 786440 | tf_op jit(solution)/shard_map/ppermute | solution.py:35
  161.9 11.5 %collective-permute-start.9 = (bf16[256,16,32]{0,2,1:T(8,128)(2,1)S(1)}, bf16[256,16,32]{0,2,1:T(8,128)(2,1)S(1)}, u32[]{:S(2)}, u32[]{:S(2)}) collective-permute-start(bf16[256,16,32]{0,2,1:T(8,128)(2,1)S(1)} %fusion.4), channel_id=1, source_target_pairs={{0,3},{1,0},{2,1},{3,2},{4,7},{5,4},{6,5},{7,6},{8,11},{9,8},{10,9... | collective-permute-start | bytes 786440 | tf_op jit(solution)/shard_map/ppermute | solution.py:35
  173.6 2.2 %copy-start.2 = (bf16[512,32,128]{2,1,0:T(8,128)(2,1)S(1)}, bf16[512,32,128]{2,1,0:T(8,128)(2,1)}, u32[]{:S(2)}) copy-start(bf16[512,32,128]{2,1,0:T(8,128)(2,1)} %param.15) | copy-start | bytes 12582916

commit v7 on v5

--- a/solution.py
+++ b/solution.py
@@ -116,7 +116,7 @@
         slot_place.astype(jnp.bfloat16).T, returned_flat, preferred_element_type=jnp.float32
     )
     touch_low = touch_low.astype(jnp.bfloat16).reshape((touch_count,) + value_shape)
-    touch_full = harm_gather(touch_low, 2)
+    touch_full = pick_rows(harm_gather(touch_low, 2), jnp.arange(touch_count, dtype=jnp.int32))
     correction = tile_product(return_tiles, touch_full, couple_node, node_count)
     update_low = (own_side - correction).astype(jnp.bfloat16)
     update_full = harm_gather(update_low, 2)

time: 184 us -> 181 us (0.984)
    concatenate x1 -> x0, local copies, waits for them, and re-layouts: 1.92 us -> none  [harm_gather(): return jnp.concatenate(blocks, axis)]
    unnamed x24 -> x26, local copies, waits for them, and re-layouts: 8.6 us -> 9.71 us
    dot_general x3 -> x4, matrix products: 3.76 us -> 4.24 us  [pick_rows(): jnp.einsum('tn,nrk->trk', marks, table, preferred_element_type=jnp.float32)]
where the time goes in v7:
time: 181 us
  waiting for transfers between devices  61.6 us (34%)
  local copies, waits for them, and re-layouts  33 us (18%)
  starting transfers between devices  32 us (18%)
  blocking collectives  25.2 us (14%)
  matrix products  25.1 us (14%)
  other arithmetic  2.94 us (2%)
    ppermute x12, waiting for transfers between devices, harm_gather(): lax.ppermute(values, 'harm', [(i, (i + s) % count) for i in range(count)])  32.8 us
    all_to_all x1, waiting for transfers between devices, on_device(): lax.all_to_all(packet, 'sub', split_axis=0, concat_axis=0, tiled=True)  28.8 us
    all_to_all x1, blocking collectives, on_device(): lax.all_to_all(replies, 'sub', split_axis=0, concat_axis=0, tiled=True)  25.2 us
    ppermute x12, starting transfers between devices, harm_gather(): lax.ppermute(values, 'harm', [(i, (i + s) % count) for i in range(count)])  19 us
    all_to_all x1, starting transfers between devices, on_device(): lax.all_to_all(packet, 'sub', split_axis=0, concat_axis=0, tiled=True)  13 us
    dot_general x3, matrix products, tile_product(): jnp.einsum('tok,trk->tro', tile_set, columns, preferred_element_type=jnp....  11.1 us
    unnamed x26, local copies, waits for them, and re-layouts  9.71 us
    dot_general x3, local copies, waits for them, and re-layouts, tile_product(): jnp.einsum('tok,trk->tro', tile_set, columns, preferred_element_type=jnp....  8.13 us
  transfers between devices with their start and end apart: 13, of which 9 were waited for; matrix products, arithmetic and copies ran while one was open for 2% of the time, Pallas kernels for 0%

profile of v7, /device:TPU:1, one launch (start us, length us, event | category | flops | bytes accessed | tf_op | source)
XLA Modules:
  0.0 180.8 jit_solution(7546298262046222657)
XLA Ops:
  0.7 2.5 %convolution_convert_fusion.1 = bf16[512,16,128]{2,0,1:T(8,128)(2,1)S(1)} fusion(f32[16,128,256]{2,1,0:T(8,128)} %param.13, s32[512]{0:T(512)} %param.17), kind=kOutput, calls=%fused_computation.6 | convolution fusion | flops 538574848 | bytes 4196352 | tf_op jit(solution)/shard_map/tn,nrk->trk/dot_general | solution.py:27
  3.6 4.3 %fusion.2 = f32[512,16,32]{2,1,0:T(8,128)} fusion(bf16[512,32,128]{2,1,0:T(8,128)(2,1)S(1)} %copy-done.1, bf16[512,16,128]{2,0,1:T(8,128)(2,1)S(1)} %convolution_convert_fusion.1), kind=kOutput, calls=%fused_computation.3 | convolution fusion | flops 67108864 | bytes 7340032 | tf_op jit(solution)/shard_map/tok,trk->tro/dot_general | solution.py:19
  7.9 2.8 %copy.49 = f32[512,16,32]{0,2,1:T(8,128)S(1)} copy(f32[512,16,32]{2,1,0:T(8,128)} %fusion.2) | data formatting | bytes 2097152 | tf_op jit(solution)/shard_map/tok,trk->tro/dot_general | solution.py:19
  11.5 2.2 %collective-permute-start.2 = (bf16[256,16,32]{0,2,1:T(8,128)(2,1)S(1)}, bf16[256,16,32]{0,2,1:T(8,128)(2,1)S(1)}, u32[]{:S(2)}, u32[]{:S(2)}) collective-permute-start(bf16[256,16,32]{0,2,1:T(8,128)(2,1)S(1)} %convolution_convert_fusion.5), channel_id=1, source_target_pairs={{0,1},{1,2},{2,3},{3,0},{4,5},{5,6},{6,7},{7,4},{8,9},{9,10},{10,1... | collective-permute-start | bytes 786440 | tf_op jit(solution)/shard_map/ppermute | solution.py:35
  13.6 2.6 %collective-permute-start.1 = (bf16[256,16,32]{0,2,1:T(8,128)(2,1)S(1)}, bf16[256,16,32]{0,2,1:T(8,128)(2,1)S(1)}, u32[]{:S(2)}, u32[]{:S(2)}) collective-permute-start(bf16[256,16,32]{0,2,1:T(8,128)(2,1)S(1)} %convolution_convert_fusion.5), channel_id=1, source_target_pairs={{0,2},{1,3},{2,0},{3,1},{4,6},{5,7},{6,4},{7,5},{8,10},{9,11},{10,... | collective-permute-start | bytes 786440 | tf_op jit(solution)/shard_map/ppermute | solution.py:35
  19.9 7.7 %collective-permute-done.1 = bf16[256,16,32]{0,2,1:T(8,128)(2,1)S(1)} collective-permute-done((bf16[256,16,32]{0,2,1:T(8,128)(2,1)S(1)}, bf16[256,16,32]{0,2,1:T(8,128)(2,1)S(1)}, u32[]{:S(2)}, u32[]{:S(2)}) %collective-permute-start.1) | collective-permute-done | bytes 262176 | tf_op jit(solution)/shard_map/ppermute | solution.py:35
  28.3 2.6 %fusion.33 = f32[256,16,32]{2,1,0:T(8,128)} fusion(bf16[256,32,128]{2,1,0:T(8,128)(2,1)S(1)} %copy-done, bf16[256,16,128]{2,0,1:T(8,128)(2,1)S(1)} %convolution_convert_fusion.3), kind=kOutput, calls=%fused_computation.45 | convolution fusion | flops 33554432 | bytes 3670016 | tf_op jit(solution)/shard_map/tok,trk->tro/dot_general | solution.py:75
  30.8 2.5 %copy.52 = f32[256,16,32]{0,2,1:T(8,128)S(1)} copy(f32[256,16,32]{2,1,0:T(8,128)} %fusion.33) | data formatting | bytes 1048576 | tf_op jit(solution)/shard_map/tok,trk->tro/dot_general | solution.py:75
  33.3 1.6 fusion.37
  36.4 1.7 all_to_all.11
  38.2 13.0 %all-to-all-start = ((f32[64,1,4224]{2,1,0:T(1,128)}), f32[64,1,4224]{2,1,0:T(1,128)S(1)}, u32[]{:S(2)}, u32[]{:S(2)}) async-start(f32[64,1,4224]{2,1,0:T(1,128)} %all_to_all.11), calls=%async_computation | async-start | bytes 2162688 | tf_op jit(solution)/shard_map/all_to_all | solution.py:100
  51.2 28.8 %all-to-all-done = f32[64,1,4224]{2,1,0:T(1,128)S(1)} async-done(((f32[64,1,4224]{2,1,0:T(1,128)}), f32[64,1,4224]{2,1,0:T(1,128)S(1)}, u32[]{:S(2)}, u32[]{:S(2)}) %all-to-all-start) | async-done | bytes 1081376 | tf_op jit(solution)/shard_map/all_to_all | solution.py:100
  81.5 1.6 copy.53
  85.5 2.1 %collective-permute-start.4 = (bf16[32,16,32]{2,0,1:T(8,128)(2,1)S(1)}, bf16[32,16,32]{2,0,1:T(8,128)(2,1)S(1)}, u32[]{:S(2)}, u32[]{:S(2)}) collective-permute-start(bf16[32,16,32]{2,0,1:T(8,128)(2,1)S(1)} %fusion.5), channel_id=1, source_target_pairs={{0,2},{1,3},{2,0},{3,1},{4,6},{5,7},{6,4},{7,5},{8,10},{9,11},{10,... | collective-permute-start | bytes 98312 | tf_op jit(solution)/shard_map/ppermute | solution.py:35
  89.6 2.9 %collective-permute-done.4 = bf16[32,16,32]{2,0,1:T(8,128)(2,1)S(1)} collective-permute-done((bf16[32,16,32]{2,0,1:T(8,128)(2,1)S(1)}, bf16[32,16,32]{2,0,1:T(8,128)(2,1)S(1)}, u32[]{:S(2)}, u32[]{:S(2)}) %collective-permute-start.4) | collective-permute-done | bytes 32800 | tf_op jit(solution)/shard_map/ppermute | solution.py:35
  93.2 2.8 %gather_fusion = bf16[512,16,32]{2,1,0:T(8,128)(2,1)} fusion(bf16[32,16,32]{2,1,0:T(8,128)(2,1)S(1)} %get-tuple-element.38, s32[1024]{0:T(1024)S(1)} %pad_clamp_fusion), kind=kCustom, calls=%fused_computation | custom fusion | bytes 1050624 | tf_op jit(solution)/shard_map/gather | solution.py:112
  96.0 3.7 %reshape.163 = bf16[64,2,2048]{2,1,0:T(2,128)(2,1)S(1)} reshape(bf16[64,8,16,32]{3,2,1,0:T(8,128)(2,1)} %bitcast.90) | data formatting | bytes 1048576
  99.7 25.2 %all_to_all.17 = bf16[64,2,2048]{2,1,0:T(2,128)(2,1)S(1)} all-to-all(bf16[64,2,2048]{2,1,0:T(2,128)(2,1)S(1)} %reshape.163), channel_id=1, replica_groups=mesh['sub'=64,'harm'=4] {'sub'}, dimensions={0} | all-to-all | bytes 1048576 | tf_op jit(solution)/shard_map/all_to_all | solution.py:113
  124.9 2.0 %reshape.164 = bf16[64,8,16,32]{3,2,1,0:T(8,128)(2,1)} reshape(bf16[64,2,2048]{2,1,0:T(2,128)(2,1)S(1)} %all_to_all.17) | data formatting | bytes 1048576
  127.0 3.4 %reshape.144 = bf16[512,512]{1,0:T(8,128)(2,1)S(1)} reshape(bf16[64,8,16,32]{3,2,1,0:T(8,128)(2,1)} %reshape.164) | data formatting | bytes 1048576 | tf_op jit(solution)/shard_map/reshape | solution.py:114
  130.8 1.5 collective-permute-start.8
  132.4 2.1 %collective-permute-start.7 = (bf16[256,16,32]{0,2,1:T(8,128)(2,1)S(1)}, bf16[256,16,32]{0,2,1:T(8,128)(2,1)S(1)}, u32[]{:S(2)}, u32[]{:S(2)}) collective-permute-start(bf16[256,16,32]{0,2,1:T(8,128)(2,1)S(1)} %bitcast.97), channel_id=1, source_target_pairs={{0,2},{1,3},{2,0},{3,1},{4,6},{5,7},{6,4},{7,5},{8,10},{9,11},{10,... | collective-permute-start | bytes 786440 | tf_op jit(solution)/shard_map/ppermute | solution.py:35
  135.3 4.3 %collective-permute-done.8 = bf16[256,16,32]{0,2,1:T(8,128)(2,1)S(1)} collective-permute-done((bf16[256,16,32]{0,2,1:T(8,128)(2,1)S(1)}, bf16[256,16,32]{0,2,1:T(8,128)(2,1)S(1)}, u32[]{:S(2)}, u32[]{:S(2)}) %collective-permute-start.8) | collective-permute-done | bytes 262176 | tf_op jit(solution)/shard_map/ppermute | solution.py:35
  139.6 6.5 %collective-permute-done.7 = bf16[256,16,32]{0,2,1:T(8,128)(2,1)S(1)} collective-permute-done((bf16[256,16,32]{0,2,1:T(8,128)(2,1)S(1)}, bf16[256,16,32]{0,2,1:T(8,128)(2,1)S(1)}, u32[]{:S(2)}, u32[]{:S(2)}) %collective-permute-start.7) | collective-permute-done | bytes 262176 | tf_op jit(solution)/shard_map/ppermute | solution.py:35
  147.8 2.5 %fusion.31 = f32[256,16,32]{2,1,0:T(8,128)} fusion(bf16[256,32,128]{2,1,0:T(8,128)(2,1)S(1)} %copy-done.3, bf16[256,16,128]{2,0,1:T(8,128)(2,1)S(1)} %convolution_convert_fusion.2), kind=kOutput, calls=%fused_computation.43 | convolution fusion | flops 33554432 | bytes 3670016 | tf_op jit(solution)/shard_map/tok,trk->tro/dot_general | solution.py:19
  150.4 2.5 %copy.58 = f32[256,16,32]{0,2,1:T(8,128)S(1)} copy(f32[256,16,32]{2,1,0:T(8,128)} %fusion.31) | data formatting | bytes 1048576 | tf_op jit(solution)/shard_map/tok,trk->tro/dot_general | solution.py:19
  154.4 1.7 collective-permute-start.11
  156.1 2.4 %collective-permute-start.10 = (bf16[256,16,32]{0,2,1:T(8,128)(2,1)S(1)}, bf16[256,16,32]{0,2,1:T(8,128)(2,1)S(1)}, u32[]{:S(2)}, u32[]{:S(2)}) collective-permute-start(bf16[256,16,32]{0,2,1:T(8,128)(2,1)S(1)} %fusion.4), channel_id=1, source_target_pairs={{0,2},{1,3},{2,0},{3,1},{4,6},{5,7},{6,4},{7,5},{8,10},{9,11},{10,... | collective-permute-start | bytes 786440 | tf_op jit(solution)/shard_map/ppermute | solution.py:35
  159.4 3.1 %collective-permute-done.11 = bf16[256,16,32]{0,2,1:T(8,128)(2,1)S(1)} collective-permute-done((bf16[256,16,32]{0,2,1:T(8,128)(2,1)S(1)}, bf16[256,16,32]{0,2,1:T(8,128)(2,1)S(1)}, u32[]{:S(2)}, u32[]{:S(2)}) %collective-permute-start.11) | collective-permute-done | bytes 262176 | tf_op jit(solution)/shard_map/ppermute | solution.py:35
  162.6 7.4 %collective-permute-done.10 = bf16[256,16,32]{0,2,1:T(8,128)(2,1)S(1)} collective-permute-done((bf16[256,16,32]{0,2,1:T(8,128)(2,1)S(1)}, bf16[256,16,32]{0,2,1:T(8,128)(2,1)S(1)}, u32[]{:S(2)}, u32[]{:S(2)}) %collective-permute-start.10) | collective-permute-done | bytes 262176 | tf_op jit(solution)/shard_map/ppermute | solution.py:35
  172.3 4.3 %fusion = f32[512,16,32]{2,1,0:T(8,128)} fusion(bf16[512,32,128]{2,1,0:T(8,128)(2,1)S(1)} %copy-done.2, bf16[512,16,128]{2,0,1:T(8,128)(2,1)S(1)} %convolution_convert_fusion), kind=kOutput, calls=%fused_computation.1 | convolution fusion | flops 67108864 | bytes 7340032 | tf_op jit(solution)/shard_map/tok,trk->tro/dot_general | solution.py:19
  176.6 2.8 %copy.61 = f32[512,16,32]{0,2,1:T(8,128)S(1)} copy(f32[512,16,32]{2,1,0:T(8,128)} %fusion) | data formatting | bytes 2097152 | tf_op jit(solution)/shard_map/tok,trk->tro/dot_general | solution.py:19
  (70 shorter events, 22.6 us)
Async XLA Ops:
  0.6 27.6 %copy-start = (bf16[256,32,128]{2,1,0:T(8,128)(2,1)S(1)}, bf16[256,32,128]{2,1,0:T(8,128)(2,1)}, u32[]{:S(2)}) copy-start(bf16[256,32,128]{2,1,0:T(8,128)(2,1)} %param.18) | copy-start | bytes 6291460
  0.6 3.0 %copy-start.1 = (bf16[512,32,128]{2,1,0:T(8,128)(2,1)S(1)}, bf16[512,32,128]{2,1,0:T(8,128)(2,1)}, u32[]{:S(2)}) copy-start(bf16[512,32,128]{2,1,0:T(8,128)(2,1)} %param.15) | copy-start | bytes 12582916
  7.9 2.9 %copy-start.7 = (s32[512]{0:T(512)S(1)}, s32[512]{0:T(512)}, u32[]{:S(2)}) copy-start(s32[512]{0:T(512)} %param.16) | copy-start | bytes 6148
  7.9 9.4 %copy-start.6 = (s32[256,1]{0,1:T(1,128)S(1)}, s32[256,1]{0,1:T(1,128)}, u32[]{:S(2)}) copy-start(s32[256,1]{0,1:T(1,128)} %param.21) | copy-start | bytes 3076
  7.9 10.4 %copy-start.9 = (s32[256]{0:T(256)S(1)}, s32[256]{0:T(256)}, u32[]{:S(2)}) copy-start(s32[256]{0:T(256)} %param.22) | copy-start | bytes 3076
  10.8 17.0 %copy-start.10 = (s32[256]{0:T(256)S(1)}, s32[256]{0:T(256)}, u32[]{:S(2)}) copy-start(s32[256]{0:T(256)} %param.20) | copy-start | bytes 3076
  11.5 8.5 %collective-permute-start.2 = (bf16[256,16,32]{0,2,1:T(8,128)(2,1)S(1)}, bf16[256,16,32]{0,2,1:T(8,128)(2,1)S(1)}, u32[]{:S(2)}, u32[]{:S(2)}) collective-permute-start(bf16[256,16,32]{0,2,1:T(8,128)(2,1)S(1)} %convolution_convert_fusion.5), channel_id=1, source_target_pairs={{0,1},{1,2},{2,3},{3,0},{4,5},{5,6},{6,7},{7,4},{8,9},{9,10},{10,1... | collective-permute-start | bytes 786440 | tf_op jit(solution)/shard_map/ppermute | solution.py:35
  13.6 14.0 %collective-permute-start.1 = (bf16[256,16,32]{0,2,1:T(8,128)(2,1)S(1)}, bf16[256,16,32]{0,2,1:T(8,128)(2,1)S(1)}, u32[]{:S(2)}, u32[]{:S(2)}) collective-permute-start(bf16[256,16,32]{0,2,1:T(8,128)(2,1)S(1)} %convolution_convert_fusion.5), channel_id=1, source_target_pairs={{0,2},{1,3},{2,0},{3,1},{4,6},{5,7},{6,4},{7,5},{8,10},{9,11},{10,... | collective-permute-start | bytes 786440 | tf_op jit(solution)/shard_map/ppermute | solution.py:35
  16.3 11.3 %collective-permute-start = (bf16[256,16,32]{0,2,1:T(8,128)(2,1)S(1)}, bf16[256,16,32]{0,2,1:T(8,128)(2,1)S(1)}, u32[]{:S(2)}, u32[]{:S(2)}) collective-permute-start(bf16[256,16,32]{0,2,1:T(8,128)(2,1)S(1)} %convolution_convert_fusion.5), channel_id=1, source_target_pairs={{0,3},{1,0},{2,1},{3,2},{4,7},{5,4},{6,5},{7,6},{8,11},{9,8},{10,9... | collective-permute-start | bytes 786440 | tf_op jit(solution)/shard_map/ppermute | solution.py:35
  38.2 41.8 %all-to-all-start = ((f32[64,1,4224]{2,1,0:T(1,128)}), f32[64,1,4224]{2,1,0:T(1,128)S(1)}, u32[]{:S(2)}, u32[]{:S(2)}) async-start(f32[64,1,4224]{2,1,0:T(1,128)} %all_to_all.11), calls=%async_computation | async-start | bytes 2162688 | tf_op jit(solution)/shard_map/all_to_all | solution.py:100
  80.4 2.8 %copy-start.5 = (f32[16,128,32]{1,2,0:T(8,128)S(1)}, f32[16,128,32]{1,2,0:T(8,128)}, u32[]{:S(2)}) copy-start(f32[16,128,32]{1,2,0:T(8,128)} %param.14) | copy-start | bytes 786436
  83.1 9.9 %copy-start.4 = (bf16[32,32,128]{2,1,0:T(8,128)(2,1)S(1)}, bf16[32,32,128]{2,1,0:T(8,128)(2,1)}, u32[]{:S(2)}) copy-start(bf16[32,32,128]{2,1,0:T(8,128)(2,1)} %param.23) | copy-start | bytes 786436
  84.4 5.1 %collective-permute-start.5 = (bf16[32,16,32]{2,0,1:T(8,128)(2,1)S(1)}, bf16[32,16,32]{2,0,1:T(8,128)(2,1)S(1)}, u32[]{:S(2)}, u32[]{:S(2)}) collective-permute-start(bf16[32,16,32]{2,0,1:T(8,128)(2,1)S(1)} %fusion.5), channel_id=1, source_target_pairs={{0,1},{1,2},{2,3},{3,0},{4,5},{5,6},{6,7},{7,4},{8,9},{9,10},{10,1... | collective-permute-start | bytes 98312 | tf_op jit(solution)/shard_map/ppermute | solution.py:35
  85.5 7.0 %collective-permute-start.4 = (bf16[32,16,32]{2,0,1:T(8,128)(2,1)S(1)}, bf16[32,16,32]{2,0,1:T(8,128)(2,1)S(1)}, u32[]{:S(2)}, u32[]{:S(2)}) collective-permute-start(bf16[32,16,32]{2,0,1:T(8,128)(2,1)S(1)} %fusion.5), channel_id=1, source_target_pairs={{0,2},{1,3},{2,0},{3,1},{4,6},{5,7},{6,4},{7,5},{8,10},{9,11},{10,... | collective-permute-start | bytes 98312 | tf_op jit(solution)/shard_map/ppermute | solution.py:35
  87.6 5.1 %collective-permute-start.3 = (bf16[32,16,32]{2,0,1:T(8,128)(2,1)S(1)}, bf16[32,16,32]{2,0,1:T(8,128)(2,1)S(1)}, u32[]{:S(2)}, u32[]{:S(2)}) collective-permute-start(bf16[32,16,32]{2,0,1:T(8,128)(2,1)S(1)} %fusion.5), channel_id=1, source_target_pairs={{0,3},{1,0},{2,1},{3,2},{4,7},{5,4},{6,5},{7,6},{8,11},{9,8},{10,9... | collective-permute-start | bytes 98312 | tf_op jit(solution)/shard_map/ppermute | solution.py:35
  130.8 8.8 %collective-permute-start.8 = (bf16[256,16,32]{0,2,1:T(8,128)(2,1)S(1)}, bf16[256,16,32]{0,2,1:T(8,128)(2,1)S(1)}, u32[]{:S(2)}, u32[]{:S(2)}) collective-permute-start(bf16[256,16,32]{0,2,1:T(8,128)(2,1)S(1)} %bitcast.96), channel_id=1, source_target_pairs={{0,1},{1,2},{2,3},{3,0},{4,5},{5,6},{6,7},{7,4},{8,9},{9,10},{10,1... | collective-permute-start | bytes 786440 | tf_op jit(solution)/shard_map/ppermute | solution.py:35
  132.4 13.7 %collective-permute-start.7 = (bf16[256,16,32]{0,2,1:T(8,128)(2,1)S(1)}, bf16[256,16,32]{0,2,1:T(8,128)(2,1)S(1)}, u32[]{:S(2)}, u32[]{:S(2)}) collective-permute-start(bf16[256,16,32]{0,2,1:T(8,128)(2,1)S(1)} %bitcast.97), channel_id=1, source_target_pairs={{0,2},{1,3},{2,0},{3,1},{4,6},{5,7},{6,4},{7,5},{8,10},{9,11},{10,... | collective-permute-start | bytes 786440 | tf_op jit(solution)/shard_map/ppermute | solution.py:35
  134.5 11.6 %collective-permute-start.6 = (bf16[256,16,32]{0,2,1:T(8,128)(2,1)S(1)}, bf16[256,16,32]{0,2,1:T(8,128)(2,1)S(1)}, u32[]{:S(2)}, u32[]{:S(2)}) collective-permute-start(bf16[256,16,32]{0,2,1:T(8,128)(2,1)S(1)} %bitcast.98), channel_id=1, source_target_pairs={{0,3},{1,0},{2,1},{3,2},{4,7},{5,4},{6,5},{7,6},{8,11},{9,8},{10,9... | collective-permute-start | bytes 786440 | tf_op jit(solution)/shard_map/ppermute | solution.py:35
  146.2 1.6 copy-start.3
  152.9 17.2 %copy-start.8 = (s32[512]{0:T(512)S(1)}, s32[512]{0:T(512)}, u32[]{:S(2)}) copy-start(s32[512]{0:T(512)} %param.17) | copy-start | bytes 6148
  154.4 8.2 %collective-permute-start.11 = (bf16[256,16,32]{0,2,1:T(8,128)(2,1)S(1)}, bf16[256,16,32]{0,2,1:T(8,128)(2,1)S(1)}, u32[]{:S(2)}, u32[]{:S(2)}) collective-permute-start(bf16[256,16,32]{0,2,1:T(8,128)(2,1)S(1)} %fusion.4), channel_id=1, source_target_pairs={{0,1},{1,2},{2,3},{3,0},{4,5},{5,6},{6,7},{7,4},{8,9},{9,10},{10,1... | collective-permute-start | bytes 786440 | tf_op jit(solution)/shard_map/ppermute | solution.py:35
  156.1 13.9 %collective-permute-start.10 = (bf16[256,16,32]{0,2,1:T(8,128)(2,1)S(1)}, bf16[256,16,32]{0,2,1:T(8,128)(2,1)S(1)}, u32[]{:S(2)}, u32[]{:S(2)}) collective-permute-start(bf16[256,16,32]{0,2,1:T(8,128)(2,1)S(1)} %fusion.4), channel_id=1, source_target_pairs={{0,2},{1,3},{2,0},{3,1},{4,6},{5,7},{6,4},{7,5},{8,10},{9,11},{10,... | collective-permute-start | bytes 786440 | tf_op jit(solution)/shard_map/ppermute | solution.py:35
  158.4 11.5 %collective-permute-start.9 = (bf16[256,16,32]{0,2,1:T(8,128)(2,1)S(1)}, bf16[256,16,32]{0,2,1:T(8,128)(2,1)S(1)}, u32[]{:S(2)}, u32[]{:S(2)}) collective-permute-start(bf16[256,16,32]{0,2,1:T(8,128)(2,1)S(1)} %fusion.4), channel_id=1, source_target_pairs={{0,3},{1,0},{2,1},{3,2},{4,7},{5,4},{6,5},{7,6},{8,11},{9,8},{10,9... | collective-permute-start | bytes 786440 | tf_op jit(solution)/shard_map/ppermute | solution.py:35
  170.1 2.2 %copy-start.2 = (bf16[512,32,128]{2,1,0:T(8,128)(2,1)S(1)}, bf16[512,32,128]{2,1,0:T(8,128)(2,1)}, u32[]{:S(2)}) copy-start(bf16[512,32,128]{2,1,0:T(8,128)(2,1)} %param.15) | copy-start | bytes 12582916

commit v8 on v7

--- a/solution.py
+++ b/solution.py
@@ -104,7 +104,7 @@
     arrived_rows = arrived_rows.astype(jnp.int32).reshape(-1)
     incoming = collect(arrived, arrived_rows, row_count).reshape((row_count,) + value_shape)
     residual_low = (own_border - incoming).astype(jnp.bfloat16)
-    residual_full = harm_gather(residual_low, 2)
+    residual_full = pick_rows(harm_gather(residual_low, 2), jnp.arange(row_count, dtype=jnp.int32))
     solved = jnp.einsum(
         "bok,brk->bro", border_inverse, residual_full, preferred_element_type=jnp.float32
     )

time: 181 us -> 182 us (level)
    dot_general x4 -> x5, matrix products: 4.24 us -> 4.55 us  [pick_rows(): jnp.einsum('tn,nrk->trk', marks, table, preferred_element_type=jnp.float32)]
where the time goes in v8:
time: 182 us; the launch traced here: 181 us
  waiting for transfers between devices  61.6 us (34%)
  local copies, waits for them, and re-layouts  33 us (18%)
  starting transfers between devices  32 us (18%)
  matrix products  25.4 us (14%)
  blocking collectives  25.2 us (14%)
  other arithmetic  2.75 us (2%)
    ppermute x12, waiting for transfers between devices, harm_gather(): lax.ppermute(values, 'harm', [(i, (i + s) % count) for i in range(count)])  32.8 us
    all_to_all x1, waiting for transfers between devices, on_device(): lax.all_to_all(packet, 'sub', split_axis=0, concat_axis=0, tiled=True)  28.8 us
    all_to_all x1, blocking collectives, on_device(): lax.all_to_all(replies, 'sub', split_axis=0, concat_axis=0, tiled=True)  25.2 us
    ppermute x12, starting transfers between devices, harm_gather(): lax.ppermute(values, 'harm', [(i, (i + s) % count) for i in range(count)])  19 us
    all_to_all x1, starting transfers between devices, on_device(): lax.all_to_all(packet, 'sub', split_axis=0, concat_axis=0, tiled=True)  13 us
    dot_general x3, matrix products, tile_product(): jnp.einsum('tok,trk->tro', tile_set, columns, preferred_element_type=jnp....  11.1 us
    unnamed x26, local copies, waits for them, and re-layouts  9.7 us
    dot_general x3, local copies, waits for them, and re-layouts, tile_product(): jnp.einsum('tok,trk->tro', tile_set, columns, preferred_element_type=jnp....  8.13 us
  transfers between devices with their start and end apart: 13, of which 9 were waited for; matrix products, arithmetic and copies ran while one was open for 2% of the time, Pallas kernels for 0%

profile of v8, /device:TPU:1, one launch (start us, length us, event | category | flops | bytes accessed | tf_op | source)
XLA Modules:
  0.0 181.0 jit_solution(17866517053594382605)
XLA Ops:
  0.7 2.5 %convolution_convert_fusion.1 = bf16[512,16,128]{2,0,1:T(8,128)(2,1)S(1)} fusion(f32[16,128,256]{2,1,0:T(8,128)} %param.13, s32[512]{0:T(512)} %param.17), kind=kOutput, calls=%fused_computation.6 | convolution fusion | flops 538574848 | bytes 4196352 | tf_op jit(solution)/shard_map/tn,nrk->trk/dot_general | solution.py:27
  3.6 4.3 %fusion.2 = f32[512,16,32]{2,1,0:T(8,128)} fusion(bf16[512,32,128]{2,1,0:T(8,128)(2,1)S(1)} %copy-done.1, bf16[512,16,128]{2,0,1:T(8,128)(2,1)S(1)} %convolution_convert_fusion.1), kind=kOutput, calls=%fused_computation.3 | convolution fusion | flops 67108864 | bytes 7340032 | tf_op jit(solution)/shard_map/tok,trk->tro/dot_general | solution.py:19
  7.9 2.8 %copy.47 = f32[512,16,32]{0,2,1:T(8,128)S(1)} copy(f32[512,16,32]{2,1,0:T(8,128)} %fusion.2) | data formatting | bytes 2097152 | tf_op jit(solution)/shard_map/tok,trk->tro/dot_general | solution.py:19
  11.5 2.2 %collective-permute-start.2 = (bf16[256,16,32]{0,2,1:T(8,128)(2,1)S(1)}, bf16[256,16,32]{0,2,1:T(8,128)(2,1)S(1)}, u32[]{:S(2)}, u32[]{:S(2)}) collective-permute-start(bf16[256,16,32]{0,2,1:T(8,128)(2,1)S(1)} %convolution_convert_fusion.5), channel_id=1, source_target_pairs={{0,1},{1,2},{2,3},{3,0},{4,5},{5,6},{6,7},{7,4},{8,9},{9,10},{10,1... | collective-permute-start | bytes 786440 | tf_op jit(solution)/shard_map/ppermute | solution.py:35
  13.6 2.6 %collective-permute-start.1 = (bf16[256,16,32]{0,2,1:T(8,128)(2,1)S(1)}, bf16[256,16,32]{0,2,1:T(8,128)(2,1)S(1)}, u32[]{:S(2)}, u32[]{:S(2)}) collective-permute-start(bf16[256,16,32]{0,2,1:T(8,128)(2,1)S(1)} %convolution_convert_fusion.5), channel_id=1, source_target_pairs={{0,2},{1,3},{2,0},{3,1},{4,6},{5,7},{6,4},{7,5},{8,10},{9,11},{10,... | collective-permute-start | bytes 786440 | tf_op jit(solution)/shard_map/ppermute | solution.py:35
  19.9 7.7 %collective-permute-done.1 = bf16[256,16,32]{0,2,1:T(8,128)(2,1)S(1)} collective-permute-done((bf16[256,16,32]{0,2,1:T(8,128)(2,1)S(1)}, bf16[256,16,32]{0,2,1:T(8,128)(2,1)S(1)}, u32[]{:S(2)}, u32[]{:S(2)}) %collective-permute-start.1) | collective-permute-done | bytes 262176 | tf_op jit(solution)/shard_map/ppermute | solution.py:35
  28.3 2.6 %fusion.33 = f32[256,16,32]{2,1,0:T(8,128)} fusion(bf16[256,32,128]{2,1,0:T(8,128)(2,1)S(1)} %copy-done, bf16[256,16,128]{2,0,1:T(8,128)(2,1)S(1)} %convolution_convert_fusion.3), kind=kOutput, calls=%fused_computation.46 | convolution fusion | flops 33554432 | bytes 3670016 | tf_op jit(solution)/shard_map/tok,trk->tro/dot_general | solution.py:75
  30.8 2.5 %copy.50 = f32[256,16,32]{0,2,1:T(8,128)S(1)} copy(f32[256,16,32]{2,1,0:T(8,128)} %fusion.33) | data formatting | bytes 1048576 | tf_op jit(solution)/shard_map/tok,trk->tro/dot_general | solution.py:75
  33.3 1.6 fusion.37
  36.4 1.7 all_to_all.11
  38.2 13.0 %all-to-all-start = ((f32[64,1,4224]{2,1,0:T(1,128)}), f32[64,1,4224]{2,1,0:T(1,128)S(1)}, u32[]{:S(2)}, u32[]{:S(2)}) async-start(f32[64,1,4224]{2,1,0:T(1,128)} %all_to_all.11), calls=%async_computation | async-start | bytes 2162688 | tf_op jit(solution)/shard_map/all_to_all | solution.py:100
  51.2 28.8 %all-to-all-done = f32[64,1,4224]{2,1,0:T(1,128)S(1)} async-done(((f32[64,1,4224]{2,1,0:T(1,128)}), f32[64,1,4224]{2,1,0:T(1,128)S(1)}, u32[]{:S(2)}, u32[]{:S(2)}) %all-to-all-start) | async-done | bytes 1081376 | tf_op jit(solution)/shard_map/all_to_all | solution.py:100
  81.5 1.6 copy.51
  85.5 2.1 %collective-permute-start.4 = (bf16[32,16,32]{2,0,1:T(8,128)(2,1)S(1)}, bf16[32,16,32]{2,0,1:T(8,128)(2,1)S(1)}, u32[]{:S(2)}, u32[]{:S(2)}) collective-permute-start(bf16[32,16,32]{2,0,1:T(8,128)(2,1)S(1)} %fusion.5), channel_id=1, source_target_pairs={{0,2},{1,3},{2,0},{3,1},{4,6},{5,7},{6,4},{7,5},{8,10},{9,11},{10,... | collective-permute-start | bytes 98312 | tf_op jit(solution)/shard_map/ppermute | solution.py:35
  89.6 2.9 %collective-permute-done.4 = bf16[32,16,32]{2,0,1:T(8,128)(2,1)S(1)} collective-permute-done((bf16[32,16,32]{2,0,1:T(8,128)(2,1)S(1)}, bf16[32,16,32]{2,0,1:T(8,128)(2,1)S(1)}, u32[]{:S(2)}, u32[]{:S(2)}) %collective-permute-start.4) | collective-permute-done | bytes 32800 | tf_op jit(solution)/shard_map/ppermute | solution.py:35
  93.3 2.8 %gather_fusion = bf16[512,16,32]{2,1,0:T(8,128)(2,1)} fusion(bf16[32,16,32]{2,1,0:T(8,128)(2,1)S(1)} %get-tuple-element.38, s32[1024]{0:T(1024)S(1)} %pad_clamp_fusion), kind=kCustom, calls=%fused_computation | custom fusion | bytes 1050624 | tf_op jit(solution)/shard_map/gather | solution.py:112
  96.1 3.7 %reshape.164 = bf16[64,2,2048]{2,1,0:T(2,128)(2,1)S(1)} reshape(bf16[64,8,16,32]{3,2,1,0:T(8,128)(2,1)} %bitcast.93) | data formatting | bytes 1048576
  99.8 25.2 %all_to_all.17 = bf16[64,2,2048]{2,1,0:T(2,128)(2,1)S(1)} all-to-all(bf16[64,2,2048]{2,1,0:T(2,128)(2,1)S(1)} %reshape.164), channel_id=1, replica_groups=mesh['sub'=64,'harm'=4] {'sub'}, dimensions={0} | all-to-all | bytes 1048576 | tf_op jit(solution)/shard_map/all_to_all | solution.py:113
  125.1 2.0 %reshape.165 = bf16[64,8,16,32]{3,2,1,0:T(8,128)(2,1)} reshape(bf16[64,2,2048]{2,1,0:T(2,128)(2,1)S(1)} %all_to_all.17) | data formatting | bytes 1048576
  127.1 3.4 %reshape.144 = bf16[512,512]{1,0:T(8,128)(2,1)S(1)} reshape(bf16[64,8,16,32]{3,2,1,0:T(8,128)(2,1)} %reshape.165) | data formatting | bytes 1048576 | tf_op jit(solution)/shard_map/reshape | solution.py:114
  131.0 1.5 collective-permute-start.8
  132.5 2.1 %collective-permute-start.7 = (bf16[256,16,32]{0,2,1:T(8,128)(2,1)S(1)}, bf16[256,16,32]{0,2,1:T(8,128)(2,1)S(1)}, u32[]{:S(2)}, u32[]{:S(2)}) collective-permute-start(bf16[256,16,32]{0,2,1:T(8,128)(2,1)S(1)} %bitcast.100), channel_id=1, source_target_pairs={{0,2},{1,3},{2,0},{3,1},{4,6},{5,7},{6,4},{7,5},{8,10},{9,11},{10,... | collective-permute-start | bytes 786440 | tf_op jit(solution)/shard_map/ppermute | solution.py:35
  135.4 4.3 %collective-permute-done.8 = bf16[256,16,32]{0,2,1:T(8,128)(2,1)S(1)} collective-permute-done((bf16[256,16,32]{0,2,1:T(8,128)(2,1)S(1)}, bf16[256,16,32]{0,2,1:T(8,128)(2,1)S(1)}, u32[]{:S(2)}, u32[]{:S(2)}) %collective-permute-start.8) | collective-permute-done | bytes 262176 | tf_op jit(solution)/shard_map/ppermute | solution.py:35
  139.7 6.5 %collective-permute-done.7 = bf16[256,16,32]{0,2,1:T(8,128)(2,1)S(1)} collective-permute-done((bf16[256,16,32]{0,2,1:T(8,128)(2,1)S(1)}, bf16[256,16,32]{0,2,1:T(8,128)(2,1)S(1)}, u32[]{:S(2)}, u32[]{:S(2)}) %collective-permute-start.7) | collective-permute-done | bytes 262176 | tf_op jit(solution)/shard_map/ppermute | solution.py:35
  148.0 2.5 %fusion.31 = f32[256,16,32]{2,1,0:T(8,128)} fusion(bf16[256,32,128]{2,1,0:T(8,128)(2,1)S(1)} %copy-done.3, bf16[256,16,128]{2,0,1:T(8,128)(2,1)S(1)} %convolution_convert_fusion.2), kind=kOutput, calls=%fused_computation.44 | convolution fusion | flops 33554432 | bytes 3670016 | tf_op jit(solution)/shard_map/tok,trk->tro/dot_general | solution.py:19
  150.5 2.5 %copy.56 = f32[256,16,32]{0,2,1:T(8,128)S(1)} copy(f32[256,16,32]{2,1,0:T(8,128)} %fusion.31) | data formatting | bytes 1048576 | tf_op jit(solution)/shard_map/tok,trk->tro/dot_general | solution.py:19
  154.5 1.7 collective-permute-start.11
  156.2 2.4 %collective-permute-start.10 = (bf16[256,16,32]{0,2,1:T(8,128)(2,1)S(1)}, bf16[256,16,32]{0,2,1:T(8,128)(2,1)S(1)}, u32[]{:S(2)}, u32[]{:S(2)}) collective-permute-start(bf16[256,16,32]{0,2,1:T(8,128)(2,1)S(1)} %fusion.4), channel_id=1, source_target_pairs={{0,2},{1,3},{2,0},{3,1},{4,6},{5,7},{6,4},{7,5},{8,10},{9,11},{10,... | collective-permute-start | bytes 786440 | tf_op jit(solution)/shard_map/ppermute | solution.py:35
  159.6 3.1 %collective-permute-done.11 = bf16[256,16,32]{0,2,1:T(8,128)(2,1)S(1)} collective-permute-done((bf16[256,16,32]{0,2,1:T(8,128)(2,1)S(1)}, bf16[256,16,32]{0,2,1:T(8,128)(2,1)S(1)}, u32[]{:S(2)}, u32[]{:S(2)}) %collective-permute-start.11) | collective-permute-done | bytes 262176 | tf_op jit(solution)/shard_map/ppermute | solution.py:35
  162.7 7.4 %collective-permute-done.10 = bf16[256,16,32]{0,2,1:T(8,128)(2,1)S(1)} collective-permute-done((bf16[256,16,32]{0,2,1:T(8,128)(2,1)S(1)}, bf16[256,16,32]{0,2,1:T(8,128)(2,1)S(1)}, u32[]{:S(2)}, u32[]{:S(2)}) %collective-permute-start.10) | collective-permute-done | bytes 262176 | tf_op jit(solution)/shard_map/ppermute | solution.py:35
  172.4 4.3 %fusion = f32[512,16,32]{2,1,0:T(8,128)} fusion(bf16[512,32,128]{2,1,0:T(8,128)(2,1)S(1)} %copy-done.2, bf16[512,16,128]{2,0,1:T(8,128)(2,1)S(1)} %convolution_convert_fusion), kind=kOutput, calls=%fused_computation.1 | convolution fusion | flops 67108864 | bytes 7340032 | tf_op jit(solution)/shard_map/tok,trk->tro/dot_general | solution.py:19
  176.7 2.8 %copy.59 = f32[512,16,32]{0,2,1:T(8,128)S(1)} copy(f32[512,16,32]{2,1,0:T(8,128)} %fusion) | data formatting | bytes 2097152 | tf_op jit(solution)/shard_map/tok,trk->tro/dot_general | solution.py:19
  (70 shorter events, 22.7 us)
Async XLA Ops:
  0.6 27.6 %copy-start = (bf16[256,32,128]{2,1,0:T(8,128)(2,1)S(1)}, bf16[256,32,128]{2,1,0:T(8,128)(2,1)}, u32[]{:S(2)}) copy-start(bf16[256,32,128]{2,1,0:T(8,128)(2,1)} %param.18) | copy-start | bytes 6291460
  0.6 3.0 %copy-start.1 = (bf16[512,32,128]{2,1,0:T(8,128)(2,1)S(1)}, bf16[512,32,128]{2,1,0:T(8,128)(2,1)}, u32[]{:S(2)}) copy-start(bf16[512,32,128]{2,1,0:T(8,128)(2,1)} %param.15) | copy-start | bytes 12582916
  7.9 2.9 %copy-start.7 = (s32[512]{0:T(512)S(1)}, s32[512]{0:T(512)}, u32[]{:S(2)}) copy-start(s32[512]{0:T(512)} %param.16) | copy-start | bytes 6148
  7.9 9.4 %copy-start.6 = (s32[256,1]{0,1:T(1,128)S(1)}, s32[256,1]{0,1:T(1,128)}, u32[]{:S(2)}) copy-start(s32[256,1]{0,1:T(1,128)} %param.21) | copy-start | bytes 3076
  7.9 10.4 %copy-start.9 = (s32[256]{0:T(256)S(1)}, s32[256]{0:T(256)}, u32[]{:S(2)}) copy-start(s32[256]{0:T(256)} %param.22) | copy-start | bytes 3076
  10.8 17.0 %copy-start.10 = (s32[256]{0:T(256)S(1)}, s32[256]{0:T(256)}, u32[]{:S(2)}) copy-start(s32[256]{0:T(256)} %param.20) | copy-start | bytes 3076
  11.5 8.5 %collective-permute-start.2 = (bf16[256,16,32]{0,2,1:T(8,128)(2,1)S(1)}, bf16[256,16,32]{0,2,1:T(8,128)(2,1)S(1)}, u32[]{:S(2)}, u32[]{:S(2)}) collective-permute-start(bf16[256,16,32]{0,2,1:T(8,128)(2,1)S(1)} %convolution_convert_fusion.5), channel_id=1, source_target_pairs={{0,1},{1,2},{2,3},{3,0},{4,5},{5,6},{6,7},{7,4},{8,9},{9,10},{10,1... | collective-permute-start | bytes 786440 | tf_op jit(solution)/shard_map/ppermute | solution.py:35
  13.6 14.0 %collective-permute-start.1 = (bf16[256,16,32]{0,2,1:T(8,128)(2,1)S(1)}, bf16[256,16,32]{0,2,1:T(8,128)(2,1)S(1)}, u32[]{:S(2)}, u32[]{:S(2)}) collective-permute-start(bf16[256,16,32]{0,2,1:T(8,128)(2,1)S(1)} %convolution_convert_fusion.5), channel_id=1, source_target_pairs={{0,2},{1,3},{2,0},{3,1},{4,6},{5,7},{6,4},{7,5},{8,10},{9,11},{10,... | collective-permute-start | bytes 786440 | tf_op jit(solution)/shard_map/ppermute | solution.py:35
  16.3 11.3 %collective-permute-start = (bf16[256,16,32]{0,2,1:T(8,128)(2,1)S(1)}, bf16[256,16,32]{0,2,1:T(8,128)(2,1)S(1)}, u32[]{:S(2)}, u32[]{:S(2)}) collective-permute-start(bf16[256,16,32]{0,2,1:T(8,128)(2,1)S(1)} %convolution_convert_fusion.5), channel_id=1, source_target_pairs={{0,3},{1,0},{2,1},{3,2},{4,7},{5,4},{6,5},{7,6},{8,11},{9,8},{10,9... | collective-permute-start | bytes 786440 | tf_op jit(solution)/shard_map/ppermute | solution.py:35
  38.2 41.8 %all-to-all-start = ((f32[64,1,4224]{2,1,0:T(1,128)}), f32[64,1,4224]{2,1,0:T(1,128)S(1)}, u32[]{:S(2)}, u32[]{:S(2)}) async-start(f32[64,1,4224]{2,1,0:T(1,128)} %all_to_all.11), calls=%async_computation | async-start | bytes 2162688 | tf_op jit(solution)/shard_map/all_to_all | solution.py:100
  80.4 2.8 %copy-start.5 = (f32[16,128,32]{1,2,0:T(8,128)S(1)}, f32[16,128,32]{1,2,0:T(8,128)}, u32[]{:S(2)}) copy-start(f32[16,128,32]{1,2,0:T(8,128)} %param.14) | copy-start | bytes 786436
  83.1 10.0 %copy-start.4 = (bf16[32,32,128]{2,1,0:T(8,128)(2,1)S(1)}, bf16[32,32,128]{2,1,0:T(8,128)(2,1)}, u32[]{:S(2)}) copy-start(bf16[32,32,128]{2,1,0:T(8,128)(2,1)} %param.23) | copy-start | bytes 786436
  84.4 5.1 %collective-permute-start.5 = (bf16[32,16,32]{2,0,1:T(8,128)(2,1)S(1)}, bf16[32,16,32]{2,0,1:T(8,128)(2,1)S(1)}, u32[]{:S(2)}, u32[]{:S(2)}) collective-permute-start(bf16[32,16,32]{2,0,1:T(8,128)(2,1)S(1)} %fusion.5), channel_id=1, source_target_pairs={{0,1},{1,2},{2,3},{3,0},{4,5},{5,6},{6,7},{7,4},{8,9},{9,10},{10,1... | collective-permute-start | bytes 98312 | tf_op jit(solution)/shard_map/ppermute | solution.py:35
  85.5 7.0 %collective-permute-start.4 = (bf16[32,16,32]{2,0,1:T(8,128)(2,1)S(1)}, bf16[32,16,32]{2,0,1:T(8,128)(2,1)S(1)}, u32[]{:S(2)}, u32[]{:S(2)}) collective-permute-start(bf16[32,16,32]{2,0,1:T(8,128)(2,1)S(1)} %fusion.5), channel_id=1, source_target_pairs={{0,2},{1,3},{2,0},{3,1},{4,6},{5,7},{6,4},{7,5},{8,10},{9,11},{10,... | collective-permute-start | bytes 98312 | tf_op jit(solution)/shard_map/ppermute | solution.py:35
  87.6 5.1 %collective-permute-start.3 = (bf16[32,16,32]{2,0,1:T(8,128)(2,1)S(1)}, bf16[32,16,32]{2,0,1:T(8,128)(2,1)S(1)}, u32[]{:S(2)}, u32[]{:S(2)}) collective-permute-start(bf16[32,16,32]{2,0,1:T(8,128)(2,1)S(1)} %fusion.5), channel_id=1, source_target_pairs={{0,3},{1,0},{2,1},{3,2},{4,7},{5,4},{6,5},{7,6},{8,11},{9,8},{10,9... | collective-permute-start | bytes 98312 | tf_op jit(solution)/shard_map/ppermute | solution.py:35
  131.0 8.8 %collective-permute-start.8 = (bf16[256,16,32]{0,2,1:T(8,128)(2,1)S(1)}, bf16[256,16,32]{0,2,1:T(8,128)(2,1)S(1)}, u32[]{:S(2)}, u32[]{:S(2)}) collective-permute-start(bf16[256,16,32]{0,2,1:T(8,128)(2,1)S(1)} %bitcast.99), channel_id=1, source_target_pairs={{0,1},{1,2},{2,3},{3,0},{4,5},{5,6},{6,7},{7,4},{8,9},{9,10},{10,1... | collective-permute-start | bytes 786440 | tf_op jit(solution)/shard_map/ppermute | solution.py:35
  132.5 13.7 %collective-permute-start.7 = (bf16[256,16,32]{0,2,1:T(8,128)(2,1)S(1)}, bf16[256,16,32]{0,2,1:T(8,128)(2,1)S(1)}, u32[]{:S(2)}, u32[]{:S(2)}) collective-permute-start(bf16[256,16,32]{0,2,1:T(8,128)(2,1)S(1)} %bitcast.100), channel_id=1, source_target_pairs={{0,2},{1,3},{2,0},{3,1},{4,6},{5,7},{6,4},{7,5},{8,10},{9,11},{10,... | collective-permute-start | bytes 786440 | tf_op jit(solution)/shard_map/ppermute | solution.py:35
  134.6 11.6 %collective-permute-start.6 = (bf16[256,16,32]{0,2,1:T(8,128)(2,1)S(1)}, bf16[256,16,32]{0,2,1:T(8,128)(2,1)S(1)}, u32[]{:S(2)}, u32[]{:S(2)}) collective-permute-start(bf16[256,16,32]{0,2,1:T(8,128)(2,1)S(1)} %bitcast.101), channel_id=1, source_target_pairs={{0,3},{1,0},{2,1},{3,2},{4,7},{5,4},{6,5},{7,6},{8,11},{9,8},{10,9... | collective-permute-start | bytes 786440 | tf_op jit(solution)/shard_map/ppermute | solution.py:35
  146.4 1.6 copy-start.3
  153.0 17.2 %copy-start.8 = (s32[512]{0:T(512)S(1)}, s32[512]{0:T(512)}, u32[]{:S(2)}) copy-start(s32[512]{0:T(512)} %param.17) | copy-start | bytes 6148
  154.5 8.2 %collective-permute-start.11 = (bf16[256,16,32]{0,2,1:T(8,128)(2,1)S(1)}, bf16[256,16,32]{0,2,1:T(8,128)(2,1)S(1)}, u32[]{:S(2)}, u32[]{:S(2)}) collective-permute-start(bf16[256,16,32]{0,2,1:T(8,128)(2,1)S(1)} %fusion.4), channel_id=1, source_target_pairs={{0,1},{1,2},{2,3},{3,0},{4,5},{5,6},{6,7},{7,4},{8,9},{9,10},{10,1... | collective-permute-start | bytes 786440 | tf_op jit(solution)/shard_map/ppermute | solution.py:35
  156.2 13.9 %collective-permute-start.10 = (bf16[256,16,32]{0,2,1:T(8,128)(2,1)S(1)}, bf16[256,16,32]{0,2,1:T(8,128)(2,1)S(1)}, u32[]{:S(2)}, u32[]{:S(2)}) collective-permute-start(bf16[256,16,32]{0,2,1:T(8,128)(2,1)S(1)} %fusion.4), channel_id=1, source_target_pairs={{0,2},{1,3},{2,0},{3,1},{4,6},{5,7},{6,4},{7,5},{8,10},{9,11},{10,... | collective-permute-start | bytes 786440 | tf_op jit(solution)/shard_map/ppermute | solution.py:35
  158.6 11.5 %collective-permute-start.9 = (bf16[256,16,32]{0,2,1:T(8,128)(2,1)S(1)}, bf16[256,16,32]{0,2,1:T(8,128)(2,1)S(1)}, u32[]{:S(2)}, u32[]{:S(2)}) collective-permute-start(bf16[256,16,32]{0,2,1:T(8,128)(2,1)S(1)} %fusion.4), channel_id=1, source_target_pairs={{0,3},{1,0},{2,1},{3,2},{4,7},{5,4},{6,5},{7,6},{8,11},{9,8},{10,9... | collective-permute-start | bytes 786440 | tf_op jit(solution)/shard_map/ppermute | solution.py:35
  170.2 2.2 %copy-start.2 = (bf16[512,32,128]{2,1,0:T(8,128)(2,1)S(1)}, bf16[512,32,128]{2,1,0:T(8,128)(2,1)}, u32[]{:S(2)}) copy-start(bf16[512,32,128]{2,1,0:T(8,128)(2,1)} %param.15) | copy-start | bytes 12582916

commit v9 on v8

--- a/solution.py
+++ b/solution.py
@@ -73,10 +73,10 @@
     )
     first_full = harm_gather(first_pass, 2)
     partials = jnp.einsum(
-        "tok,trk->tro", couple_tiles, pick_rows(first_full, couple_node), preferred_element_type=jnp.float32
+        "tok,trk->rot", couple_tiles, pick_rows(first_full, couple_node), preferred_element_type=jnp.float32
     )
     owner_list = border_owner[:, 0]
-    value_shape = partials.shape[1:]
+    value_shape = (partials.shape[0], partials.shape[1])
     capacity = min(touch_count, max(4, 2 * touch_count // sub_count))
     owner_marks = (owner_list[:, None] == jnp.arange(sub_count, dtype=jnp.int32)[None, :]).astype(
         jnp.int32
@@ -85,12 +85,9 @@
     slot_index = owner_list * capacity + jnp.sum(earlier * owner_marks, axis=1)
     slot_place = jnp.arange(sub_count * capacity, dtype=jnp.int32)[:, None] == slot_index[None, :]
     place_float = slot_place.astype(jnp.float32)
-    send_values = jnp.dot(
-        place_float,
-        partials.reshape(touch_count, -1),
-        precision=lax.Precision.HIGHEST,
-        preferred_element_type=jnp.float32,
-    )
+    send_values = jnp.einsum(
+        "st,rot->sro", place_float, partials, precision=lax.Precision.HIGHEST
+    ).reshape(place_float.shape[0], -1)
     send_rows = jnp.sum(slot_place.astype(jnp.int32) * border_row[None, :], axis=1)
     row_block = jnp.zeros((sub_count, 128), jnp.float32)
     row_block = row_block.at[:, :capacity].set(

time: 182 us -> 184 us (1.011)
  local copies, waits for them, and re-layouts: 33 us -> 36.6 us
    another operation x3 -> x4, local copies, waits for them, and re-layouts: 0.27 us -> 3.78 us  [the longest x1 3.51 us: on_device(): send_values.reshape(sub_count, -1)]
    dot_general x1 -> x2, local copies, waits for them, and re-layouts: 2.49 us -> 5.23 us  [the longest x1 3.68 us: on_device(): jnp.einsum('st,rot->sro', place_float, partials, precision=lax.Precision....]
where the time goes in v9:
time: 184 us
  waiting for transfers between devices  61.4 us (33%)
  local copies, waits for them, and re-layouts  36.6 us (20%)
  starting transfers between devices  32.3 us (18%)
  blocking collectives  25.2 us (14%)
  matrix products  24.6 us (13%)
  other arithmetic  2.75 us (1%)
    ppermute x12, waiting for transfers between devices, harm_gather(): lax.ppermute(values, 'harm', [(i, (i + s) % count) for i in range(count)])  32.5 us
    all_to_all x1, waiting for transfers between devices, on_device(): lax.all_to_all(packet, 'sub', split_axis=0, concat_axis=0, tiled=True)  28.8 us
    all_to_all x1, blocking collectives, on_device(): lax.all_to_all(replies, 'sub', split_axis=0, concat_axis=0, tiled=True)  25.2 us
    ppermute x12, starting transfers between devices, harm_gather(): lax.ppermute(values, 'harm', [(i, (i + s) % count) for i in range(count)])  19.3 us
    all_to_all x1, starting transfers between devices, on_device(): lax.all_to_all(packet, 'sub', split_axis=0, concat_axis=0, tiled=True)  13 us
    dot_general x3, matrix products, tile_product(): jnp.einsum('tok,trk->tro', tile_set, columns, preferred_element_type=jnp....  11.1 us
    unnamed x26, local copies, waits for them, and re-layouts  9.71 us
    dot_general x3, local copies, waits for them, and re-layouts, tile_product(): jnp.einsum('tok,trk->tro', tile_set, columns, preferred_element_type=jnp....  8.13 us
  transfers between devices with their start and end apart: 13, of which 9 were waited for; matrix products, arithmetic and copies ran while one was open for 2% of the time, Pallas kernels for 0%

profile of v9, /device:TPU:1, one launch (start us, length us, event | category | flops | bytes accessed | tf_op | source)
XLA Modules:
  0.0 183.9 jit_solution(6379045621315447613)
XLA Ops:
  0.7 2.5 %convolution_convert_fusion.1 = bf16[512,16,128]{2,0,1:T(8,128)(2,1)S(1)} fusion(f32[16,128,256]{2,1,0:T(8,128)} %param.13, s32[512]{0:T(512)} %param.17), kind=kOutput, calls=%fused_computation.8 | convolution fusion | flops 538574848 | bytes 4196352 | tf_op jit(solution)/shard_map/tn,nrk->trk/dot_general | solution.py:27
  3.6 4.3 %fusion.4 = f32[512,16,32]{2,1,0:T(8,128)} fusion(bf16[512,32,128]{2,1,0:T(8,128)(2,1)S(1)} %copy-done.1, bf16[512,16,128]{2,0,1:T(8,128)(2,1)S(1)} %convolution_convert_fusion.1), kind=kOutput, calls=%fused_computation.5 | convolution fusion | flops 67108864 | bytes 7340032 | tf_op jit(solution)/shard_map/tok,trk->tro/dot_general | solution.py:19
  7.9 2.8 %copy.29 = f32[512,16,32]{0,2,1:T(8,128)S(1)} copy(f32[512,16,32]{2,1,0:T(8,128)} %fusion.4) | data formatting | bytes 2097152 | tf_op jit(solution)/shard_map/tok,trk->tro/dot_general | solution.py:19
  11.5 2.2 %collective-permute-start.2 = (bf16[256,16,32]{0,2,1:T(8,128)(2,1)S(1)}, bf16[256,16,32]{0,2,1:T(8,128)(2,1)S(1)}, u32[]{:S(2)}, u32[]{:S(2)}) collective-permute-start(bf16[256,16,32]{0,2,1:T(8,128)(2,1)S(1)} %convolution_convert_fusion.5), channel_id=1, source_target_pairs={{0,1},{1,2},{2,3},{3,0},{4,5},{5,6},{6,7},{7,4},{8,9},{9,10},{10,1... | collective-permute-start | bytes 786440 | tf_op jit(solution)/shard_map/ppermute | solution.py:35
  13.6 2.6 %collective-permute-start.1 = (bf16[256,16,32]{0,2,1:T(8,128)(2,1)S(1)}, bf16[256,16,32]{0,2,1:T(8,128)(2,1)S(1)}, u32[]{:S(2)}, u32[]{:S(2)}) collective-permute-start(bf16[256,16,32]{0,2,1:T(8,128)(2,1)S(1)} %convolution_convert_fusion.5), channel_id=1, source_target_pairs={{0,2},{1,3},{2,0},{3,1},{4,6},{5,7},{6,4},{7,5},{8,10},{9,11},{10,... | collective-permute-start | bytes 786440 | tf_op jit(solution)/shard_map/ppermute | solution.py:35
  20.0 7.7 %collective-permute-done.1 = bf16[256,16,32]{0,2,1:T(8,128)(2,1)S(1)} collective-permute-done((bf16[256,16,32]{0,2,1:T(8,128)(2,1)S(1)}, bf16[256,16,32]{0,2,1:T(8,128)(2,1)S(1)}, u32[]{:S(2)}, u32[]{:S(2)}) %collective-permute-start.1) | collective-permute-done | bytes 262176 | tf_op jit(solution)/shard_map/ppermute | solution.py:35
  29.5 2.2 %fusion.2 = f32[512,16,32]{0,2,1:T(8,128)S(1)} fusion(f32[16,32,256]{1,0,2:T(8,128)S(1)} %convolution_bitcast_fusion, s32[256]{0:T(256)S(1)} %multiply_add_fusion), kind=kOutput, calls=%fused_computation.3 | convolution fusion | flops 805437440 | bytes 1573888 | tf_op jit(solution)/shard_map/st,rot->sro/dot_general | solution.py:88
  31.7 3.7 %copy.33 = f32[512,16,32]{2,1,0:T(8,128)} copy(f32[512,16,32]{0,2,1:T(8,128)S(1)} %fusion.2) | data formatting | bytes 2097152 | tf_op jit(solution)/shard_map/st,rot->sro/dot_general | solution.py:88
  35.4 3.5 %reshape_reshape.3 = f32[64,4096]{1,0:T(8,128)S(1)} reshape(f32[512,16,32]{2,1,0:T(8,128)} %copy.33) | data formatting | bytes 2097152 | tf_op jit(solution)/shard_map/reshape;reshape | solution.py:96
  39.0 2.1 %copy.34 = f32[64,1,4224]{2,1,0:T(1,128)} copy(f32[64,1,4224]{2,0,1:T(8,128)S(1)} %fusion.8) | data formatting | bytes 2162688 | tf_op jit(solution)/shard_map/all_to_all | solution.py:97
  41.1 13.0 %all-to-all-start = ((f32[64,1,4224]{2,1,0:T(1,128)}), f32[64,1,4224]{2,1,0:T(1,128)S(1)}, u32[]{:S(2)}, u32[]{:S(2)}) async-start(f32[64,1,4224]{2,1,0:T(1,128)} %copy.34), calls=%async_computation | async-start | bytes 2162688 | tf_op jit(solution)/shard_map/all_to_all | solution.py:97
  54.1 28.8 %all-to-all-done = f32[64,1,4224]{2,1,0:T(1,128)S(1)} async-done(((f32[64,1,4224]{2,1,0:T(1,128)}), f32[64,1,4224]{2,1,0:T(1,128)S(1)}, u32[]{:S(2)}, u32[]{:S(2)}) %all-to-all-start) | async-done | bytes 1081376 | tf_op jit(solution)/shard_map/all_to_all | solution.py:97
  84.5 1.6 copy.35
  88.4 2.1 %collective-permute-start.4 = (bf16[32,16,32]{2,0,1:T(8,128)(2,1)S(1)}, bf16[32,16,32]{2,0,1:T(8,128)(2,1)S(1)}, u32[]{:S(2)}, u32[]{:S(2)}) collective-permute-start(bf16[32,16,32]{2,0,1:T(8,128)(2,1)S(1)} %fusion.7), channel_id=1, source_target_pairs={{0,2},{1,3},{2,0},{3,1},{4,6},{5,7},{6,4},{7,5},{8,10},{9,11},{10,... | collective-permute-start | bytes 98312 | tf_op jit(solution)/shard_map/ppermute | solution.py:35
  92.5 2.9 %collective-permute-done.4 = bf16[32,16,32]{2,0,1:T(8,128)(2,1)S(1)} collective-permute-done((bf16[32,16,32]{2,0,1:T(8,128)(2,1)S(1)}, bf16[32,16,32]{2,0,1:T(8,128)(2,1)S(1)}, u32[]{:S(2)}, u32[]{:S(2)}) %collective-permute-start.4) | collective-permute-done | bytes 32800 | tf_op jit(solution)/shard_map/ppermute | solution.py:35
  96.3 2.8 %gather_fusion = bf16[512,16,32]{2,1,0:T(8,128)(2,1)} fusion(bf16[32,16,32]{2,1,0:T(8,128)(2,1)S(1)} %get-tuple-element.36, s32[1024]{0:T(1024)S(1)} %pad_clamp_fusion), kind=kCustom, calls=%fused_computation | custom fusion | bytes 1050624 | tf_op jit(solution)/shard_map/gather | solution.py:109
  99.0 3.7 %reshape.157 = bf16[64,2,2048]{2,1,0:T(2,128)(2,1)S(1)} reshape(bf16[64,8,16,32]{3,2,1,0:T(8,128)(2,1)} %bitcast.97) | data formatting | bytes 1048576
  102.8 25.2 %all_to_all.17 = bf16[64,2,2048]{2,1,0:T(2,128)(2,1)S(1)} all-to-all(bf16[64,2,2048]{2,1,0:T(2,128)(2,1)S(1)} %reshape.157), channel_id=1, replica_groups=mesh['sub'=64,'harm'=4] {'sub'}, dimensions={0} | all-to-all | bytes 1048576 | tf_op jit(solution)/shard_map/all_to_all | solution.py:110
  128.0 2.0 %reshape.158 = bf16[64,8,16,32]{3,2,1,0:T(8,128)(2,1)} reshape(bf16[64,2,2048]{2,1,0:T(2,128)(2,1)S(1)} %all_to_all.17) | data formatting | bytes 1048576
  130.0 3.4 %reshape.136 = bf16[512,512]{1,0:T(8,128)(2,1)S(1)} reshape(bf16[64,8,16,32]{3,2,1,0:T(8,128)(2,1)} %reshape.158) | data formatting | bytes 1048576 | tf_op jit(solution)/shard_map/reshape | solution.py:111
  133.9 1.5 collective-permute-start.8
  135.4 2.1 %collective-permute-start.7 = (bf16[256,16,32]{0,2,1:T(8,128)(2,1)S(1)}, bf16[256,16,32]{0,2,1:T(8,128)(2,1)S(1)}, u32[]{:S(2)}, u32[]{:S(2)}) collective-permute-start(bf16[256,16,32]{0,2,1:T(8,128)(2,1)S(1)} %bitcast.104), channel_id=1, source_target_pairs={{0,2},{1,3},{2,0},{3,1},{4,6},{5,7},{6,4},{7,5},{8,10},{9,11},{10,... | collective-permute-start | bytes 786440 | tf_op jit(solution)/shard_map/ppermute | solution.py:35
  138.4 4.3 %collective-permute-done.8 = bf16[256,16,32]{0,2,1:T(8,128)(2,1)S(1)} collective-permute-done((bf16[256,16,32]{0,2,1:T(8,128)(2,1)S(1)}, bf16[256,16,32]{0,2,1:T(8,128)(2,1)S(1)}, u32[]{:S(2)}, u32[]{:S(2)}) %collective-permute-start.8) | collective-permute-done | bytes 262176 | tf_op jit(solution)/shard_map/ppermute | solution.py:35
  142.6 6.5 %collective-permute-done.7 = bf16[256,16,32]{0,2,1:T(8,128)(2,1)S(1)} collective-permute-done((bf16[256,16,32]{0,2,1:T(8,128)(2,1)S(1)}, bf16[256,16,32]{0,2,1:T(8,128)(2,1)S(1)}, u32[]{:S(2)}, u32[]{:S(2)}) %collective-permute-start.7) | collective-permute-done | bytes 262176 | tf_op jit(solution)/shard_map/ppermute | solution.py:35
  150.9 2.5 %fusion.34 = f32[256,16,32]{2,1,0:T(8,128)} fusion(bf16[256,32,128]{2,1,0:T(8,128)(2,1)S(1)} %copy-done.3, bf16[256,16,128]{2,0,1:T(8,128)(2,1)S(1)} %convolution_convert_fusion.2), kind=kOutput, calls=%fused_computation.48 | convolution fusion | flops 33554432 | bytes 3670016 | tf_op jit(solution)/shard_map/tok,trk->tro/dot_general | solution.py:19
  153.4 2.5 %copy.40 = f32[256,16,32]{0,2,1:T(8,128)S(1)} copy(f32[256,16,32]{2,1,0:T(8,128)} %fusion.34) | data formatting | bytes 1048576 | tf_op jit(solution)/shard_map/tok,trk->tro/dot_general | solution.py:19
  157.4 1.7 collective-permute-start.11
  159.1 2.4 %collective-permute-start.10 = (bf16[256,16,32]{0,2,1:T(8,128)(2,1)S(1)}, bf16[256,16,32]{0,2,1:T(8,128)(2,1)S(1)}, u32[]{:S(2)}, u32[]{:S(2)}) collective-permute-start(bf16[256,16,32]{0,2,1:T(8,128)(2,1)S(1)} %fusion.6), channel_id=1, source_target_pairs={{0,2},{1,3},{2,0},{3,1},{4,6},{5,7},{6,4},{7,5},{8,10},{9,11},{10,... | collective-permute-start | bytes 786440 | tf_op jit(solution)/shard_map/ppermute | solution.py:35
  162.7 2.9 %collective-permute-done.11 = bf16[256,16,32]{0,2,1:T(8,128)(2,1)S(1)} collective-permute-done((bf16[256,16,32]{0,2,1:T(8,128)(2,1)S(1)}, bf16[256,16,32]{0,2,1:T(8,128)(2,1)S(1)}, u32[]{:S(2)}, u32[]{:S(2)}) %collective-permute-start.11) | collective-permute-done | bytes 262176 | tf_op jit(solution)/shard_map/ppermute | solution.py:35
  165.6 7.4 %collective-permute-done.10 = bf16[256,16,32]{0,2,1:T(8,128)(2,1)S(1)} collective-permute-done((bf16[256,16,32]{0,2,1:T(8,128)(2,1)S(1)}, bf16[256,16,32]{0,2,1:T(8,128)(2,1)S(1)}, u32[]{:S(2)}, u32[]{:S(2)}) %collective-permute-start.10) | collective-permute-done | bytes 262176 | tf_op jit(solution)/shard_map/ppermute | solution.py:35
  175.4 4.3 %fusion = f32[512,16,32]{2,1,0:T(8,128)} fusion(bf16[512,32,128]{2,1,0:T(8,128)(2,1)S(1)} %copy-done.2, bf16[512,16,128]{2,0,1:T(8,128)(2,1)S(1)} %convolution_convert_fusion), kind=kOutput, calls=%fused_computation.1 | convolution fusion | flops 67108864 | bytes 7340032 | tf_op jit(solution)/shard_map/tok,trk->tro/dot_general | solution.py:19
  179.6 2.8 %copy.43 = f32[512,16,32]{0,2,1:T(8,128)S(1)} copy(f32[512,16,32]{2,1,0:T(8,128)} %fusion) | data formatting | bytes 2097152 | tf_op jit(solution)/shard_map/tok,trk->tro/dot_general | solution.py:19
  (70 shorter events, 22.8 us)
Async XLA Ops:
  0.6 27.6 %copy-start = (bf16[256,32,128]{2,1,0:T(8,128)(2,1)S(1)}, bf16[256,32,128]{2,1,0:T(8,128)(2,1)}, u32[]{:S(2)}) copy-start(bf16[256,32,128]{2,1,0:T(8,128)(2,1)} %param.18) | copy-start | bytes 6291460
  0.6 3.0 %copy-start.1 = (bf16[512,32,128]{2,1,0:T(8,128)(2,1)S(1)}, bf16[512,32,128]{2,1,0:T(8,128)(2,1)}, u32[]{:S(2)}) copy-start(bf16[512,32,128]{2,1,0:T(8,128)(2,1)} %param.15) | copy-start | bytes 12582916
  7.9 2.9 %copy-start.7 = (s32[512]{0:T(512)S(1)}, s32[512]{0:T(512)}, u32[]{:S(2)}) copy-start(s32[512]{0:T(512)} %param.16) | copy-start | bytes 6148
  7.9 9.4 %copy-start.6 = (s32[256,1]{0,1:T(1,128)S(1)}, s32[256,1]{0,1:T(1,128)}, u32[]{:S(2)}) copy-start(s32[256,1]{0,1:T(1,128)} %param.21) | copy-start | bytes 3076
  7.9 10.4 %copy-start.9 = (s32[256]{0:T(256)S(1)}, s32[256]{0:T(256)}, u32[]{:S(2)}) copy-start(s32[256]{0:T(256)} %param.22) | copy-start | bytes 3076
  10.8 17.0 %copy-start.10 = (s32[256]{0:T(256)S(1)}, s32[256]{0:T(256)}, u32[]{:S(2)}) copy-start(s32[256]{0:T(256)} %param.20) | copy-start | bytes 3076
  11.5 8.5 %collective-permute-start.2 = (bf16[256,16,32]{0,2,1:T(8,128)(2,1)S(1)}, bf16[256,16,32]{0,2,1:T(8,128)(2,1)S(1)}, u32[]{:S(2)}, u32[]{:S(2)}) collective-permute-start(bf16[256,16,32]{0,2,1:T(8,128)(2,1)S(1)} %convolution_convert_fusion.5), channel_id=1, source_target_pairs={{0,1},{1,2},{2,3},{3,0},{4,5},{5,6},{6,7},{7,4},{8,9},{9,10},{10,1... | collective-permute-start | bytes 786440 | tf_op jit(solution)/shard_map/ppermute | solution.py:35
  13.6 14.0 %collective-permute-start.1 = (bf16[256,16,32]{0,2,1:T(8,128)(2,1)S(1)}, bf16[256,16,32]{0,2,1:T(8,128)(2,1)S(1)}, u32[]{:S(2)}, u32[]{:S(2)}) collective-permute-start(bf16[256,16,32]{0,2,1:T(8,128)(2,1)S(1)} %convolution_convert_fusion.5), channel_id=1, source_target_pairs={{0,2},{1,3},{2,0},{3,1},{4,6},{5,7},{6,4},{7,5},{8,10},{9,11},{10,... | collective-permute-start | bytes 786440 | tf_op jit(solution)/shard_map/ppermute | solution.py:35
  16.3 11.3 %collective-permute-start = (bf16[256,16,32]{0,2,1:T(8,128)(2,1)S(1)}, bf16[256,16,32]{0,2,1:T(8,128)(2,1)S(1)}, u32[]{:S(2)}, u32[]{:S(2)}) collective-permute-start(bf16[256,16,32]{0,2,1:T(8,128)(2,1)S(1)} %convolution_convert_fusion.5), channel_id=1, source_target_pairs={{0,3},{1,0},{2,1},{3,2},{4,7},{5,4},{6,5},{7,6},{8,11},{9,8},{10,9... | collective-permute-start | bytes 786440 | tf_op jit(solution)/shard_map/ppermute | solution.py:35
  41.1 41.8 %all-to-all-start = ((f32[64,1,4224]{2,1,0:T(1,128)}), f32[64,1,4224]{2,1,0:T(1,128)S(1)}, u32[]{:S(2)}, u32[]{:S(2)}) async-start(f32[64,1,4224]{2,1,0:T(1,128)} %copy.34), calls=%async_computation | async-start | bytes 2162688 | tf_op jit(solution)/shard_map/all_to_all | solution.py:97
  83.3 2.8 %copy-start.5 = (f32[16,128,32]{1,2,0:T(8,128)S(1)}, f32[16,128,32]{1,2,0:T(8,128)}, u32[]{:S(2)}) copy-start(f32[16,128,32]{1,2,0:T(8,128)} %param.14) | copy-start | bytes 786436
  86.0 10.0 %copy-start.4 = (bf16[32,32,128]{2,1,0:T(8,128)(2,1)S(1)}, bf16[32,32,128]{2,1,0:T(8,128)(2,1)}, u32[]{:S(2)}) copy-start(bf16[32,32,128]{2,1,0:T(8,128)(2,1)} %param.23) | copy-start | bytes 786436
  87.4 5.1 %collective-permute-start.5 = (bf16[32,16,32]{2,0,1:T(8,128)(2,1)S(1)}, bf16[32,16,32]{2,0,1:T(8,128)(2,1)S(1)}, u32[]{:S(2)}, u32[]{:S(2)}) collective-permute-start(bf16[32,16,32]{2,0,1:T(8,128)(2,1)S(1)} %fusion.7), channel_id=1, source_target_pairs={{0,1},{1,2},{2,3},{3,0},{4,5},{5,6},{6,7},{7,4},{8,9},{9,10},{10,1... | collective-permute-start | bytes 98312 | tf_op jit(solution)/shard_map/ppermute | solution.py:35
  88.4 7.0 %collective-permute-start.4 = (bf16[32,16,32]{2,0,1:T(8,128)(2,1)S(1)}, bf16[32,16,32]{2,0,1:T(8,128)(2,1)S(1)}, u32[]{:S(2)}, u32[]{:S(2)}) collective-permute-start(bf16[32,16,32]{2,0,1:T(8,128)(2,1)S(1)} %fusion.7), channel_id=1, source_target_pairs={{0,2},{1,3},{2,0},{3,1},{4,6},{5,7},{6,4},{7,5},{8,10},{9,11},{10,... | collective-permute-start | bytes 98312 | tf_op jit(solution)/shard_map/ppermute | solution.py:35
  90.5 5.1 %collective-permute-start.3 = (bf16[32,16,32]{2,0,1:T(8,128)(2,1)S(1)}, bf16[32,16,32]{2,0,1:T(8,128)(2,1)S(1)}, u32[]{:S(2)}, u32[]{:S(2)}) collective-permute-start(bf16[32,16,32]{2,0,1:T(8,128)(2,1)S(1)} %fusion.7), channel_id=1, source_target_pairs={{0,3},{1,0},{2,1},{3,2},{4,7},{5,4},{6,5},{7,6},{8,11},{9,8},{10,9... | collective-permute-start | bytes 98312 | tf_op jit(solution)/shard_map/ppermute | solution.py:35
  133.9 8.8 %collective-permute-start.8 = (bf16[256,16,32]{0,2,1:T(8,128)(2,1)S(1)}, bf16[256,16,32]{0,2,1:T(8,128)(2,1)S(1)}, u32[]{:S(2)}, u32[]{:S(2)}) collective-permute-start(bf16[256,16,32]{0,2,1:T(8,128)(2,1)S(1)} %bitcast.103), channel_id=1, source_target_pairs={{0,1},{1,2},{2,3},{3,0},{4,5},{5,6},{6,7},{7,4},{8,9},{9,10},{10,1... | collective-permute-start | bytes 786440 | tf_op jit(solution)/shard_map/ppermute | solution.py:35
  135.4 13.7 %collective-permute-start.7 = (bf16[256,16,32]{0,2,1:T(8,128)(2,1)S(1)}, bf16[256,16,32]{0,2,1:T(8,128)(2,1)S(1)}, u32[]{:S(2)}, u32[]{:S(2)}) collective-permute-start(bf16[256,16,32]{0,2,1:T(8,128)(2,1)S(1)} %bitcast.104), channel_id=1, source_target_pairs={{0,2},{1,3},{2,0},{3,1},{4,6},{5,7},{6,4},{7,5},{8,10},{9,11},{10,... | collective-permute-start | bytes 786440 | tf_op jit(solution)/shard_map/ppermute | solution.py:35
  137.5 11.6 %collective-permute-start.6 = (bf16[256,16,32]{0,2,1:T(8,128)(2,1)S(1)}, bf16[256,16,32]{0,2,1:T(8,128)(2,1)S(1)}, u32[]{:S(2)}, u32[]{:S(2)}) collective-permute-start(bf16[256,16,32]{0,2,1:T(8,128)(2,1)S(1)} %bitcast.105), channel_id=1, source_target_pairs={{0,3},{1,0},{2,1},{3,2},{4,7},{5,4},{6,5},{7,6},{8,11},{9,8},{10,9... | collective-permute-start | bytes 786440 | tf_op jit(solution)/shard_map/ppermute | solution.py:35
  149.3 1.6 copy-start.3
  155.9 17.2 %copy-start.8 = (s32[512]{0:T(512)S(1)}, s32[512]{0:T(512)}, u32[]{:S(2)}) copy-start(s32[512]{0:T(512)} %param.17) | copy-start | bytes 6148
  157.4 8.2 %collective-permute-start.11 = (bf16[256,16,32]{0,2,1:T(8,128)(2,1)S(1)}, bf16[256,16,32]{0,2,1:T(8,128)(2,1)S(1)}, u32[]{:S(2)}, u32[]{:S(2)}) collective-permute-start(bf16[256,16,32]{0,2,1:T(8,128)(2,1)S(1)} %fusion.6), channel_id=1, source_target_pairs={{0,1},{1,2},{2,3},{3,0},{4,5},{5,6},{6,7},{7,4},{8,9},{9,10},{10,1... | collective-permute-start | bytes 786440 | tf_op jit(solution)/shard_map/ppermute | solution.py:35
  159.1 13.9 %collective-permute-start.10 = (bf16[256,16,32]{0,2,1:T(8,128)(2,1)S(1)}, bf16[256,16,32]{0,2,1:T(8,128)(2,1)S(1)}, u32[]{:S(2)}, u32[]{:S(2)}) collective-permute-start(bf16[256,16,32]{0,2,1:T(8,128)(2,1)S(1)} %fusion.6), channel_id=1, source_target_pairs={{0,2},{1,3},{2,0},{3,1},{4,6},{5,7},{6,4},{7,5},{8,10},{9,11},{10,... | collective-permute-start | bytes 786440 | tf_op jit(solution)/shard_map/ppermute | solution.py:35
  161.5 11.5 %collective-permute-start.9 = (bf16[256,16,32]{0,2,1:T(8,128)(2,1)S(1)}, bf16[256,16,32]{0,2,1:T(8,128)(2,1)S(1)}, u32[]{:S(2)}, u32[]{:S(2)}) collective-permute-start(bf16[256,16,32]{0,2,1:T(8,128)(2,1)S(1)} %fusion.6), channel_id=1, source_target_pairs={{0,3},{1,0},{2,1},{3,2},{4,7},{5,4},{6,5},{7,6},{8,11},{9,8},{10,9... | collective-permute-start | bytes 786440 | tf_op jit(solution)/shard_map/ppermute | solution.py:35
  173.2 2.2 %copy-start.2 = (bf16[512,32,128]{2,1,0:T(8,128)(2,1)S(1)}, bf16[512,32,128]{2,1,0:T(8,128)(2,1)}, u32[]{:S(2)}) copy-start(bf16[512,32,128]{2,1,0:T(8,128)(2,1)} %param.15) | copy-start | bytes 12582916
